TPU v7x, 1024 devices: a whole 8x8x8 slice. The times are simulated.
1024 devices in a mesh: section: 8 (over x), dp: 128 (over z, y, core).
Axes of the slice: x: 8, y: 8, z: 8, core: 2. Of those that a mesh axis runs over, the one named last changes fastest.
Arguments:
- images: bfloat16 [4, 128, 10, 10, 352], P(None, 'dp'), may hold values from -6 to 6
- cotangent: bfloat16 [4, 128, 10, 10, 352], P(None, 'dp'), may hold values from -6 to 6
- dw_kernel: float32 [8, 49, 352], P('section'), may hold values from -0.875 to 0.875
- layer_scale: float32 [8, 352], P('section'), may hold values from 0.2 to 2
- w_in: bfloat16 [8, 1408, 352], P('section'), may hold values from -0.3125 to 0.3125
- w_out: bfloat16 [8, 1408, 352], P('section'), may hold values from -0.15625 to 0.15625
Outputs:
- grad_in: float32 [8, 1408, 352], P('section', 'dp')
- input_grads: bfloat16 [8, 4, 128, 10, 10, 352], P('section', None, 'dp')
All inputs are finite; a program needn't handle non-finite values.
Results may differ from a plain program's by a relative error of at most 0.024.
Values may be sent and summed in bfloat16 or wider, within the bound.
No kernel may reach another device: no remote copies, remote signals or barrier semaphores. Data moves between devices by JAX's collectives and lax.ppermute only.
A program may use at most 32 MiB of HBM per device.

v0:
```python
import jax
import jax.numpy as jnp
from jax import lax
from jax.sharding import PartitionSpec as P

KS = 7


EPS = 1e-06


def shifted(block, axis, distance):
    devices = range(lax.axis_size(axis))
    route = [(i - distance, i) for i in devices if i - distance in devices]
    return lax.ppermute(block, axis, route)


def depthwise(field, kernel):
    reach = KS // 2
    height = field.shape[1]
    padded = jnp.pad(field, ((0, 0), (reach, reach), (reach, reach), (0, 0)))
    total = jnp.zeros(field.shape, jnp.float32)
    for row in range(KS):
        for col in range(KS):
            total = (
                total
                + padded[:, row : row + height, col : col + height, :] * kernel[row * KS + col]
            )
    return total


def depthwise_adjoint(field, kernel):
    reach = KS // 2
    height = field.shape[1]
    padded = jnp.pad(field, ((0, 0), (reach, reach), (reach, reach), (0, 0)))
    total = jnp.zeros(field.shape, jnp.float32)
    for row in range(KS):
        for col in range(KS):
            top = 2 * reach - row
            left = 2 * reach - col
            total = (
                total
                + padded[:, top : top + height, left : left + height, :] * kernel[row * KS + col]
            )
    return total


def gelu_parts(value):
    normal_cdf = 0.5 * (1.0 + lax.erf(value * 0.7071067811865476))
    density = jnp.exp(-0.5 * value * value) * 0.3989422804014327
    return (value * normal_cdf, normal_cdf + value * density)


def block_inner(inputs, kernel, weight_in):
    width = inputs.shape[-1]
    mixed = depthwise(inputs.astype(jnp.float32), kernel)
    center = mixed - jnp.mean(mixed, axis=-1, keepdims=True)
    inv_std = lax.rsqrt(jnp.mean(center * center, axis=-1, keepdims=True) + EPS)
    normed = center * inv_std
    flat = normed.reshape(-1, width).astype(jnp.bfloat16)
    pre = lax.dot_general(
        flat, weight_in, (((1,), (1,)), ((), ())), preferred_element_type=jnp.float32
    )
    active, slope = gelu_parts(pre)
    hidden = active.astype(jnp.bfloat16)
    return (normed, inv_std, flat, slope, hidden)


def block_forward(inputs, kernel, scale, weight_in, weight_out):
    width = inputs.shape[-1]
    normed, inv_std, flat, slope, hidden = block_inner(inputs, kernel, weight_in)
    branch = jnp.dot(hidden, weight_out, preferred_element_type=jnp.float32)
    output = inputs.reshape(-1, width).astype(jnp.float32) + scale * branch
    return output.astype(jnp.bfloat16).reshape(inputs.shape)


def block_backward(inputs, upstream, kernel, scale, weight_in, weight_out):
    width = inputs.shape[-1]
    normed, inv_std, flat, slope, hidden = block_inner(inputs, kernel, weight_in)
    up_flat = upstream.reshape(-1, width).astype(jnp.float32)
    branch_grad = (scale * up_flat).astype(jnp.bfloat16)
    hidden_grad = lax.dot_general(
        branch_grad, weight_out, (((1,), (1,)), ((), ())), preferred_element_type=jnp.float32
    )
    pre_grad = (hidden_grad * slope).astype(jnp.bfloat16)
    normed_grad = jnp.dot(pre_grad, weight_in, preferred_element_type=jnp.float32).reshape(
        inputs.shape
    )
    mean_grad = jnp.mean(normed_grad, axis=-1, keepdims=True)
    mean_cross = jnp.mean(normed_grad * normed, axis=-1, keepdims=True)
    mixed_grad = inv_std * (normed_grad - mean_grad - normed * mean_cross)
    input_grad = (upstream.astype(jnp.float32) + depthwise_adjoint(mixed_grad, kernel)).astype(
        jnp.bfloat16
    )
    return (input_grad, flat, pre_grad)


def place(buffer, value, slot, active):
    former = lax.dynamic_index_in_dim(buffer, slot, 0, keepdims=False)
    return lax.dynamic_update_index_in_dim(buffer, jnp.where(active, value, former), slot, 0)


def body(images, cotangent, dw_kernel, layer_scale, w_in, w_out):
    section = lax.axis_index("section")
    sections = lax.axis_size("section")
    micro_count, img_count, side, _, width = images.shape
    kernel = dw_kernel[0]
    scale = layer_scale[0]
    weight_in = w_in[0]
    weight_out = w_out[0]
    hidden_width = weight_in.shape[0]
    pixel_rows = img_count * side * side
    ticks = micro_count + sections - 1
    factor = 1.0 / (micro_count * pixel_rows)
    blank = jnp.zeros(images.shape[1:], jnp.bfloat16)

    def run_forward(entering):
        return block_forward(entering, kernel, scale, weight_in, weight_out)

    def skip_forward(entering):
        return jnp.zeros_like(entering)

    def forward_tick(tick, carry):
        incoming, kept = carry
        micro = tick - section
        active = (micro >= 0) & (micro < micro_count)
        slot = jnp.clip(micro, 0, micro_count - 1)
        own = lax.dynamic_index_in_dim(images, slot, 0, keepdims=False)
        entering = jnp.where(section == 0, own, incoming)
        leaving = lax.cond(active, run_forward, skip_forward, entering)
        kept = place(kept, entering, slot, active)
        incoming = shifted(leaving, "section", 1)
        return (incoming, kept)

    _, kept = lax.fori_loop(0, ticks, forward_tick, (blank, jnp.zeros(images.shape, jnp.bfloat16)))

    def run_backward(entering, upstream):
        return block_backward(entering, upstream, kernel, scale, weight_in, weight_out)

    def skip_backward(entering, upstream):
        return (
            jnp.zeros_like(upstream),
            jnp.zeros((pixel_rows, width), jnp.bfloat16),
            jnp.zeros((pixel_rows, hidden_width), jnp.bfloat16),
        )

    stores = (
        jnp.zeros((micro_count, pixel_rows, width), jnp.bfloat16),
        jnp.zeros((micro_count, pixel_rows, hidden_width), jnp.bfloat16),
    )
    summed = jnp.zeros((1,), jnp.float32)

    def backward_tick(tick, carry):
        incoming, grads, stored, total = carry
        micro = tick - (sections - 1 - section)
        active = (micro >= 0) & (micro < micro_count)
        slot = jnp.clip(micro, 0, micro_count - 1)
        own = lax.dynamic_index_in_dim(cotangent, slot, 0, keepdims=False)
        upstream = jnp.where(section == sections - 1, own, incoming)
        entering = lax.dynamic_index_in_dim(kept, slot, 0, keepdims=False)
        input_grad, flat, pre_grad = lax.cond(
            active, run_backward, skip_backward, entering, upstream
        )
        grads = place(grads, input_grad, slot, active)
        stored = (place(stored[0], flat, slot, active), place(stored[1], pre_grad, slot, active))
        incoming = shifted(input_grad, "section", -1)
        return (incoming, grads, stored, total)

    _, grads, stores, summed = lax.fori_loop(
        0, ticks, backward_tick, (blank, jnp.zeros(images.shape, jnp.bfloat16), stores, summed)
    )
    all_flat = stores[0].reshape(micro_count * pixel_rows, width)
    all_pre = stores[1].reshape(micro_count * pixel_rows, hidden_width)
    sums = lax.psum_scatter(
        lax.dot_general(
            all_pre, all_flat, (((0,), (0,)), ((), ())), preferred_element_type=jnp.float32
        )
        * factor,
        "dp",
        scatter_dimension=0,
        tiled=True,
    )
    return (sums[None], grads[None])


def solution(mesh):
    return jax.shard_map(
        body,
        mesh=mesh,
        in_specs=(
            P(None, "dp", None, None, None),
            P(None, "dp", None, None, None),
            P("section", None, None),
            P("section", None),
            P("section", None, None),
            P("section", None, None),
        ),
        out_specs=(P("section", "dp", None), P("section", None, "dp", None, None, None)),
        check_vma=False,
    )
```

profile of v0, /device:TPU:133, one launch (start us, length us, event | category | flops | bytes accessed | tf_op | source)
XLA Modules:
  0.0 956.8 jit_solution(5707570081684585072)
XLA Ops:
  6.9 115.5 %while.37 = (s32[]{:T(128)}, bf16[1,10,10,352]{3,2,1,0:T(8,128)(2,1)S(1)}, bf16[4,1,10,10,352]{4,3,2,1,0:T(8,128)(2,1)}, s32[]{:T(128)}, pred[]{:T(512)}, /*inde...) while((s32[]{:T(128)}, ...), condition=%wide.region_5.6_spmd, body=%wide.region_0.5_spmd.sunk | while | flops 202822496 | bytes 4644152 | solution.py:135
  19.6 7.8 collective-permute-done
  93.1 9.1 collective-permute-start
  125.1 231.3 %while.38 = (s32[]{:T(128)}, bf16[1,10,10,352]{3,2,1,0:T(8,128)(2,1)S(1)}, bf16[4,1,10,10,352]{4,3,2,1,0:T(8,128)(2,1)}, bf16[4,100,352]{2,1,0:T(8,128)(2,1)}, b...) while((s32[]{:T(128)}, ...), condition=%wide.region_13.14_spmd, body=%wide.region_6.13_spmd.sunk | while | flops 306697696 | bytes 13743495 | solution.py:169
  165.2 70.0 %collective-permute-done.1 = bf16[1,10,10,352]{3,2,1,0:T(8,128)(2,1)S(1)} collective-permute-done((bf16[1,10,10,352]{3,2,1,0:T(8,128)(2,1)}, bf16[1,10,10,352]{3,2,1,0:T(8,128)(2,1)S(1)}, u32[]{:S(2)}, u32[]{:S(2)}) %collective-permute-start.1) | collective-permute-done | bytes 70432 | tf_op jit(solution)/shard_map/while/body/eval_jaxpr/ppermute | solution.py:15
  235.2 15.3 %conditional.5 = (bf16[1,10,10,352]{3,2,1,0:T(8,128)(2,1)}, bf16[100,352]{1,0:T(8,128)(2,1)S(1)}, bf16[100,1408]{1,0:T(8,128)(2,1)S(1)}) conditional(s32[]{:T(128)} %convert_element_type.112, () %tuple.198, (pred[]{:T(512)}, bf16[4,1,10,10,352]{4,3,2,1,0:T(8,128)(2,1)}, s32[]{:T(128)}, bf16[1,10,10,352]{3,2,1,0:T(8,128)(2,1)S(1)}, ...), branch_computations={%region_7.7_spmd, %region_8.12_spmd} | conditional | flops 306486496 | bytes 11222317 | solution.py:161
  258.3 15.3 %conditional.5 = (bf16[1,10,10,352]{3,2,1,0:T(8,128)(2,1)}, bf16[100,352]{1,0:T(8,128)(2,1)S(1)}, bf16[100,1408]{1,0:T(8,128)(2,1)S(1)}) conditional(s32[]{:T(128)} %convert_element_type.112, () %tuple.198, (pred[]{:T(512)}, bf16[4,1,10,10,352]{4,3,2,1,0:T(8,128)(2,1)}, s32[]{:T(128)}, bf16[1,10,10,352]{3,2,1,0:T(8,128)(2,1)S(1)}, ...), branch_computations={%region_7.7_spmd, %region_8.12_spmd} | conditional | flops 306486496 | bytes 11222317 | solution.py:161
  281.4 15.3 %conditional.5 = (bf16[1,10,10,352]{3,2,1,0:T(8,128)(2,1)}, bf16[100,352]{1,0:T(8,128)(2,1)S(1)}, bf16[100,1408]{1,0:T(8,128)(2,1)S(1)}) conditional(s32[]{:T(128)} %convert_element_type.112, () %tuple.198, (pred[]{:T(512)}, bf16[4,1,10,10,352]{4,3,2,1,0:T(8,128)(2,1)}, s32[]{:T(128)}, bf16[1,10,10,352]{3,2,1,0:T(8,128)(2,1)S(1)}, ...), branch_computations={%region_7.7_spmd, %region_8.12_spmd} | conditional | flops 306486496 | bytes 11222317 | solution.py:161
  304.5 15.3 %conditional.5 = (bf16[1,10,10,352]{3,2,1,0:T(8,128)(2,1)}, bf16[100,352]{1,0:T(8,128)(2,1)S(1)}, bf16[100,1408]{1,0:T(8,128)(2,1)S(1)}) conditional(s32[]{:T(128)} %convert_element_type.112, () %tuple.198, (pred[]{:T(512)}, bf16[4,1,10,10,352]{4,3,2,1,0:T(8,128)(2,1)}, s32[]{:T(128)}, bf16[1,10,10,352]{3,2,1,0:T(8,128)(2,1)S(1)}, ...), branch_computations={%region_7.7_spmd, %region_8.12_spmd} | conditional | flops 306486496 | bytes 11222317 | solution.py:161
  328.3 14.6 %collective-permute-start.1 = (bf16[1,10,10,352]{3,2,1,0:T(8,128)(2,1)}, bf16[1,10,10,352]{3,2,1,0:T(8,128)(2,1)S(1)}, u32[]{:S(2)}, u32[]{:S(2)}) collective-permute-start(bf16[1,10,10,352]{3,2,1,0:T(8,128)(2,1)} %get-tuple-element.959), channel_id=1, source_target_pairs={{128,0},{256,128},{384,256},{512,384},{640,512},{768,640},{896,768... | collective-permute-start | bytes 211208 | tf_op jit(solution)/shard_map/while/body/eval_jaxpr/ppermute | solution.py:15
  360.0 304.5 %fusion = f32[16,352]{1,0:T(8,128)S(1)} fusion(f32[1408,352]{1,0:T(8,128)} %fusion.307), kind=kCustom, calls=%all-reduce-scatter | all-reduce-scatter fusion | flops 720897 | bytes 2009088
  674.3 30.5 %collective-permute-start.13 = (f32[16,352]{1,0:T(8,128)S(1)}, f32[16,352]{1,0:T(8,128)S(1)}, u32[]{:S(2)}, u32[]{:S(2)}) collective-permute-start(f32[16,352]{1,0:T(8,128)S(1)} %fusion), channel_id=1, source_target_pairs={{0,12},{1,13},{2,14},{3,15},{4,16},{5,17},{6,18},{7,19},{8,20},{9,... | collective-permute-start | bytes 67592
  718.2 13.5 %collective-permute-start.15 = (f32[16,352]{1,0:T(8,128)S(1)}, f32[16,352]{1,0:T(8,128)S(1)}, u32[]{:S(2)}, u32[]{:S(2)}) collective-permute-start(f32[16,352]{1,0:T(8,128)S(1)} %fusion), channel_id=1, source_target_pairs={{0,14},{1,15},{2,16},{3,17},{4,18},{5,19},{6,20},{7,21},{8,22},{9,... | collective-permute-start | bytes 67592
  746.1 12.7 %collective-permute-start.2 = (f32[16,352]{1,0:T(8,128)S(1)}, f32[16,352]{1,0:T(8,128)S(1)}, u32[]{:S(2)}, u32[]{:S(2)}) collective-permute-start(f32[16,352]{1,0:T(8,128)S(1)} %fusion), channel_id=1, source_target_pairs={{0,1},{1,2},{2,3},{3,4},{4,5},{5,6},{6,7},{7,8},{8,9},{9,10},{10,1... | collective-permute-start | bytes 67592
  783.3 8.0 collective-permute-start.24
  798.9 14.6 %collective-permute-start.3 = (f32[16,352]{1,0:T(8,128)S(1)}, f32[16,352]{1,0:T(8,128)S(1)}, u32[]{:S(2)}, u32[]{:S(2)}) collective-permute-start(f32[16,352]{1,0:T(8,128)S(1)} %fusion), channel_id=1, source_target_pairs={{0,2},{1,3},{2,4},{3,5},{4,6},{5,7},{6,8},{7,9},{8,10},{9,11},{10,... | collective-permute-start | bytes 67592
  813.5 7.5 collective-permute-start.30
  821.0 8.1 collective-permute-start.31
  850.8 12.1 %collective-permute-start.4 = (f32[16,352]{1,0:T(8,128)S(1)}, f32[16,352]{1,0:T(8,128)S(1)}, u32[]{:S(2)}, u32[]{:S(2)}) collective-permute-start(f32[16,352]{1,0:T(8,128)S(1)} %fusion), channel_id=1, source_target_pairs={{0,3},{1,4},{2,5},{3,6},{4,7},{5,8},{6,9},{7,10},{8,11},{9,12},{10... | collective-permute-start | bytes 67592
  863.0 11.8 %collective-permute-start.40 = (f32[16,352]{1,0:T(8,128)S(1)}, f32[16,352]{1,0:T(8,128)S(1)}, u32[]{:S(2)}, u32[]{:S(2)}) collective-permute-start(f32[16,352]{1,0:T(8,128)S(1)} %fusion), channel_id=1, source_target_pairs={{0,39},{1,40},{2,41},{3,42},{4,43},{5,44},{6,45},{7,46},{8,47},{9,... | collective-permute-start | bytes 67592
  874.7 15.1 %collective-permute-start.5 = (f32[16,352]{1,0:T(8,128)S(1)}, f32[16,352]{1,0:T(8,128)S(1)}, u32[]{:S(2)}, u32[]{:S(2)}) collective-permute-start(f32[16,352]{1,0:T(8,128)S(1)} %fusion), channel_id=1, source_target_pairs={{0,4},{1,5},{2,6},{3,7},{4,8},{5,9},{6,10},{7,11},{8,12},{9,13},{1... | collective-permute-start | bytes 67592
  889.9 22.1 %collective-permute-start.6 = (f32[16,352]{1,0:T(8,128)S(1)}, f32[16,352]{1,0:T(8,128)S(1)}, u32[]{:S(2)}, u32[]{:S(2)}) collective-permute-start(f32[16,352]{1,0:T(8,128)S(1)} %fusion), channel_id=1, source_target_pairs={{0,5},{1,6},{2,7},{3,8},{4,9},{5,10},{6,11},{7,12},{8,13},{9,14},{... | collective-permute-start | bytes 67592
  912.1 22.1 %collective-permute-start.7 = (f32[16,352]{1,0:T(8,128)S(1)}, f32[16,352]{1,0:T(8,128)S(1)}, u32[]{:S(2)}, u32[]{:S(2)}) collective-permute-start(f32[16,352]{1,0:T(8,128)S(1)} %fusion), channel_id=1, source_target_pairs={{0,6},{1,7},{2,8},{3,9},{4,10},{5,11},{6,12},{7,13},{8,14},{9,15},... | collective-permute-start | bytes 67592
  934.2 7.8 collective-permute-start.8
  (751 shorter events, 380.7 us)
Async XLA Ops:
  158.3 76.9 %collective-permute-start.1 = (bf16[1,10,10,352]{3,2,1,0:T(8,128)(2,1)}, bf16[1,10,10,352]{3,2,1,0:T(8,128)(2,1)S(1)}, u32[]{:S(2)}, u32[]{:S(2)}) collective-permute-start(bf16[1,10,10,352]{3,2,1,0:T(8,128)(2,1)} %get-tuple-element.959), channel_id=1, source_target_pairs={{128,0},{256,128},{384,256},{512,384},{640,512},{768,640},{896,768... | collective-permute-start | bytes 211208 | tf_op jit(solution)/shard_map/while/body/eval_jaxpr/ppermute | solution.py:15
  664.5 53.7 %collective-permute-start.10 = (f32[16,352]{1,0:T(8,128)S(1)}, f32[16,352]{1,0:T(8,128)S(1)}, u32[]{:S(2)}, u32[]{:S(2)}) collective-permute-start(f32[16,352]{1,0:T(8,128)S(1)} %fusion), channel_id=1, source_target_pairs={{0,9},{1,10},{2,11},{3,12},{4,13},{5,14},{6,15},{7,16},{8,17},{9,1... | collective-permute-start | bytes 67592
  666.4 65.3 %collective-permute-start.11 = (f32[16,352]{1,0:T(8,128)S(1)}, f32[16,352]{1,0:T(8,128)S(1)}, u32[]{:S(2)}, u32[]{:S(2)}) collective-permute-start(f32[16,352]{1,0:T(8,128)S(1)} %fusion), channel_id=1, source_target_pairs={{0,10},{1,11},{2,12},{3,13},{4,14},{5,15},{6,16},{7,17},{8,18},{9,... | collective-permute-start | bytes 67592
  668.4 65.3 %collective-permute-start.12 = (f32[16,352]{1,0:T(8,128)S(1)}, f32[16,352]{1,0:T(8,128)S(1)}, u32[]{:S(2)}, u32[]{:S(2)}) collective-permute-start(f32[16,352]{1,0:T(8,128)S(1)} %fusion), channel_id=1, source_target_pairs={{0,11},{1,12},{2,13},{3,14},{4,15},{5,16},{6,17},{7,18},{8,19},{9,... | collective-permute-start | bytes 67592
  674.3 61.5 %collective-permute-start.13 = (f32[16,352]{1,0:T(8,128)S(1)}, f32[16,352]{1,0:T(8,128)S(1)}, u32[]{:S(2)}, u32[]{:S(2)}) collective-permute-start(f32[16,352]{1,0:T(8,128)S(1)} %fusion), channel_id=1, source_target_pairs={{0,12},{1,13},{2,14},{3,15},{4,16},{5,17},{6,18},{7,19},{8,20},{9,... | collective-permute-start | bytes 67592
  718.2 27.9 %collective-permute-start.15 = (f32[16,352]{1,0:T(8,128)S(1)}, f32[16,352]{1,0:T(8,128)S(1)}, u32[]{:S(2)}, u32[]{:S(2)}) collective-permute-start(f32[16,352]{1,0:T(8,128)S(1)} %fusion), channel_id=1, source_target_pairs={{0,14},{1,15},{2,16},{3,17},{4,18},{5,19},{6,20},{7,21},{8,22},{9,... | collective-permute-start | bytes 67592
  731.7 27.1 %collective-permute-start.16 = (f32[16,352]{1,0:T(8,128)S(1)}, f32[16,352]{1,0:T(8,128)S(1)}, u32[]{:S(2)}, u32[]{:S(2)}) collective-permute-start(f32[16,352]{1,0:T(8,128)S(1)} %fusion), channel_id=1, source_target_pairs={{0,15},{1,16},{2,17},{3,18},{4,19},{5,20},{6,21},{7,22},{8,23},{9,... | collective-permute-start | bytes 67592
  733.6 31.7 %collective-permute-start.17 = (f32[16,352]{1,0:T(8,128)S(1)}, f32[16,352]{1,0:T(8,128)S(1)}, u32[]{:S(2)}, u32[]{:S(2)}) collective-permute-start(f32[16,352]{1,0:T(8,128)S(1)} %fusion), channel_id=1, source_target_pairs={{0,16},{1,17},{2,18},{3,19},{4,20},{5,21},{6,22},{7,23},{8,24},{9,... | collective-permute-start | bytes 67592
  735.8 37.0 %collective-permute-start.18 = (f32[16,352]{1,0:T(8,128)S(1)}, f32[16,352]{1,0:T(8,128)S(1)}, u32[]{:S(2)}, u32[]{:S(2)}) collective-permute-start(f32[16,352]{1,0:T(8,128)S(1)} %fusion), channel_id=1, source_target_pairs={{0,17},{1,18},{2,19},{3,20},{4,21},{5,22},{6,23},{7,24},{8,25},{9,... | collective-permute-start | bytes 67592
  738.6 40.1 %collective-permute-start.19 = (f32[16,352]{1,0:T(8,128)S(1)}, f32[16,352]{1,0:T(8,128)S(1)}, u32[]{:S(2)}, u32[]{:S(2)}) collective-permute-start(f32[16,352]{1,0:T(8,128)S(1)} %fusion), channel_id=1, source_target_pairs={{0,18},{1,19},{2,20},{3,21},{4,22},{5,23},{6,24},{7,25},{8,26},{9,... | collective-permute-start | bytes 67592
  746.1 37.2 %collective-permute-start.2 = (f32[16,352]{1,0:T(8,128)S(1)}, f32[16,352]{1,0:T(8,128)S(1)}, u32[]{:S(2)}, u32[]{:S(2)}) collective-permute-start(f32[16,352]{1,0:T(8,128)S(1)} %fusion), channel_id=1, source_target_pairs={{0,1},{1,2},{2,3},{3,4},{4,5},{5,6},{6,7},{7,8},{8,9},{9,10},{10,1... | collective-permute-start | bytes 67592
  758.8 32.5 %collective-permute-start.20 = (f32[16,352]{1,0:T(8,128)S(1)}, f32[16,352]{1,0:T(8,128)S(1)}, u32[]{:S(2)}, u32[]{:S(2)}) collective-permute-start(f32[16,352]{1,0:T(8,128)S(1)} %fusion), channel_id=1, source_target_pairs={{0,19},{1,20},{2,21},{3,22},{4,23},{5,24},{6,25},{7,26},{8,27},{9,... | collective-permute-start | bytes 67592
  765.3 28.2 %collective-permute-start.21 = (f32[16,352]{1,0:T(8,128)S(1)}, f32[16,352]{1,0:T(8,128)S(1)}, u32[]{:S(2)}, u32[]{:S(2)}) collective-permute-start(f32[16,352]{1,0:T(8,128)S(1)} %fusion), channel_id=1, source_target_pairs={{0,20},{1,21},{2,22},{3,23},{4,24},{5,25},{6,26},{7,27},{8,28},{9,... | collective-permute-start | bytes 67592
  796.2 32.9 %collective-permute-start.28 = (f32[16,352]{1,0:T(8,128)S(1)}, f32[16,352]{1,0:T(8,128)S(1)}, u32[]{:S(2)}, u32[]{:S(2)}) collective-permute-start(f32[16,352]{1,0:T(8,128)S(1)} %fusion), channel_id=1, source_target_pairs={{0,27},{1,28},{2,29},{3,30},{4,31},{5,32},{6,33},{7,34},{8,35},{9,... | collective-permute-start | bytes 67592
  797.6 37.0 %collective-permute-start.29 = (f32[16,352]{1,0:T(8,128)S(1)}, f32[16,352]{1,0:T(8,128)S(1)}, u32[]{:S(2)}, u32[]{:S(2)}) collective-permute-start(f32[16,352]{1,0:T(8,128)S(1)} %fusion), channel_id=1, source_target_pairs={{0,28},{1,29},{2,30},{3,31},{4,32},{5,33},{6,34},{7,35},{8,36},{9,... | collective-permute-start | bytes 67592
  798.9 37.0 %collective-permute-start.3 = (f32[16,352]{1,0:T(8,128)S(1)}, f32[16,352]{1,0:T(8,128)S(1)}, u32[]{:S(2)}, u32[]{:S(2)}) collective-permute-start(f32[16,352]{1,0:T(8,128)S(1)} %fusion), channel_id=1, source_target_pairs={{0,2},{1,3},{2,4},{3,5},{4,6},{5,7},{6,8},{7,9},{8,10},{9,11},{10,... | collective-permute-start | bytes 67592
  842.6 32.2 %collective-permute-start.37 = (f32[16,352]{1,0:T(8,128)S(1)}, f32[16,352]{1,0:T(8,128)S(1)}, u32[]{:S(2)}, u32[]{:S(2)}) collective-permute-start(f32[16,352]{1,0:T(8,128)S(1)} %fusion), channel_id=1, source_target_pairs={{0,36},{1,37},{2,38},{3,39},{4,40},{5,41},{6,42},{7,43},{8,44},{9,... | collective-permute-start | bytes 67592
  845.5 44.4 %collective-permute-start.38 = (f32[16,352]{1,0:T(8,128)S(1)}, f32[16,352]{1,0:T(8,128)S(1)}, u32[]{:S(2)}, u32[]{:S(2)}) collective-permute-start(f32[16,352]{1,0:T(8,128)S(1)} %fusion), channel_id=1, source_target_pairs={{0,37},{1,38},{2,39},{3,40},{4,41},{5,42},{6,43},{7,44},{8,45},{9,... | collective-permute-start | bytes 67592
  848.8 63.3 %collective-permute-start.39 = (f32[16,352]{1,0:T(8,128)S(1)}, f32[16,352]{1,0:T(8,128)S(1)}, u32[]{:S(2)}, u32[]{:S(2)}) collective-permute-start(f32[16,352]{1,0:T(8,128)S(1)} %fusion), channel_id=1, source_target_pairs={{0,38},{1,39},{2,40},{3,41},{4,42},{5,43},{6,44},{7,45},{8,46},{9,... | collective-permute-start | bytes 67592
  850.8 83.4 %collective-permute-start.4 = (f32[16,352]{1,0:T(8,128)S(1)}, f32[16,352]{1,0:T(8,128)S(1)}, u32[]{:S(2)}, u32[]{:S(2)}) collective-permute-start(f32[16,352]{1,0:T(8,128)S(1)} %fusion), channel_id=1, source_target_pairs={{0,3},{1,4},{2,5},{3,6},{4,7},{5,8},{6,9},{7,10},{8,11},{9,12},{10... | collective-permute-start | bytes 67592
  863.0 79.1 %collective-permute-start.40 = (f32[16,352]{1,0:T(8,128)S(1)}, f32[16,352]{1,0:T(8,128)S(1)}, u32[]{:S(2)}, u32[]{:S(2)}) collective-permute-start(f32[16,352]{1,0:T(8,128)S(1)} %fusion), channel_id=1, source_target_pairs={{0,39},{1,40},{2,41},{3,42},{4,43},{5,44},{6,45},{7,46},{8,47},{9,... | collective-permute-start | bytes 67592
  874.7 73.7 %collective-permute-start.5 = (f32[16,352]{1,0:T(8,128)S(1)}, f32[16,352]{1,0:T(8,128)S(1)}, u32[]{:S(2)}, u32[]{:S(2)}) collective-permute-start(f32[16,352]{1,0:T(8,128)S(1)} %fusion), channel_id=1, source_target_pairs={{0,4},{1,5},{2,6},{3,7},{4,8},{5,9},{6,10},{7,11},{8,12},{9,13},{1... | collective-permute-start | bytes 67592
  889.9 58.6 %collective-permute-start.6 = (f32[16,352]{1,0:T(8,128)S(1)}, f32[16,352]{1,0:T(8,128)S(1)}, u32[]{:S(2)}, u32[]{:S(2)}) collective-permute-start(f32[16,352]{1,0:T(8,128)S(1)} %fusion), channel_id=1, source_target_pairs={{0,5},{1,6},{2,7},{3,8},{4,9},{5,10},{6,11},{7,12},{8,13},{9,14},{... | collective-permute-start | bytes 67592
  912.1 36.5 %collective-permute-start.7 = (f32[16,352]{1,0:T(8,128)S(1)}, f32[16,352]{1,0:T(8,128)S(1)}, u32[]{:S(2)}, u32[]{:S(2)}) collective-permute-start(f32[16,352]{1,0:T(8,128)S(1)} %fusion), channel_id=1, source_target_pairs={{0,6},{1,7},{2,8},{3,9},{4,10},{5,11},{6,12},{7,13},{8,14},{9,15},... | collective-permute-start | bytes 67592
  (210 other events, 2016.7 us)
where the time goes:
time: 961 us; the launch traced here: 957 us
  starting transfers between devices  359 us (37%)
  blocking collectives  304 us (32%)
  waiting for transfers between devices  112 us (12%)
  other arithmetic  85.4 us (9%)
  local copies, waits for them, and re-layouts  68.6 us (7%)
  matrix products  21.6 us (2%)
    unnamed x1, blocking collectives  304 us
    unnamed x40, starting transfers between devices  280 us
    ppermute x22, waiting for transfers between devices, shifted(): return lax.ppermute(block, axis, route)  108 us
    ppermute x22, starting transfers between devices, shifted(): return lax.ppermute(block, axis, route)  79.5 us
    dynamic_slice x44, local copies, waits for them, and re-layouts, place(): former = lax.dynamic_index_in_dim(buffer, slot, 0, keepdims=False)  40.9 us
    dynamic_update_slice x44, other arithmetic, place(): lax.dynamic_update_index_in_dim(buffer, jnp.where(active, value, former),...  35 us
  transfers between devices with their start and end apart: 62, of which 18 were waited for; matrix products, arithmetic and copies ran while one was open for 6% of the time, Pallas kernels for 0%

commit v1 on v0

--- a/solution.py
+++ b/solution.py
@@ -171,15 +171,20 @@
     )
     all_flat = stores[0].reshape(micro_count * pixel_rows, width)
     all_pre = stores[1].reshape(micro_count * pixel_rows, hidden_width)
-    sums = lax.psum_scatter(
+    partial = (
         lax.dot_general(
             all_pre, all_flat, (((0,), (0,)), ((), ())), preferred_element_type=jnp.float32
         )
-        * factor,
-        "dp",
-        scatter_dimension=0,
-        tiled=True,
-    )
+        * factor
+    )
+    replicas = lax.axis_size("dp")
+    share = (hidden_width // replicas) * width
+    padded = -(-share // 1024) * 1024
+    chunks = jnp.pad(partial.reshape(replicas, share), ((0, 0), (0, padded - share)))
+    mine = lax.psum_scatter(
+        chunks.reshape(replicas, padded // 128, 128), "dp", scatter_dimension=0, tiled=True
+    )
+    sums = mine.reshape(padded)[:share].reshape(hidden_width // replicas, width)
     return (sums[None], grads[None])
 
 

time: 961 us -> 633 us (0.66)
  the two profiles are of different devices: /device:TPU:133 before, /device:TPU:2 now
where the time goes in v1:
time: 633 us; the launch traced here: 630 us
  waiting for transfers between devices  350 us (55%)
  other arithmetic  85.4 us (13%)
  starting transfers between devices  83.2 us (13%)
  local copies, waits for them, and re-layouts  72.2 us (11%)
  matrix products  21.2 us (3%)
  between operations  14.1 us (2%)
    reduce_scatter x1, waiting for transfers between devices, body(): lax.psum_scatter(chunks.reshape(replicas, padded // 128, 128), 'dp', scat...  203 us
    ppermute x22, waiting for transfers between devices, shifted(): return lax.ppermute(block, axis, route)  147 us
    ppermute x22, starting transfers between devices, shifted(): return lax.ppermute(block, axis, route)  83.1 us
    dynamic_slice x44, local copies, waits for them, and re-layouts, place(): former = lax.dynamic_index_in_dim(buffer, slot, 0, keepdims=False)  40.9 us
    dynamic_update_slice x44, other arithmetic, place(): lax.dynamic_update_index_in_dim(buffer, jnp.where(active, value, former),...  35.2 us
    reduce_sum x8, other arithmetic, block_inner(): center = mixed - jnp.mean(mixed, axis=-1, keepdims=True)  18.3 us
  transfers between devices with their start and end apart: 23, of which 21 were waited for; matrix products, arithmetic and copies ran while one was open for 9% of the time, Pallas kernels for 0%

profile of v1, /device:TPU:2, one launch (start us, length us, event | category | flops | bytes accessed | tf_op | source)
XLA Modules:
  0.0 629.7 jit_solution(4107354849573257387)
XLA Ops:
  13.5 135.3 %while.37 = (s32[]{:T(128)}, bf16[1,10,10,352]{3,2,1,0:T(8,128)(2,1)S(1)}, bf16[4,1,10,10,352]{4,3,2,1,0:T(8,128)(2,1)}, s32[]{:T(128)}, pred[]{:T(512)}, /*inde...) while((s32[]{:T(128)}, ...), condition=%wide.region_5.6_spmd, body=%wide.region_0.5_spmd.sunk | while | flops 202822496 | bytes 4644152 | solution.py:135
  18.6 18.0 %collective-permute-done = bf16[1,10,10,352]{3,2,1,0:T(8,128)(2,1)S(1)} collective-permute-done((bf16[1,10,10,352]{3,2,1,0:T(8,128)(2,1)S(1)}, bf16[1,10,10,352]{3,2,1,0:T(8,128)(2,1)S(1)}, u32[]{:S(2)}, u32[]{:S(2)}) %collective-permute-start) | collective-permute-done | bytes 70432 | tf_op jit(solution)/shard_map/while/body/eval_jaxpr/ppermute | solution.py:15
  38.2 4.1 conditional.4
  44.2 4.8 collective-permute-done
  50.7 4.1 conditional.4
  56.7 4.8 collective-permute-done
  63.2 4.1 conditional.4
  69.3 5.2 collective-permute-done
  76.1 4.1 conditional.4
  82.2 4.8 collective-permute-done
  88.7 6.9 %collective-permute-start = (bf16[1,10,10,352]{3,2,1,0:T(8,128)(2,1)S(1)}, bf16[1,10,10,352]{3,2,1,0:T(8,128)(2,1)S(1)}, u32[]{:S(2)}, u32[]{:S(2)}) collective-permute-start(bf16[1,10,10,352]{3,2,1,0:T(8,128)(2,1)S(1)} %get-tuple-element.1032), channel_id=1, source_target_pairs={{0,128},{128,256},{256,384},{384,512},{512,640},{640,768},{768,896... | collective-permute-start | bytes 211208 | tf_op jit(solution)/shard_map/while/body/eval_jaxpr/ppermute | solution.py:15
  99.7 4.3 collective-permute-start
  108.1 6.9 %collective-permute-start = (bf16[1,10,10,352]{3,2,1,0:T(8,128)(2,1)S(1)}, bf16[1,10,10,352]{3,2,1,0:T(8,128)(2,1)S(1)}, u32[]{:S(2)}, u32[]{:S(2)}) collective-permute-start(bf16[1,10,10,352]{3,2,1,0:T(8,128)(2,1)S(1)} %get-tuple-element.1032), channel_id=1, source_target_pairs={{0,128},{128,256},{256,384},{384,512},{512,640},{640,768},{768,896... | collective-permute-start | bytes 211208 | tf_op jit(solution)/shard_map/while/body/eval_jaxpr/ppermute | solution.py:15
  119.1 5.0 collective-permute-start
  128.2 8.5 %collective-permute-start = (bf16[1,10,10,352]{3,2,1,0:T(8,128)(2,1)S(1)}, bf16[1,10,10,352]{3,2,1,0:T(8,128)(2,1)S(1)}, u32[]{:S(2)}, u32[]{:S(2)}) collective-permute-start(bf16[1,10,10,352]{3,2,1,0:T(8,128)(2,1)S(1)} %get-tuple-element.1032), channel_id=1, source_target_pairs={{0,128},{128,256},{256,384},{384,512},{512,640},{640,768},{768,896... | collective-permute-start | bytes 211208 | tf_op jit(solution)/shard_map/while/body/eval_jaxpr/ppermute | solution.py:15
  140.8 5.6 collective-permute-start
  151.5 254.3 %while.38 = (s32[]{:T(128)}, bf16[1,10,10,352]{3,2,1,0:T(8,128)(2,1)S(1)}, bf16[4,1,10,10,352]{4,3,2,1,0:T(8,128)(2,1)}, bf16[4,100,352]{2,1,0:T(8,128)(2,1)}, b...) while((s32[]{:T(128)}, ...), condition=%wide.region_13.14_spmd, body=%wide.region_6.13_spmd.sunk | while | flops 306697696 | bytes 13743495 | solution.py:169
  204.9 85.6 %collective-permute-done.1 = bf16[1,10,10,352]{3,2,1,0:T(8,128)(2,1)S(1)} collective-permute-done((bf16[1,10,10,352]{3,2,1,0:T(8,128)(2,1)}, bf16[1,10,10,352]{3,2,1,0:T(8,128)(2,1)S(1)}, u32[]{:S(2)}, u32[]{:S(2)}) %collective-permute-start.1) | collective-permute-done | bytes 70432 | tf_op jit(solution)/shard_map/while/body/eval_jaxpr/ppermute | solution.py:15
  290.5 15.2 %conditional.5 = (bf16[1,10,10,352]{3,2,1,0:T(8,128)(2,1)}, bf16[100,352]{1,0:T(8,128)(2,1)S(1)}, bf16[100,1408]{1,0:T(8,128)(2,1)S(1)}) conditional(s32[]{:T(128)} %convert_element_type.114, () %tuple.193, (pred[]{:T(512)}, bf16[4,1,10,10,352]{4,3,2,1,0:T(8,128)(2,1)}, s32[]{:T(128)}, bf16[1,10,10,352]{3,2,1,0:T(8,128)(2,1)S(1)}, ...), branch_computations={%region_7.7_spmd, %region_8.12_spmd} | conditional | flops 306486496 | bytes 11222317 | solution.py:161
  313.9 15.2 %conditional.5 = (bf16[1,10,10,352]{3,2,1,0:T(8,128)(2,1)}, bf16[100,352]{1,0:T(8,128)(2,1)S(1)}, bf16[100,1408]{1,0:T(8,128)(2,1)S(1)}) conditional(s32[]{:T(128)} %convert_element_type.114, () %tuple.193, (pred[]{:T(512)}, bf16[4,1,10,10,352]{4,3,2,1,0:T(8,128)(2,1)}, s32[]{:T(128)}, bf16[1,10,10,352]{3,2,1,0:T(8,128)(2,1)S(1)}, ...), branch_computations={%region_7.7_spmd, %region_8.12_spmd} | conditional | flops 306486496 | bytes 11222317 | solution.py:161
  337.3 15.2 %conditional.5 = (bf16[1,10,10,352]{3,2,1,0:T(8,128)(2,1)}, bf16[100,352]{1,0:T(8,128)(2,1)S(1)}, bf16[100,1408]{1,0:T(8,128)(2,1)S(1)}) conditional(s32[]{:T(128)} %convert_element_type.114, () %tuple.193, (pred[]{:T(512)}, bf16[4,1,10,10,352]{4,3,2,1,0:T(8,128)(2,1)}, s32[]{:T(128)}, bf16[1,10,10,352]{3,2,1,0:T(8,128)(2,1)S(1)}, ...), branch_computations={%region_7.7_spmd, %region_8.12_spmd} | conditional | flops 306486496 | bytes 11222317 | solution.py:161
  361.4 15.2 %conditional.5 = (bf16[1,10,10,352]{3,2,1,0:T(8,128)(2,1)}, bf16[100,352]{1,0:T(8,128)(2,1)S(1)}, bf16[100,1408]{1,0:T(8,128)(2,1)S(1)}) conditional(s32[]{:T(128)} %convert_element_type.114, () %tuple.193, (pred[]{:T(512)}, bf16[4,1,10,10,352]{4,3,2,1,0:T(8,128)(2,1)}, s32[]{:T(128)}, bf16[1,10,10,352]{3,2,1,0:T(8,128)(2,1)S(1)}, ...), branch_computations={%region_7.7_spmd, %region_8.12_spmd} | conditional | flops 306486496 | bytes 11222317 | solution.py:161
  385.1 15.6 %collective-permute-start.1 = (bf16[1,10,10,352]{3,2,1,0:T(8,128)(2,1)}, bf16[1,10,10,352]{3,2,1,0:T(8,128)(2,1)S(1)}, u32[]{:S(2)}, u32[]{:S(2)}) collective-permute-start(bf16[1,10,10,352]{3,2,1,0:T(8,128)(2,1)} %get-tuple-element.930), channel_id=1, source_target_pairs={{128,0},{256,128},{384,256},{512,384},{640,512},{768,640},{896,768... | collective-permute-start | bytes 211208 | tf_op jit(solution)/shard_map/while/body/eval_jaxpr/ppermute | solution.py:15
  418.7 202.8 %reduce-scatter.2.cloned.1.call-done = f32[1,32,128]{2,1,0:T(8,128)} async-done(((f32[128,32,128]{2,1,0:T(8,128)}), f32[1,32,128]{2,1,0:T(8,128)}) %reduce-scatter.2.cloned.1.call-update) | async-done | bytes 16400 | tf_op jit(solution)/shard_map/reduce_scatter | solution.py:184
  (673 shorter events, 238.2 us)
Async XLA Ops:
  7.2 614.3 %reduce-scatter.2.cloned.1.call-start = ((), (), s32[]{:S(2)}) async-start(), calls=%async_computation.1 | async-start | bytes 2113536 | tf_op jit(solution)/shard_map/reduce_scatter | solution.py:184
  15.2 21.4 %collective-permute-start = (bf16[1,10,10,352]{3,2,1,0:T(8,128)(2,1)S(1)}, bf16[1,10,10,352]{3,2,1,0:T(8,128)(2,1)S(1)}, u32[]{:S(2)}, u32[]{:S(2)}) collective-permute-start(bf16[1,10,10,352]{3,2,1,0:T(8,128)(2,1)S(1)} %get-tuple-element.1032), channel_id=1, source_target_pairs={{0,128},{128,256},{256,384},{384,512},{512,640},{640,768},{768,896... | collective-permute-start | bytes 211208 | tf_op jit(solution)/shard_map/while/body/eval_jaxpr/ppermute | solution.py:15
  42.3 6.8 %collective-permute-start = (bf16[1,10,10,352]{3,2,1,0:T(8,128)(2,1)S(1)}, bf16[1,10,10,352]{3,2,1,0:T(8,128)(2,1)S(1)}, u32[]{:S(2)}, u32[]{:S(2)}) collective-permute-start(bf16[1,10,10,352]{3,2,1,0:T(8,128)(2,1)S(1)} %get-tuple-element.1032), channel_id=1, source_target_pairs={{0,128},{128,256},{256,384},{384,512},{512,640},{640,768},{768,896... | collective-permute-start | bytes 211208 | tf_op jit(solution)/shard_map/while/body/eval_jaxpr/ppermute | solution.py:15
  54.8 6.8 %collective-permute-start = (bf16[1,10,10,352]{3,2,1,0:T(8,128)(2,1)S(1)}, bf16[1,10,10,352]{3,2,1,0:T(8,128)(2,1)S(1)}, u32[]{:S(2)}, u32[]{:S(2)}) collective-permute-start(bf16[1,10,10,352]{3,2,1,0:T(8,128)(2,1)S(1)} %get-tuple-element.1032), channel_id=1, source_target_pairs={{0,128},{128,256},{256,384},{384,512},{512,640},{640,768},{768,896... | collective-permute-start | bytes 211208 | tf_op jit(solution)/shard_map/while/body/eval_jaxpr/ppermute | solution.py:15
  67.3 7.2 %collective-permute-start = (bf16[1,10,10,352]{3,2,1,0:T(8,128)(2,1)S(1)}, bf16[1,10,10,352]{3,2,1,0:T(8,128)(2,1)S(1)}, u32[]{:S(2)}, u32[]{:S(2)}) collective-permute-start(bf16[1,10,10,352]{3,2,1,0:T(8,128)(2,1)S(1)} %get-tuple-element.1032), channel_id=1, source_target_pairs={{0,128},{128,256},{256,384},{384,512},{512,640},{640,768},{768,896... | collective-permute-start | bytes 211208 | tf_op jit(solution)/shard_map/while/body/eval_jaxpr/ppermute | solution.py:15
  80.2 6.8 %collective-permute-start = (bf16[1,10,10,352]{3,2,1,0:T(8,128)(2,1)S(1)}, bf16[1,10,10,352]{3,2,1,0:T(8,128)(2,1)S(1)}, u32[]{:S(2)}, u32[]{:S(2)}) collective-permute-start(bf16[1,10,10,352]{3,2,1,0:T(8,128)(2,1)S(1)} %get-tuple-element.1032), channel_id=1, source_target_pairs={{0,128},{128,256},{256,384},{384,512},{512,640},{640,768},{768,896... | collective-permute-start | bytes 211208 | tf_op jit(solution)/shard_map/while/body/eval_jaxpr/ppermute | solution.py:15
  88.7 9.4 %collective-permute-start = (bf16[1,10,10,352]{3,2,1,0:T(8,128)(2,1)S(1)}, bf16[1,10,10,352]{3,2,1,0:T(8,128)(2,1)S(1)}, u32[]{:S(2)}, u32[]{:S(2)}) collective-permute-start(bf16[1,10,10,352]{3,2,1,0:T(8,128)(2,1)S(1)} %get-tuple-element.1032), channel_id=1, source_target_pairs={{0,128},{128,256},{256,384},{384,512},{512,640},{640,768},{768,896... | collective-permute-start | bytes 211208 | tf_op jit(solution)/shard_map/while/body/eval_jaxpr/ppermute | solution.py:15
  99.7 6.8 %collective-permute-start = (bf16[1,10,10,352]{3,2,1,0:T(8,128)(2,1)S(1)}, bf16[1,10,10,352]{3,2,1,0:T(8,128)(2,1)S(1)}, u32[]{:S(2)}, u32[]{:S(2)}) collective-permute-start(bf16[1,10,10,352]{3,2,1,0:T(8,128)(2,1)S(1)} %get-tuple-element.1032), channel_id=1, source_target_pairs={{0,128},{128,256},{256,384},{384,512},{512,640},{640,768},{768,896... | collective-permute-start | bytes 211208 | tf_op jit(solution)/shard_map/while/body/eval_jaxpr/ppermute | solution.py:15
  108.1 9.3 %collective-permute-start = (bf16[1,10,10,352]{3,2,1,0:T(8,128)(2,1)S(1)}, bf16[1,10,10,352]{3,2,1,0:T(8,128)(2,1)S(1)}, u32[]{:S(2)}, u32[]{:S(2)}) collective-permute-start(bf16[1,10,10,352]{3,2,1,0:T(8,128)(2,1)S(1)} %get-tuple-element.1032), channel_id=1, source_target_pairs={{0,128},{128,256},{256,384},{384,512},{512,640},{640,768},{768,896... | collective-permute-start | bytes 211208 | tf_op jit(solution)/shard_map/while/body/eval_jaxpr/ppermute | solution.py:15
  119.1 7.4 %collective-permute-start = (bf16[1,10,10,352]{3,2,1,0:T(8,128)(2,1)S(1)}, bf16[1,10,10,352]{3,2,1,0:T(8,128)(2,1)S(1)}, u32[]{:S(2)}, u32[]{:S(2)}) collective-permute-start(bf16[1,10,10,352]{3,2,1,0:T(8,128)(2,1)S(1)} %get-tuple-element.1032), channel_id=1, source_target_pairs={{0,128},{128,256},{256,384},{384,512},{512,640},{640,768},{768,896... | collective-permute-start | bytes 211208 | tf_op jit(solution)/shard_map/while/body/eval_jaxpr/ppermute | solution.py:15
  128.2 11.0 %collective-permute-start = (bf16[1,10,10,352]{3,2,1,0:T(8,128)(2,1)S(1)}, bf16[1,10,10,352]{3,2,1,0:T(8,128)(2,1)S(1)}, u32[]{:S(2)}, u32[]{:S(2)}) collective-permute-start(bf16[1,10,10,352]{3,2,1,0:T(8,128)(2,1)S(1)} %get-tuple-element.1032), channel_id=1, source_target_pairs={{0,128},{128,256},{256,384},{384,512},{512,640},{640,768},{768,896... | collective-permute-start | bytes 211208 | tf_op jit(solution)/shard_map/while/body/eval_jaxpr/ppermute | solution.py:15
  140.8 8.0 %collective-permute-start = (bf16[1,10,10,352]{3,2,1,0:T(8,128)(2,1)S(1)}, bf16[1,10,10,352]{3,2,1,0:T(8,128)(2,1)S(1)}, u32[]{:S(2)}, u32[]{:S(2)}) collective-permute-start(bf16[1,10,10,352]{3,2,1,0:T(8,128)(2,1)S(1)} %get-tuple-element.1032), channel_id=1, source_target_pairs={{0,128},{128,256},{256,384},{384,512},{512,640},{640,768},{768,896... | collective-permute-start | bytes 211208 | tf_op jit(solution)/shard_map/while/body/eval_jaxpr/ppermute | solution.py:15
  152.2 8.8 %collective-permute-start.1 = (bf16[1,10,10,352]{3,2,1,0:T(8,128)(2,1)}, bf16[1,10,10,352]{3,2,1,0:T(8,128)(2,1)S(1)}, u32[]{:S(2)}, u32[]{:S(2)}) collective-permute-start(bf16[1,10,10,352]{3,2,1,0:T(8,128)(2,1)} %get-tuple-element.930), channel_id=1, source_target_pairs={{128,0},{256,128},{384,256},{512,384},{640,512},{768,640},{896,768... | collective-permute-start | bytes 211208 | tf_op jit(solution)/shard_map/while/body/eval_jaxpr/ppermute | solution.py:15
  161.7 8.5 %collective-permute-start.1 = (bf16[1,10,10,352]{3,2,1,0:T(8,128)(2,1)}, bf16[1,10,10,352]{3,2,1,0:T(8,128)(2,1)S(1)}, u32[]{:S(2)}, u32[]{:S(2)}) collective-permute-start(bf16[1,10,10,352]{3,2,1,0:T(8,128)(2,1)} %get-tuple-element.930), channel_id=1, source_target_pairs={{128,0},{256,128},{384,256},{512,384},{640,512},{768,640},{896,768... | collective-permute-start | bytes 211208 | tf_op jit(solution)/shard_map/while/body/eval_jaxpr/ppermute | solution.py:15
  170.9 8.6 %collective-permute-start.1 = (bf16[1,10,10,352]{3,2,1,0:T(8,128)(2,1)}, bf16[1,10,10,352]{3,2,1,0:T(8,128)(2,1)S(1)}, u32[]{:S(2)}, u32[]{:S(2)}) collective-permute-start(bf16[1,10,10,352]{3,2,1,0:T(8,128)(2,1)} %get-tuple-element.930), channel_id=1, source_target_pairs={{128,0},{256,128},{384,256},{512,384},{640,512},{768,640},{896,768... | collective-permute-start | bytes 211208 | tf_op jit(solution)/shard_map/while/body/eval_jaxpr/ppermute | solution.py:15
  180.2 8.2 %collective-permute-start.1 = (bf16[1,10,10,352]{3,2,1,0:T(8,128)(2,1)}, bf16[1,10,10,352]{3,2,1,0:T(8,128)(2,1)S(1)}, u32[]{:S(2)}, u32[]{:S(2)}) collective-permute-start(bf16[1,10,10,352]{3,2,1,0:T(8,128)(2,1)} %get-tuple-element.930), channel_id=1, source_target_pairs={{128,0},{256,128},{384,256},{512,384},{640,512},{768,640},{896,768... | collective-permute-start | bytes 211208 | tf_op jit(solution)/shard_map/while/body/eval_jaxpr/ppermute | solution.py:15
  189.1 8.2 %collective-permute-start.1 = (bf16[1,10,10,352]{3,2,1,0:T(8,128)(2,1)}, bf16[1,10,10,352]{3,2,1,0:T(8,128)(2,1)S(1)}, u32[]{:S(2)}, u32[]{:S(2)}) collective-permute-start(bf16[1,10,10,352]{3,2,1,0:T(8,128)(2,1)} %get-tuple-element.930), channel_id=1, source_target_pairs={{128,0},{256,128},{384,256},{512,384},{640,512},{768,640},{896,768... | collective-permute-start | bytes 211208 | tf_op jit(solution)/shard_map/while/body/eval_jaxpr/ppermute | solution.py:15
  198.0 92.5 %collective-permute-start.1 = (bf16[1,10,10,352]{3,2,1,0:T(8,128)(2,1)}, bf16[1,10,10,352]{3,2,1,0:T(8,128)(2,1)S(1)}, u32[]{:S(2)}, u32[]{:S(2)}) collective-permute-start(bf16[1,10,10,352]{3,2,1,0:T(8,128)(2,1)} %get-tuple-element.930), channel_id=1, source_target_pairs={{128,0},{256,128},{384,256},{512,384},{640,512},{768,640},{896,768... | collective-permute-start | bytes 211208 | tf_op jit(solution)/shard_map/while/body/eval_jaxpr/ppermute | solution.py:15
  305.7 8.2 %collective-permute-start.1 = (bf16[1,10,10,352]{3,2,1,0:T(8,128)(2,1)}, bf16[1,10,10,352]{3,2,1,0:T(8,128)(2,1)S(1)}, u32[]{:S(2)}, u32[]{:S(2)}) collective-permute-start(bf16[1,10,10,352]{3,2,1,0:T(8,128)(2,1)} %get-tuple-element.930), channel_id=1, source_target_pairs={{128,0},{256,128},{384,256},{512,384},{640,512},{768,640},{896,768... | collective-permute-start | bytes 211208 | tf_op jit(solution)/shard_map/while/body/eval_jaxpr/ppermute | solution.py:15
  314.0 6.4 %copy-start.5 = (f32[352]{0:T(512)}, f32[352]{0:T(512)S(1)}, u32[]{:S(2)}) copy-start(f32[352]{0:T(512)S(1)} %get-tuple-element.684) | copy-start | bytes 4228 | tf_op jit(solution)/shard_map/while/body/eval_jaxpr/cond
  329.1 8.2 %collective-permute-start.1 = (bf16[1,10,10,352]{3,2,1,0:T(8,128)(2,1)}, bf16[1,10,10,352]{3,2,1,0:T(8,128)(2,1)S(1)}, u32[]{:S(2)}, u32[]{:S(2)}) collective-permute-start(bf16[1,10,10,352]{3,2,1,0:T(8,128)(2,1)} %get-tuple-element.930), channel_id=1, source_target_pairs={{128,0},{256,128},{384,256},{512,384},{640,512},{768,640},{896,768... | collective-permute-start | bytes 211208 | tf_op jit(solution)/shard_map/while/body/eval_jaxpr/ppermute | solution.py:15
  352.5 8.8 %collective-permute-start.1 = (bf16[1,10,10,352]{3,2,1,0:T(8,128)(2,1)}, bf16[1,10,10,352]{3,2,1,0:T(8,128)(2,1)S(1)}, u32[]{:S(2)}, u32[]{:S(2)}) collective-permute-start(bf16[1,10,10,352]{3,2,1,0:T(8,128)(2,1)} %get-tuple-element.930), channel_id=1, source_target_pairs={{128,0},{256,128},{384,256},{512,384},{640,512},{768,640},{896,768... | collective-permute-start | bytes 211208 | tf_op jit(solution)/shard_map/while/body/eval_jaxpr/ppermute | solution.py:15
  376.6 7.8 %collective-permute-start.1 = (bf16[1,10,10,352]{3,2,1,0:T(8,128)(2,1)}, bf16[1,10,10,352]{3,2,1,0:T(8,128)(2,1)S(1)}, u32[]{:S(2)}, u32[]{:S(2)}) collective-permute-start(bf16[1,10,10,352]{3,2,1,0:T(8,128)(2,1)} %get-tuple-element.930), channel_id=1, source_target_pairs={{128,0},{256,128},{384,256},{512,384},{640,512},{768,640},{896,768... | collective-permute-start | bytes 211208 | tf_op jit(solution)/shard_map/while/body/eval_jaxpr/ppermute | solution.py:15
  385.1 20.6 %collective-permute-start.1 = (bf16[1,10,10,352]{3,2,1,0:T(8,128)(2,1)}, bf16[1,10,10,352]{3,2,1,0:T(8,128)(2,1)S(1)}, u32[]{:S(2)}, u32[]{:S(2)}) collective-permute-start(bf16[1,10,10,352]{3,2,1,0:T(8,128)(2,1)} %get-tuple-element.930), channel_id=1, source_target_pairs={{128,0},{256,128},{384,256},{512,384},{640,512},{768,640},{896,768... | collective-permute-start | bytes 211208 | tf_op jit(solution)/shard_map/while/body/eval_jaxpr/ppermute | solution.py:15
  (171 other events, 975.6 us)
Sparse Core Ops, SparseCore 0:
  416.9 204.4 reduce-scatter.1

commit v2 on v1

--- a/solution.py
+++ b/solution.py
@@ -1,7 +1,7 @@
 import jax
 import jax.numpy as jnp
 from jax import lax
-from jax.sharding import PartitionSpec as P
+from jax.sharding import Mesh, PartitionSpec as P
 
 KS = 7
 
@@ -95,9 +95,9 @@
     return (input_grad, flat, pre_grad)
 
 
-def place(buffer, value, slot, active):
-    former = lax.dynamic_index_in_dim(buffer, slot, 0, keepdims=False)
-    return lax.dynamic_update_index_in_dim(buffer, jnp.where(active, value, former), slot, 0)
+def place(buffer, value, micro, count):
+    slot = jnp.clip(micro, -1, count) + 1
+    return lax.dynamic_update_index_in_dim(buffer, value, slot, 0)
 
 
 def body(images, cotangent, dw_kernel, layer_scale, w_in, w_out):
@@ -128,11 +128,12 @@
         own = lax.dynamic_index_in_dim(images, slot, 0, keepdims=False)
         entering = jnp.where(section == 0, own, incoming)
         leaving = lax.cond(active, run_forward, skip_forward, entering)
-        kept = place(kept, entering, slot, active)
+        kept = place(kept, entering, micro, micro_count)
         incoming = shifted(leaving, "section", 1)
         return (incoming, kept)
 
-    _, kept = lax.fori_loop(0, ticks, forward_tick, (blank, jnp.zeros(images.shape, jnp.bfloat16)))
+    spare = (micro_count + 2,) + images.shape[1:]
+    _, kept = lax.fori_loop(0, ticks, forward_tick, (blank, jnp.zeros(spare, jnp.bfloat16)))
 
     def run_backward(entering, upstream):
         return block_backward(entering, upstream, kernel, scale, weight_in, weight_out)
@@ -145,8 +146,8 @@
         )
 
     stores = (
-        jnp.zeros((micro_count, pixel_rows, width), jnp.bfloat16),
-        jnp.zeros((micro_count, pixel_rows, hidden_width), jnp.bfloat16),
+        jnp.zeros((micro_count + 2, pixel_rows, width), jnp.bfloat16),
+        jnp.zeros((micro_count + 2, pixel_rows, hidden_width), jnp.bfloat16),
     )
     summed = jnp.zeros((1,), jnp.float32)
 
@@ -157,49 +158,62 @@
         slot = jnp.clip(micro, 0, micro_count - 1)
         own = lax.dynamic_index_in_dim(cotangent, slot, 0, keepdims=False)
         upstream = jnp.where(section == sections - 1, own, incoming)
-        entering = lax.dynamic_index_in_dim(kept, slot, 0, keepdims=False)
+        entering = lax.dynamic_index_in_dim(kept, slot + 1, 0, keepdims=False)
         input_grad, flat, pre_grad = lax.cond(
             active, run_backward, skip_backward, entering, upstream
         )
-        grads = place(grads, input_grad, slot, active)
-        stored = (place(stored[0], flat, slot, active), place(stored[1], pre_grad, slot, active))
+        grads = place(grads, input_grad, micro, micro_count)
+        stored = (
+            place(stored[0], flat, micro, micro_count),
+            place(stored[1], pre_grad, micro, micro_count),
+        )
         incoming = shifted(input_grad, "section", -1)
         return (incoming, grads, stored, total)
 
     _, grads, stores, summed = lax.fori_loop(
-        0, ticks, backward_tick, (blank, jnp.zeros(images.shape, jnp.bfloat16), stores, summed)
-    )
-    all_flat = stores[0].reshape(micro_count * pixel_rows, width)
-    all_pre = stores[1].reshape(micro_count * pixel_rows, hidden_width)
+        0, ticks, backward_tick, (blank, jnp.zeros(spare, jnp.bfloat16), stores, summed)
+    )
+    grads = grads[1 : micro_count + 1]
+    all_flat = stores[0][1 : micro_count + 1].reshape(micro_count * pixel_rows, width)
+    all_pre = stores[1][1 : micro_count + 1].reshape(micro_count * pixel_rows, hidden_width)
     partial = (
         lax.dot_general(
             all_pre, all_flat, (((0,), (0,)), ((), ())), preferred_element_type=jnp.float32
         )
         * factor
     )
-    replicas = lax.axis_size("dp")
+    cores, rows, planes = (lax.axis_size(name) for name in ("core", "y", "z"))
+    replicas = cores * rows * planes
     share = (hidden_width // replicas) * width
     padded = -(-share // 1024) * 1024
     chunks = jnp.pad(partial.reshape(replicas, share), ((0, 0), (0, padded - share)))
     mine = lax.psum_scatter(
-        chunks.reshape(replicas, padded // 128, 128), "dp", scatter_dimension=0, tiled=True
+        chunks.reshape(replicas, padded // 128, 128), ("z", "y", "core"), scatter_dimension=0, tiled=True
     )
     sums = mine.reshape(padded)[:share].reshape(hidden_width // replicas, width)
     return (sums[None], grads[None])
 
 
 def solution(mesh):
+    sections, replicas = mesh.devices.shape
+    cores = 2
+    rows = int(round((replicas // cores) ** 0.5))
+    split = Mesh(
+        mesh.devices.reshape(sections, replicas // (rows * cores), rows, cores),
+        ("section", "z", "y", "core"),
+    )
+    dp = ("z", "y", "core")
     return jax.shard_map(
         body,
-        mesh=mesh,
+        mesh=split,
         in_specs=(
-            P(None, "dp", None, None, None),
-            P(None, "dp", None, None, None),
+            P(None, dp, None, None, None),
+            P(None, dp, None, None, None),
             P("section", None, None),
             P("section", None),
             P("section", None, None),
             P("section", None, None),
         ),
-        out_specs=(P("section", "dp", None), P("section", None, "dp", None, None, None)),
+        out_specs=(P("section", dp, None), P("section", None, dp, None, None, None)),
         check_vma=False,
     )

time: 633 us -> 573 us (0.905)
  other arithmetic: 85.4 us -> 44 us
    dynamic_slice x44 -> x0, local copies, waits for them, and re-layouts: 40.9 us -> none  [place(): former = lax.dynamic_index_in_dim(buffer, slot, 0, keepdims=False)]
    dynamic_update_slice x0 -> x33, local copies, waits for them, and re-layouts: none -> 33.2 us  [place(): return lax.dynamic_update_index_in_dim(buffer, value, slot, 0)]
    dynamic_update_slice x44 -> x11, other arithmetic: 35.2 us -> 7.46 us  [place(): return lax.dynamic_update_index_in_dim(buffer, value, slot, 0)]
    ppermute x22, waiting for transfers between devices: 147 us -> 138 us  [shifted(): return lax.ppermute(block, axis, route)]
    broadcast_in_dim x2 -> x24, local copies, waits for them, and re-layouts: 1.87 us -> 8.35 us  [the longest x21 5.31 us: place(): return lax.dynamic_update_index_in_dim(buffer, value, slot, 0)]
  transfers between devices with their start and end apart: 23 -> 23, of which waited for: 21 -> 22; matrix products, arithmetic and copies ran while one was open for 9% -> 6% of each run, Pallas kernels for 0% -> 0%
where the time goes in v2:
time: 573 us; the launch traced here: 572 us
  waiting for transfers between devices  344 us (60%)
  starting transfers between devices  77.5 us (14%)
  local copies, waits for them, and re-layouts  73 us (13%)
  other arithmetic  44 us (8%)
  matrix products  18.3 us (3%)
  between operations  14.1 us (2%)
    reduce_scatter x1, waiting for transfers between devices, body(): lax.psum_scatter(chunks.reshape(replicas, padded // 128, 128), ('z', 'y',...  206 us
    ppermute x22, waiting for transfers between devices, shifted(): return lax.ppermute(block, axis, route)  138 us
    ppermute x22, starting transfers between devices, shifted(): return lax.ppermute(block, axis, route)  77.5 us
    dynamic_update_slice x33, local copies, waits for them, and re-layouts, place(): return lax.dynamic_update_index_in_dim(buffer, value, slot, 0)  33.2 us
    reduce_sum x8, other arithmetic, block_inner(): center = mixed - jnp.mean(mixed, axis=-1, keepdims=True)  15.9 us
  transfers between devices with their start and end apart: 23, of which 22 were waited for; matrix products, arithmetic and copies ran while one was open for 6% of the time, Pallas kernels for 0%

profile of v2, /device:TPU:2, one launch (start us, length us, event | category | flops | bytes accessed | tf_op | source)
XLA Modules:
  0.0 571.7 jit_solution(18010770574180968541)
XLA Ops:
  15.5 119.2 %while.39 = (s32[]{:T(128)}, bf16[1,10,10,352]{3,2,1,0:T(8,128)(2,1)S(1)}, bf16[6,1,10,10,352]{4,3,2,1,0:T(8,128)(2,1)}, s32[]{:T(128)}, pred[]{:T(512)}, /*inde...) while((s32[]{:T(128)}, ...), condition=%wide.region_5.6_spmd, body=%wide.region_0.5_spmd.sunk | while | flops 202787312 | bytes 4433037 | solution.py:136
  19.6 17.3 %collective-permute-done = bf16[1,10,10,352]{3,2,1,0:T(8,128)(2,1)S(1)} collective-permute-done((bf16[1,10,10,352]{3,2,1,0:T(8,128)(2,1)S(1)}, bf16[1,10,10,352]{3,2,1,0:T(8,128)(2,1)S(1)}, u32[]{:S(2)}, u32[]{:S(2)}) %collective-permute-start) | collective-permute-done | bytes 70432 | tf_op jit(solution)/shard_map/while/body/eval_jaxpr/ppermute | solution.py:15
  37.6 3.5 conditional.4
  42.9 4.8 collective-permute-done
  53.9 4.8 collective-permute-done
  59.4 3.5 conditional.4
  64.8 4.8 collective-permute-done
  75.7 4.8 collective-permute-done
  81.2 5.4 collective-permute-start
  89.7 4.3 collective-permute-start
  97.2 5.4 collective-permute-start
  105.7 5.5 collective-permute-start
  114.4 9.1 %collective-permute-start = (bf16[1,10,10,352]{3,2,1,0:T(8,128)(2,1)S(1)}, bf16[1,10,10,352]{3,2,1,0:T(8,128)(2,1)S(1)}, u32[]{:S(2)}, u32[]{:S(2)}) collective-permute-start(bf16[1,10,10,352]{3,2,1,0:T(8,128)(2,1)S(1)} %get-tuple-element.1169), channel_id=1, source_target_pairs={{0,128},{128,256},{256,384},{384,512},{512,640},{640,768},{768,896... | collective-permute-start | bytes 211208 | tf_op jit(solution)/shard_map/while/body/eval_jaxpr/ppermute | solution.py:15
  126.6 5.6 collective-permute-start
  137.8 206.7 %while.40 = (s32[]{:T(128)}, bf16[1,10,10,352]{3,2,1,0:T(8,128)(2,1)S(1)}, bf16[6,1,10,10,352]{4,3,2,1,0:T(8,128)(2,1)}, bf16[6,100,352]{2,1,0:T(8,128)(2,1)}, b...) while((s32[]{:T(128)}, ...), condition=%wide.region_13.14_spmd, body=%wide.region_6.13_spmd.sunk | while | flops 306486496 | bytes 9684080 | solution.py:173
  144.2 3.9 collective-permute-done.1
  154.5 5.1 collective-permute-done.1
  193.6 57.7 %collective-permute-done.1 = bf16[1,10,10,352]{3,2,1,0:T(8,128)(2,1)S(1)} collective-permute-done((bf16[1,10,10,352]{3,2,1,0:T(8,128)(2,1)}, bf16[1,10,10,352]{3,2,1,0:T(8,128)(2,1)S(1)}, u32[]{:S(2)}, u32[]{:S(2)}) %collective-permute-start.1) | collective-permute-done | bytes 70432 | tf_op jit(solution)/shard_map/while/body/eval_jaxpr/ppermute | solution.py:15
  251.3 11.3 %conditional.5 = (bf16[1,10,10,352]{3,2,1,0:T(8,128)(2,1)}, bf16[1,1,10,10,352]{4,3,2,1,0:T(8,128)(2,1)S(1)}, bf16[1,100,352]{2,1,0:T(8,128)(2,1)S(1)}, bf16[1,100,1408]{2,1,0:T(8,128)(2,1)}) conditional(s32[]{:T(128)} %convert_element_type.126, () %tuple.212, (pred[]{:T(512)}, s32[]{:T(128)}, bf16[4,1,10,10,352]{4,3,2,1,0:T(8,128)(2,1)}, ...), branch_computations={%region_7.7_spmd, %region_8.12_spmd} | conditional | flops 306486496 | bytes 8472803 | solution.py:162
  270.8 11.3 %conditional.5 = (bf16[1,10,10,352]{3,2,1,0:T(8,128)(2,1)}, bf16[1,1,10,10,352]{4,3,2,1,0:T(8,128)(2,1)S(1)}, bf16[1,100,352]{2,1,0:T(8,128)(2,1)S(1)}, bf16[1,100,1408]{2,1,0:T(8,128)(2,1)}) conditional(s32[]{:T(128)} %convert_element_type.126, () %tuple.212, (pred[]{:T(512)}, s32[]{:T(128)}, bf16[4,1,10,10,352]{4,3,2,1,0:T(8,128)(2,1)}, ...), branch_computations={%region_7.7_spmd, %region_8.12_spmd} | conditional | flops 306486496 | bytes 8472803 | solution.py:162
  290.3 11.3 %conditional.5 = (bf16[1,10,10,352]{3,2,1,0:T(8,128)(2,1)}, bf16[1,1,10,10,352]{4,3,2,1,0:T(8,128)(2,1)S(1)}, bf16[1,100,352]{2,1,0:T(8,128)(2,1)S(1)}, bf16[1,100,1408]{2,1,0:T(8,128)(2,1)}) conditional(s32[]{:T(128)} %convert_element_type.126, () %tuple.212, (pred[]{:T(512)}, s32[]{:T(128)}, bf16[4,1,10,10,352]{4,3,2,1,0:T(8,128)(2,1)}, ...), branch_computations={%region_7.7_spmd, %region_8.12_spmd} | conditional | flops 306486496 | bytes 8472803 | solution.py:162
  309.8 11.3 %conditional.5 = (bf16[1,10,10,352]{3,2,1,0:T(8,128)(2,1)}, bf16[1,1,10,10,352]{4,3,2,1,0:T(8,128)(2,1)S(1)}, bf16[1,100,352]{2,1,0:T(8,128)(2,1)S(1)}, bf16[1,100,1408]{2,1,0:T(8,128)(2,1)}) conditional(s32[]{:T(128)} %convert_element_type.126, () %tuple.212, (pred[]{:T(512)}, s32[]{:T(128)}, bf16[4,1,10,10,352]{4,3,2,1,0:T(8,128)(2,1)}, ...), branch_computations={%region_7.7_spmd, %region_8.12_spmd} | conditional | flops 306486496 | bytes 8472803 | solution.py:162
  329.6 11.8 %collective-permute-start.1 = (bf16[1,10,10,352]{3,2,1,0:T(8,128)(2,1)}, bf16[1,10,10,352]{3,2,1,0:T(8,128)(2,1)S(1)}, u32[]{:S(2)}, u32[]{:S(2)}) collective-permute-start(bf16[1,10,10,352]{3,2,1,0:T(8,128)(2,1)} %get-tuple-element.1055), channel_id=1, source_target_pairs={{128,0},{256,128},{384,256},{512,384},{640,512},{768,640},{896,768... | collective-permute-start | bytes 211208 | tf_op jit(solution)/shard_map/while/body/eval_jaxpr/ppermute | solution.py:15
  357.6 205.8 %reduce-scatter.2.cloned.1.call-done = f32[1,32,128]{2,1,0:T(8,128)} async-done(((f32[128,32,128]{2,1,0:T(8,128)}), f32[1,32,128]{2,1,0:T(8,128)}) %reduce-scatter.2.cloned.1.call-update) | async-done | bytes 16400 | tf_op jit(solution)/shard_map/reduce_scatter | solution.py:190
  (307 shorter events, 217.2 us)
Async XLA Ops:
  7.2 3.9 copy-start.1
  7.2 556.3 %reduce-scatter.2.cloned.1.call-start = ((), (), s32[]{:S(2)}) async-start(), calls=%async_computation.1 | async-start | bytes 2113536 | tf_op jit(solution)/shard_map/reduce_scatter | solution.py:190
  16.1 20.7 %collective-permute-start = (bf16[1,10,10,352]{3,2,1,0:T(8,128)(2,1)S(1)}, bf16[1,10,10,352]{3,2,1,0:T(8,128)(2,1)S(1)}, u32[]{:S(2)}, u32[]{:S(2)}) collective-permute-start(bf16[1,10,10,352]{3,2,1,0:T(8,128)(2,1)S(1)} %get-tuple-element.1169), channel_id=1, source_target_pairs={{0,128},{128,256},{256,384},{384,512},{512,640},{640,768},{768,896... | collective-permute-start | bytes 211208 | tf_op jit(solution)/shard_map/while/body/eval_jaxpr/ppermute | solution.py:15
  41.0 6.8 %collective-permute-start = (bf16[1,10,10,352]{3,2,1,0:T(8,128)(2,1)S(1)}, bf16[1,10,10,352]{3,2,1,0:T(8,128)(2,1)S(1)}, u32[]{:S(2)}, u32[]{:S(2)}) collective-permute-start(bf16[1,10,10,352]{3,2,1,0:T(8,128)(2,1)S(1)} %get-tuple-element.1169), channel_id=1, source_target_pairs={{0,128},{128,256},{256,384},{384,512},{512,640},{640,768},{768,896... | collective-permute-start | bytes 211208 | tf_op jit(solution)/shard_map/while/body/eval_jaxpr/ppermute | solution.py:15
  51.9 6.8 %collective-permute-start = (bf16[1,10,10,352]{3,2,1,0:T(8,128)(2,1)S(1)}, bf16[1,10,10,352]{3,2,1,0:T(8,128)(2,1)S(1)}, u32[]{:S(2)}, u32[]{:S(2)}) collective-permute-start(bf16[1,10,10,352]{3,2,1,0:T(8,128)(2,1)S(1)} %get-tuple-element.1169), channel_id=1, source_target_pairs={{0,128},{128,256},{256,384},{384,512},{512,640},{640,768},{768,896... | collective-permute-start | bytes 211208 | tf_op jit(solution)/shard_map/while/body/eval_jaxpr/ppermute | solution.py:15
  62.8 6.8 %collective-permute-start = (bf16[1,10,10,352]{3,2,1,0:T(8,128)(2,1)S(1)}, bf16[1,10,10,352]{3,2,1,0:T(8,128)(2,1)S(1)}, u32[]{:S(2)}, u32[]{:S(2)}) collective-permute-start(bf16[1,10,10,352]{3,2,1,0:T(8,128)(2,1)S(1)} %get-tuple-element.1169), channel_id=1, source_target_pairs={{0,128},{128,256},{256,384},{384,512},{512,640},{640,768},{768,896... | collective-permute-start | bytes 211208 | tf_op jit(solution)/shard_map/while/body/eval_jaxpr/ppermute | solution.py:15
  73.8 6.8 %collective-permute-start = (bf16[1,10,10,352]{3,2,1,0:T(8,128)(2,1)S(1)}, bf16[1,10,10,352]{3,2,1,0:T(8,128)(2,1)S(1)}, u32[]{:S(2)}, u32[]{:S(2)}) collective-permute-start(bf16[1,10,10,352]{3,2,1,0:T(8,128)(2,1)S(1)} %get-tuple-element.1169), channel_id=1, source_target_pairs={{0,128},{128,256},{256,384},{384,512},{512,640},{640,768},{768,896... | collective-permute-start | bytes 211208 | tf_op jit(solution)/shard_map/while/body/eval_jaxpr/ppermute | solution.py:15
  81.2 7.8 %collective-permute-start = (bf16[1,10,10,352]{3,2,1,0:T(8,128)(2,1)S(1)}, bf16[1,10,10,352]{3,2,1,0:T(8,128)(2,1)S(1)}, u32[]{:S(2)}, u32[]{:S(2)}) collective-permute-start(bf16[1,10,10,352]{3,2,1,0:T(8,128)(2,1)S(1)} %get-tuple-element.1169), channel_id=1, source_target_pairs={{0,128},{128,256},{256,384},{384,512},{512,640},{640,768},{768,896... | collective-permute-start | bytes 211208 | tf_op jit(solution)/shard_map/while/body/eval_jaxpr/ppermute | solution.py:15
  89.7 6.8 %collective-permute-start = (bf16[1,10,10,352]{3,2,1,0:T(8,128)(2,1)S(1)}, bf16[1,10,10,352]{3,2,1,0:T(8,128)(2,1)S(1)}, u32[]{:S(2)}, u32[]{:S(2)}) collective-permute-start(bf16[1,10,10,352]{3,2,1,0:T(8,128)(2,1)S(1)} %get-tuple-element.1169), channel_id=1, source_target_pairs={{0,128},{128,256},{256,384},{384,512},{512,640},{640,768},{768,896... | collective-permute-start | bytes 211208 | tf_op jit(solution)/shard_map/while/body/eval_jaxpr/ppermute | solution.py:15
  97.2 7.8 %collective-permute-start = (bf16[1,10,10,352]{3,2,1,0:T(8,128)(2,1)S(1)}, bf16[1,10,10,352]{3,2,1,0:T(8,128)(2,1)S(1)}, u32[]{:S(2)}, u32[]{:S(2)}) collective-permute-start(bf16[1,10,10,352]{3,2,1,0:T(8,128)(2,1)S(1)} %get-tuple-element.1169), channel_id=1, source_target_pairs={{0,128},{128,256},{256,384},{384,512},{512,640},{640,768},{768,896... | collective-permute-start | bytes 211208 | tf_op jit(solution)/shard_map/while/body/eval_jaxpr/ppermute | solution.py:15
  105.7 8.0 %collective-permute-start = (bf16[1,10,10,352]{3,2,1,0:T(8,128)(2,1)S(1)}, bf16[1,10,10,352]{3,2,1,0:T(8,128)(2,1)S(1)}, u32[]{:S(2)}, u32[]{:S(2)}) collective-permute-start(bf16[1,10,10,352]{3,2,1,0:T(8,128)(2,1)S(1)} %get-tuple-element.1169), channel_id=1, source_target_pairs={{0,128},{128,256},{256,384},{384,512},{512,640},{640,768},{768,896... | collective-permute-start | bytes 211208 | tf_op jit(solution)/shard_map/while/body/eval_jaxpr/ppermute | solution.py:15
  114.4 11.6 %collective-permute-start = (bf16[1,10,10,352]{3,2,1,0:T(8,128)(2,1)S(1)}, bf16[1,10,10,352]{3,2,1,0:T(8,128)(2,1)S(1)}, u32[]{:S(2)}, u32[]{:S(2)}) collective-permute-start(bf16[1,10,10,352]{3,2,1,0:T(8,128)(2,1)S(1)} %get-tuple-element.1169), channel_id=1, source_target_pairs={{0,128},{128,256},{256,384},{384,512},{512,640},{640,768},{768,896... | collective-permute-start | bytes 211208 | tf_op jit(solution)/shard_map/while/body/eval_jaxpr/ppermute | solution.py:15
  126.6 8.0 %collective-permute-start = (bf16[1,10,10,352]{3,2,1,0:T(8,128)(2,1)S(1)}, bf16[1,10,10,352]{3,2,1,0:T(8,128)(2,1)S(1)}, u32[]{:S(2)}, u32[]{:S(2)}) collective-permute-start(bf16[1,10,10,352]{3,2,1,0:T(8,128)(2,1)S(1)} %get-tuple-element.1169), channel_id=1, source_target_pairs={{0,128},{128,256},{256,384},{384,512},{512,640},{640,768},{768,896... | collective-permute-start | bytes 211208 | tf_op jit(solution)/shard_map/while/body/eval_jaxpr/ppermute | solution.py:15
  139.2 8.9 %collective-permute-start.1 = (bf16[1,10,10,352]{3,2,1,0:T(8,128)(2,1)}, bf16[1,10,10,352]{3,2,1,0:T(8,128)(2,1)S(1)}, u32[]{:S(2)}, u32[]{:S(2)}) collective-permute-start(bf16[1,10,10,352]{3,2,1,0:T(8,128)(2,1)} %get-tuple-element.1055), channel_id=1, source_target_pairs={{128,0},{256,128},{384,256},{512,384},{640,512},{768,640},{896,768... | collective-permute-start | bytes 211208 | tf_op jit(solution)/shard_map/while/body/eval_jaxpr/ppermute | solution.py:15
  149.6 10.1 %collective-permute-start.1 = (bf16[1,10,10,352]{3,2,1,0:T(8,128)(2,1)}, bf16[1,10,10,352]{3,2,1,0:T(8,128)(2,1)S(1)}, u32[]{:S(2)}, u32[]{:S(2)}) collective-permute-start(bf16[1,10,10,352]{3,2,1,0:T(8,128)(2,1)} %get-tuple-element.1055), channel_id=1, source_target_pairs={{128,0},{256,128},{384,256},{512,384},{640,512},{768,640},{896,768... | collective-permute-start | bytes 211208 | tf_op jit(solution)/shard_map/while/body/eval_jaxpr/ppermute | solution.py:15
  161.1 7.0 %collective-permute-start.1 = (bf16[1,10,10,352]{3,2,1,0:T(8,128)(2,1)}, bf16[1,10,10,352]{3,2,1,0:T(8,128)(2,1)S(1)}, u32[]{:S(2)}, u32[]{:S(2)}) collective-permute-start(bf16[1,10,10,352]{3,2,1,0:T(8,128)(2,1)} %get-tuple-element.1055), channel_id=1, source_target_pairs={{128,0},{256,128},{384,256},{512,384},{640,512},{768,640},{896,768... | collective-permute-start | bytes 211208 | tf_op jit(solution)/shard_map/while/body/eval_jaxpr/ppermute | solution.py:15
  169.5 8.1 %collective-permute-start.1 = (bf16[1,10,10,352]{3,2,1,0:T(8,128)(2,1)}, bf16[1,10,10,352]{3,2,1,0:T(8,128)(2,1)S(1)}, u32[]{:S(2)}, u32[]{:S(2)}) collective-permute-start(bf16[1,10,10,352]{3,2,1,0:T(8,128)(2,1)} %get-tuple-element.1055), channel_id=1, source_target_pairs={{128,0},{256,128},{384,256},{512,384},{640,512},{768,640},{896,768... | collective-permute-start | bytes 211208 | tf_op jit(solution)/shard_map/while/body/eval_jaxpr/ppermute | solution.py:15
  179.0 8.2 %collective-permute-start.1 = (bf16[1,10,10,352]{3,2,1,0:T(8,128)(2,1)}, bf16[1,10,10,352]{3,2,1,0:T(8,128)(2,1)S(1)}, u32[]{:S(2)}, u32[]{:S(2)}) collective-permute-start(bf16[1,10,10,352]{3,2,1,0:T(8,128)(2,1)} %get-tuple-element.1055), channel_id=1, source_target_pairs={{128,0},{256,128},{384,256},{512,384},{640,512},{768,640},{896,768... | collective-permute-start | bytes 211208 | tf_op jit(solution)/shard_map/while/body/eval_jaxpr/ppermute | solution.py:15
  188.6 62.6 %collective-permute-start.1 = (bf16[1,10,10,352]{3,2,1,0:T(8,128)(2,1)}, bf16[1,10,10,352]{3,2,1,0:T(8,128)(2,1)S(1)}, u32[]{:S(2)}, u32[]{:S(2)}) collective-permute-start(bf16[1,10,10,352]{3,2,1,0:T(8,128)(2,1)} %get-tuple-element.1055), channel_id=1, source_target_pairs={{128,0},{256,128},{384,256},{512,384},{640,512},{768,640},{896,768... | collective-permute-start | bytes 211208 | tf_op jit(solution)/shard_map/while/body/eval_jaxpr/ppermute | solution.py:15
  262.6 8.2 %collective-permute-start.1 = (bf16[1,10,10,352]{3,2,1,0:T(8,128)(2,1)}, bf16[1,10,10,352]{3,2,1,0:T(8,128)(2,1)S(1)}, u32[]{:S(2)}, u32[]{:S(2)}) collective-permute-start(bf16[1,10,10,352]{3,2,1,0:T(8,128)(2,1)} %get-tuple-element.1055), channel_id=1, source_target_pairs={{128,0},{256,128},{384,256},{512,384},{640,512},{768,640},{896,768... | collective-permute-start | bytes 211208 | tf_op jit(solution)/shard_map/while/body/eval_jaxpr/ppermute | solution.py:15
  282.1 8.2 %collective-permute-start.1 = (bf16[1,10,10,352]{3,2,1,0:T(8,128)(2,1)}, bf16[1,10,10,352]{3,2,1,0:T(8,128)(2,1)S(1)}, u32[]{:S(2)}, u32[]{:S(2)}) collective-permute-start(bf16[1,10,10,352]{3,2,1,0:T(8,128)(2,1)} %get-tuple-element.1055), channel_id=1, source_target_pairs={{128,0},{256,128},{384,256},{512,384},{640,512},{768,640},{896,768... | collective-permute-start | bytes 211208 | tf_op jit(solution)/shard_map/while/body/eval_jaxpr/ppermute | solution.py:15
  301.7 8.2 %collective-permute-start.1 = (bf16[1,10,10,352]{3,2,1,0:T(8,128)(2,1)}, bf16[1,10,10,352]{3,2,1,0:T(8,128)(2,1)S(1)}, u32[]{:S(2)}, u32[]{:S(2)}) collective-permute-start(bf16[1,10,10,352]{3,2,1,0:T(8,128)(2,1)} %get-tuple-element.1055), channel_id=1, source_target_pairs={{128,0},{256,128},{384,256},{512,384},{640,512},{768,640},{896,768... | collective-permute-start | bytes 211208 | tf_op jit(solution)/shard_map/while/body/eval_jaxpr/ppermute | solution.py:15
  321.2 7.0 %collective-permute-start.1 = (bf16[1,10,10,352]{3,2,1,0:T(8,128)(2,1)}, bf16[1,10,10,352]{3,2,1,0:T(8,128)(2,1)S(1)}, u32[]{:S(2)}, u32[]{:S(2)}) collective-permute-start(bf16[1,10,10,352]{3,2,1,0:T(8,128)(2,1)} %get-tuple-element.1055), channel_id=1, source_target_pairs={{128,0},{256,128},{384,256},{512,384},{640,512},{768,640},{896,768... | collective-permute-start | bytes 211208 | tf_op jit(solution)/shard_map/while/body/eval_jaxpr/ppermute | solution.py:15
  329.6 14.8 %collective-permute-start.1 = (bf16[1,10,10,352]{3,2,1,0:T(8,128)(2,1)}, bf16[1,10,10,352]{3,2,1,0:T(8,128)(2,1)S(1)}, u32[]{:S(2)}, u32[]{:S(2)}) collective-permute-start(bf16[1,10,10,352]{3,2,1,0:T(8,128)(2,1)} %get-tuple-element.1055), channel_id=1, source_target_pairs={{128,0},{256,128},{384,256},{512,384},{640,512},{768,640},{896,768... | collective-permute-start | bytes 211208 | tf_op jit(solution)/shard_map/while/body/eval_jaxpr/ppermute | solution.py:15
  (2 other events, 4.3 us)
Sparse Core Ops, SparseCore 0:
  355.6 207.7 reduce-scatter.1

commit v3 on v2

--- a/solution.py
+++ b/solution.py
@@ -100,6 +100,15 @@
     return lax.dynamic_update_index_in_dim(buffer, value, slot, 0)
 
 
+def halve(chunks, axis, bit):
+    mine = (lax.axis_index(axis) // bit) % 2
+    pairs = chunks.reshape((chunks.shape[0] // 2, 2) + chunks.shape[1:])
+    keep = lax.dynamic_index_in_dim(pairs, mine, 1, keepdims=False)
+    send = lax.dynamic_index_in_dim(pairs, 1 - mine, 1, keepdims=False)
+    route = [(i, i ^ bit) for i in range(lax.axis_size(axis))]
+    return keep + lax.ppermute(send, axis, route)
+
+
 def body(images, cotangent, dw_kernel, layer_scale, w_in, w_out):
     section = lax.axis_index("section")
     sections = lax.axis_size("section")
@@ -182,15 +191,19 @@
         )
         * factor
     )
-    cores, rows, planes = (lax.axis_size(name) for name in ("core", "y", "z"))
-    replicas = cores * rows * planes
+    replicas = 1
+    for name in ("z", "y", "core"):
+        replicas *= lax.axis_size(name)
     share = (hidden_width // replicas) * width
     padded = -(-share // 1024) * 1024
     chunks = jnp.pad(partial.reshape(replicas, share), ((0, 0), (0, padded - share)))
-    mine = lax.psum_scatter(
-        chunks.reshape(replicas, padded // 128, 128), ("z", "y", "core"), scatter_dimension=0, tiled=True
-    )
-    sums = mine.reshape(padded)[:share].reshape(hidden_width // replicas, width)
+    chunks = chunks.reshape(replicas, padded // 128, 128)
+    for name in ("core", "y", "z"):
+        bit = 1
+        while bit < lax.axis_size(name):
+            chunks = halve(chunks, name, bit)
+            bit *= 2
+    sums = chunks.reshape(padded)[:share].reshape(hidden_width // replicas, width)
     return (sums[None], grads[None])
 
 

time: 573 us -> 562 us (0.981)
  waiting for transfers between devices: 344 us -> 263 us
  starting transfers between devices: 77.5 us -> 109 us
  local copies, waits for them, and re-layouts: 73 us -> 98.7 us
  other arithmetic: 44 us -> 58.4 us
  between operations: 14.1 us -> 1.11 us
    reduce_scatter x1 -> x0, waiting for transfers between devices: 206 us -> none  [body(): lax.psum_scatter(chunks.reshape(replicas, padded // 128, 128), ('z', 'y',...]
    ppermute x22, waiting for transfers between devices: 138 us -> 209 us  [shifted(): return lax.ppermute(block, axis, route)]
    ppermute x0 -> x7, waiting for transfers between devices: none -> 54 us  [halve(): return keep + lax.ppermute(send, axis, route)]
    slice x24, local copies, waits for them, and re-layouts: 2.16 us -> 28.9 us  [depthwise(): kernel[row * KS + col]]
    ppermute x22, starting transfers between devices: 77.5 us -> 94.6 us  [shifted(): return lax.ppermute(block, axis, route)]
    ppermute x0 -> x7, starting transfers between devices: none -> 14.7 us  [halve(): return keep + lax.ppermute(send, axis, route)]
    another operation x8, other arithmetic: 0.16 us -> 7.97 us
  transfers between devices with their start and end apart: 23 -> 29, of which waited for: 22 -> 28; matrix products, arithmetic and copies ran while one was open for 6% -> 6% of each run, Pallas kernels for 0% -> 0%
where the time goes in v3:
time: 562 us; the launch traced here: 558 us
  waiting for transfers between devices  263 us (47%)
  starting transfers between devices  109 us (19%)
  local copies, waits for them, and re-layouts  98.7 us (18%)
  other arithmetic  58.4 us (10%)
  matrix products  20.9 us (4%)
  loops' own time  5.94 us (1%)
    ppermute x22, waiting for transfers between devices, shifted(): return lax.ppermute(block, axis, route)  209 us
    ppermute x22, starting transfers between devices, shifted(): return lax.ppermute(block, axis, route)  94.6 us
    ppermute x7, waiting for transfers between devices, halve(): return keep + lax.ppermute(send, axis, route)  54 us
    dynamic_update_slice x33, local copies, waits for them, and re-layouts, place(): return lax.dynamic_update_index_in_dim(buffer, value, slot, 0)  33.2 us
    slice x24, local copies, waits for them, and re-layouts, depthwise(): kernel[row * KS + col]  28.9 us
    reduce_sum x8, other arithmetic, block_inner(): center = mixed - jnp.mean(mixed, axis=-1, keepdims=True)  18.4 us
    ppermute x7, starting transfers between devices, halve(): return keep + lax.ppermute(send, axis, route)  14.7 us
    convert_element_type x4, other arithmetic, block_backward(): (upstream.astype(jnp.float32) + depthwise_adjoint(mixed_grad, kernel)).as...  11.6 us
  transfers between devices with their start and end apart: 29, of which 28 were waited for; matrix products, arithmetic and copies ran while one was open for 6% of the time, Pallas kernels for 0%

profile of v3, /device:TPU:2, one launch (start us, length us, event | category | flops | bytes accessed | tf_op | source)
XLA Modules:
  0.0 557.9 jit_solution(3596674816130258496)
XLA Ops:
  9.5 149.4 %while.39 = (s32[]{:T(128)}, bf16[1,10,10,352]{3,2,1,0:T(8,128)(2,1)S(1)}, bf16[6,1,10,10,352]{4,3,2,1,0:T(8,128)(2,1)}, s32[]{:T(128)}, pred[]{:T(512)}, /*inde...) while((s32[]{:T(128)}, ...), condition=%wide.region_5.6_spmd, body=%wide.region_0.5_spmd.sunk | while | flops 202787312 | bytes 4433037 | solution.py:145
  13.6 21.6 %collective-permute-done = bf16[1,10,10,352]{3,2,1,0:T(8,128)(2,1)S(1)} collective-permute-done((bf16[1,10,10,352]{3,2,1,0:T(8,128)(2,1)S(1)}, bf16[1,10,10,352]{3,2,1,0:T(8,128)(2,1)S(1)}, u32[]{:S(2)}, u32[]{:S(2)}) %collective-permute-start) | collective-permute-done | bytes 70432 | tf_op jit(solution)/shard_map/while/body/eval_jaxpr/ppermute | solution.py:15
  35.9 7.2 %conditional.4 = (bf16[1,10,10,352]{3,2,1,0:T(8,128)(2,1)S(1)}) conditional(s32[]{:T(128)} %convert_element_type.125, () %tuple.209, (bf16[1,10,10,352]{3,2,1,0:T(8,128)(2,1)S(1)}, f32[1,352]{1,0:T(1,128)}, f32[49,352]{1,0:T(8,128)}, bf16[1408,352]{1,0:T(8,128)(2,1)S(1)}, bf16[1408,352]{1,0:T(8,128)(2,1)S(1)}) %tuple.210), branch_computations={%region_1.1_spmd, %region_2.4_spmd} | conditional | flops 202752096 | bytes 3816476 | solution.py:139
  50.5 7.2 %conditional.4 = (bf16[1,10,10,352]{3,2,1,0:T(8,128)(2,1)S(1)}) conditional(s32[]{:T(128)} %convert_element_type.125, () %tuple.209, (bf16[1,10,10,352]{3,2,1,0:T(8,128)(2,1)S(1)}, f32[1,352]{1,0:T(1,128)}, f32[49,352]{1,0:T(8,128)}, bf16[1408,352]{1,0:T(8,128)(2,1)S(1)}, bf16[1408,352]{1,0:T(8,128)(2,1)S(1)}) %tuple.210), branch_computations={%region_1.1_spmd, %region_2.4_spmd} | conditional | flops 202752096 | bytes 3816476 | solution.py:139
  65.2 7.2 %conditional.4 = (bf16[1,10,10,352]{3,2,1,0:T(8,128)(2,1)S(1)}) conditional(s32[]{:T(128)} %convert_element_type.125, () %tuple.209, (bf16[1,10,10,352]{3,2,1,0:T(8,128)(2,1)S(1)}, f32[1,352]{1,0:T(1,128)}, f32[49,352]{1,0:T(8,128)}, bf16[1408,352]{1,0:T(8,128)(2,1)S(1)}, bf16[1408,352]{1,0:T(8,128)(2,1)S(1)}) %tuple.210), branch_computations={%region_1.1_spmd, %region_2.4_spmd} | conditional | flops 202752096 | bytes 3816476 | solution.py:139
  79.8 7.2 %conditional.4 = (bf16[1,10,10,352]{3,2,1,0:T(8,128)(2,1)S(1)}) conditional(s32[]{:T(128)} %convert_element_type.125, () %tuple.209, (bf16[1,10,10,352]{3,2,1,0:T(8,128)(2,1)S(1)}, f32[1,352]{1,0:T(1,128)}, f32[49,352]{1,0:T(8,128)}, bf16[1408,352]{1,0:T(8,128)(2,1)S(1)}, bf16[1408,352]{1,0:T(8,128)(2,1)S(1)}) %tuple.210), branch_computations={%region_1.1_spmd, %region_2.4_spmd} | conditional | flops 202752096 | bytes 3816476 | solution.py:139
  95.2 8.4 %collective-permute-start = (bf16[1,10,10,352]{3,2,1,0:T(8,128)(2,1)S(1)}, bf16[1,10,10,352]{3,2,1,0:T(8,128)(2,1)S(1)}, u32[]{:S(2)}, u32[]{:S(2)}) collective-permute-start(bf16[1,10,10,352]{3,2,1,0:T(8,128)(2,1)S(1)} %get-tuple-element.1169), channel_id=1, source_target_pairs={{0,128},{128,256},{256,384},{384,512},{512,640},{640,768},{768,896... | collective-permute-start | bytes 211208 | tf_op jit(solution)/shard_map/while/body/eval_jaxpr/ppermute | solution.py:15
  114.2 9.1 %collective-permute-start = (bf16[1,10,10,352]{3,2,1,0:T(8,128)(2,1)S(1)}, bf16[1,10,10,352]{3,2,1,0:T(8,128)(2,1)S(1)}, u32[]{:S(2)}, u32[]{:S(2)}) collective-permute-start(bf16[1,10,10,352]{3,2,1,0:T(8,128)(2,1)S(1)} %get-tuple-element.1169), channel_id=1, source_target_pairs={{0,128},{128,256},{256,384},{384,512},{512,640},{640,768},{768,896... | collective-permute-start | bytes 211208 | tf_op jit(solution)/shard_map/while/body/eval_jaxpr/ppermute | solution.py:15
  126.9 5.8 %collective-permute-start = (bf16[1,10,10,352]{3,2,1,0:T(8,128)(2,1)S(1)}, bf16[1,10,10,352]{3,2,1,0:T(8,128)(2,1)S(1)}, u32[]{:S(2)}, u32[]{:S(2)}) collective-permute-start(bf16[1,10,10,352]{3,2,1,0:T(8,128)(2,1)S(1)} %get-tuple-element.1169), channel_id=1, source_target_pairs={{0,128},{128,256},{256,384},{384,512},{512,640},{640,768},{768,896... | collective-permute-start | bytes 211208 | tf_op jit(solution)/shard_map/while/body/eval_jaxpr/ppermute | solution.py:15
  136.8 11.0 %collective-permute-start = (bf16[1,10,10,352]{3,2,1,0:T(8,128)(2,1)S(1)}, bf16[1,10,10,352]{3,2,1,0:T(8,128)(2,1)S(1)}, u32[]{:S(2)}, u32[]{:S(2)}) collective-permute-start(bf16[1,10,10,352]{3,2,1,0:T(8,128)(2,1)S(1)} %get-tuple-element.1169), channel_id=1, source_target_pairs={{0,128},{128,256},{256,384},{384,512},{512,640},{640,768},{768,896... | collective-permute-start | bytes 211208 | tf_op jit(solution)/shard_map/while/body/eval_jaxpr/ppermute | solution.py:15
  150.9 5.6 collective-permute-start
  162.0 313.5 %while.40 = (s32[]{:T(128)}, bf16[1,10,10,352]{3,2,1,0:T(8,128)(2,1)S(1)}, bf16[6,1,10,10,352]{4,3,2,1,0:T(8,128)(2,1)}, bf16[6,100,352]{2,1,0:T(8,128)(2,1)}, b...) while((s32[]{:T(128)}, ...), condition=%wide.region_13.14_spmd, body=%wide.region_6.13_spmd.sunk | while | flops 306486496 | bytes 10125560 | solution.py:182
  168.4 6.0 %collective-permute-done.1 = bf16[1,10,10,352]{3,2,1,0:T(8,128)(2,1)S(1)} collective-permute-done((bf16[1,10,10,352]{3,2,1,0:T(8,128)(2,1)}, bf16[1,10,10,352]{3,2,1,0:T(8,128)(2,1)S(1)}, u32[]{:S(2)}, u32[]{:S(2)}) %collective-permute-start.1) | collective-permute-done | bytes 70432 | tf_op jit(solution)/shard_map/while/body/eval_jaxpr/ppermute | solution.py:15
  190.9 6.0 %collective-permute-done.1 = bf16[1,10,10,352]{3,2,1,0:T(8,128)(2,1)S(1)} collective-permute-done((bf16[1,10,10,352]{3,2,1,0:T(8,128)(2,1)}, bf16[1,10,10,352]{3,2,1,0:T(8,128)(2,1)S(1)}, u32[]{:S(2)}, u32[]{:S(2)}) %collective-permute-start.1) | collective-permute-done | bytes 70432 | tf_op jit(solution)/shard_map/while/body/eval_jaxpr/ppermute | solution.py:15
  212.9 6.4 %collective-permute-done.1 = bf16[1,10,10,352]{3,2,1,0:T(8,128)(2,1)S(1)} collective-permute-done((bf16[1,10,10,352]{3,2,1,0:T(8,128)(2,1)}, bf16[1,10,10,352]{3,2,1,0:T(8,128)(2,1)S(1)}, u32[]{:S(2)}, u32[]{:S(2)}) %collective-permute-start.1) | collective-permute-done | bytes 70432 | tf_op jit(solution)/shard_map/while/body/eval_jaxpr/ppermute | solution.py:15
  225.7 113.6 %collective-permute-done.1 = bf16[1,10,10,352]{3,2,1,0:T(8,128)(2,1)S(1)} collective-permute-done((bf16[1,10,10,352]{3,2,1,0:T(8,128)(2,1)}, bf16[1,10,10,352]{3,2,1,0:T(8,128)(2,1)S(1)}, u32[]{:S(2)}, u32[]{:S(2)}) %collective-permute-start.1) | collective-permute-done | bytes 70432 | tf_op jit(solution)/shard_map/while/body/eval_jaxpr/ppermute | solution.py:15
  339.2 19.7 %conditional.5 = (bf16[1,10,10,352]{3,2,1,0:T(8,128)(2,1)}, bf16[1,1,10,10,352]{4,3,2,1,0:T(8,128)(2,1)S(1)}, bf16[1,100,352]{2,1,0:T(8,128)(2,1)S(1)}, bf16[1,100,1408]{2,1,0:T(8,128)(2,1)}) conditional(s32[]{:T(128)} %convert_element_type.126, () %tuple.212, (pred[]{:T(512)}, s32[]{:T(128)}, bf16[4,1,10,10,352]{4,3,2,1,0:T(8,128)(2,1)}, ...), branch_computations={%region_7.7_spmd, %region_8.12_spmd} | conditional | flops 306486496 | bytes 8914283 | solution.py:171
  367.1 19.7 %conditional.5 = (bf16[1,10,10,352]{3,2,1,0:T(8,128)(2,1)}, bf16[1,1,10,10,352]{4,3,2,1,0:T(8,128)(2,1)S(1)}, bf16[1,100,352]{2,1,0:T(8,128)(2,1)S(1)}, bf16[1,100,1408]{2,1,0:T(8,128)(2,1)}) conditional(s32[]{:T(128)} %convert_element_type.126, () %tuple.212, (pred[]{:T(512)}, s32[]{:T(128)}, bf16[4,1,10,10,352]{4,3,2,1,0:T(8,128)(2,1)}, ...), branch_computations={%region_7.7_spmd, %region_8.12_spmd} | conditional | flops 306486496 | bytes 8914283 | solution.py:171
  395.0 19.7 %conditional.5 = (bf16[1,10,10,352]{3,2,1,0:T(8,128)(2,1)}, bf16[1,1,10,10,352]{4,3,2,1,0:T(8,128)(2,1)S(1)}, bf16[1,100,352]{2,1,0:T(8,128)(2,1)S(1)}, bf16[1,100,1408]{2,1,0:T(8,128)(2,1)}) conditional(s32[]{:T(128)} %convert_element_type.126, () %tuple.212, (pred[]{:T(512)}, s32[]{:T(128)}, bf16[4,1,10,10,352]{4,3,2,1,0:T(8,128)(2,1)}, ...), branch_computations={%region_7.7_spmd, %region_8.12_spmd} | conditional | flops 306486496 | bytes 8914283 | solution.py:171
  424.2 19.7 %conditional.5 = (bf16[1,10,10,352]{3,2,1,0:T(8,128)(2,1)}, bf16[1,1,10,10,352]{4,3,2,1,0:T(8,128)(2,1)S(1)}, bf16[1,100,352]{2,1,0:T(8,128)(2,1)S(1)}, bf16[1,100,1408]{2,1,0:T(8,128)(2,1)}) conditional(s32[]{:T(128)} %convert_element_type.126, () %tuple.212, (pred[]{:T(512)}, s32[]{:T(128)}, bf16[4,1,10,10,352]{4,3,2,1,0:T(8,128)(2,1)}, ...), branch_computations={%region_7.7_spmd, %region_8.12_spmd} | conditional | flops 306486496 | bytes 8914283 | solution.py:171
  452.3 20.2 %collective-permute-start.1 = (bf16[1,10,10,352]{3,2,1,0:T(8,128)(2,1)}, bf16[1,10,10,352]{3,2,1,0:T(8,128)(2,1)S(1)}, u32[]{:S(2)}, u32[]{:S(2)}) collective-permute-start(bf16[1,10,10,352]{3,2,1,0:T(8,128)(2,1)} %get-tuple-element.1055), channel_id=1, source_target_pairs={{128,0},{256,128},{384,256},{512,384},{640,512},{768,640},{896,768... | collective-permute-start | bytes 211208 | tf_op jit(solution)/shard_map/while/body/eval_jaxpr/ppermute | solution.py:15
  493.5 13.9 %collective-permute-done.3 = f32[32,32,128]{2,1,0:T(8,128)S(1)} collective-permute-done((f32[32,32,128]{2,1,0:T(8,128)S(1)}, f32[32,32,128]{2,1,0:T(8,128)S(1)}, u32[]{:S(2)}, u32[]{:S(2)}) %collective-permute-start.3) | collective-permute-done | bytes 524320 | tf_op jit(solution)/shard_map/ppermute | solution.py:109
  509.5 14.0 %collective-permute-done.4 = f32[16,32,128]{2,1,0:T(8,128)S(1)} collective-permute-done((f32[16,32,128]{2,1,0:T(8,128)S(1)}, f32[16,32,128]{2,1,0:T(8,128)S(1)}, u32[]{:S(2)}, u32[]{:S(2)}) %collective-permute-start.4) | collective-permute-done | bytes 262176 | tf_op jit(solution)/shard_map/ppermute | solution.py:109
  525.5 9.2 %collective-permute-done.5 = f32[8,32,128]{2,1,0:T(8,128)S(1)} collective-permute-done((f32[8,32,128]{2,1,0:T(8,128)S(1)}, f32[8,32,128]{2,1,0:T(8,128)S(1)}, u32[]{:S(2)}, u32[]{:S(2)}) %collective-permute-start.5) | collective-permute-done | bytes 131104 | tf_op jit(solution)/shard_map/ppermute | solution.py:109
  (954 shorter events, 310.4 us)
Async XLA Ops:
  10.2 25.0 %collective-permute-start = (bf16[1,10,10,352]{3,2,1,0:T(8,128)(2,1)S(1)}, bf16[1,10,10,352]{3,2,1,0:T(8,128)(2,1)S(1)}, u32[]{:S(2)}, u32[]{:S(2)}) collective-permute-start(bf16[1,10,10,352]{3,2,1,0:T(8,128)(2,1)S(1)} %get-tuple-element.1169), channel_id=1, source_target_pairs={{0,128},{128,256},{256,384},{384,512},{512,640},{640,768},{768,896... | collective-permute-start | bytes 211208 | tf_op jit(solution)/shard_map/while/body/eval_jaxpr/ppermute | solution.py:15
  43.1 6.8 %collective-permute-start = (bf16[1,10,10,352]{3,2,1,0:T(8,128)(2,1)S(1)}, bf16[1,10,10,352]{3,2,1,0:T(8,128)(2,1)S(1)}, u32[]{:S(2)}, u32[]{:S(2)}) collective-permute-start(bf16[1,10,10,352]{3,2,1,0:T(8,128)(2,1)S(1)} %get-tuple-element.1169), channel_id=1, source_target_pairs={{0,128},{128,256},{256,384},{384,512},{512,640},{640,768},{768,896... | collective-permute-start | bytes 211208 | tf_op jit(solution)/shard_map/while/body/eval_jaxpr/ppermute | solution.py:15
  87.0 7.5 %collective-permute-start = (bf16[1,10,10,352]{3,2,1,0:T(8,128)(2,1)S(1)}, bf16[1,10,10,352]{3,2,1,0:T(8,128)(2,1)S(1)}, u32[]{:S(2)}, u32[]{:S(2)}) collective-permute-start(bf16[1,10,10,352]{3,2,1,0:T(8,128)(2,1)S(1)} %get-tuple-element.1169), channel_id=1, source_target_pairs={{0,128},{128,256},{256,384},{384,512},{512,640},{640,768},{768,896... | collective-permute-start | bytes 211208 | tf_op jit(solution)/shard_map/while/body/eval_jaxpr/ppermute | solution.py:15
  95.2 10.8 %collective-permute-start = (bf16[1,10,10,352]{3,2,1,0:T(8,128)(2,1)S(1)}, bf16[1,10,10,352]{3,2,1,0:T(8,128)(2,1)S(1)}, u32[]{:S(2)}, u32[]{:S(2)}) collective-permute-start(bf16[1,10,10,352]{3,2,1,0:T(8,128)(2,1)S(1)} %get-tuple-element.1169), channel_id=1, source_target_pairs={{0,128},{128,256},{256,384},{384,512},{512,640},{640,768},{768,896... | collective-permute-start | bytes 211208 | tf_op jit(solution)/shard_map/while/body/eval_jaxpr/ppermute | solution.py:15
  106.7 6.8 %collective-permute-start = (bf16[1,10,10,352]{3,2,1,0:T(8,128)(2,1)S(1)}, bf16[1,10,10,352]{3,2,1,0:T(8,128)(2,1)S(1)}, u32[]{:S(2)}, u32[]{:S(2)}) collective-permute-start(bf16[1,10,10,352]{3,2,1,0:T(8,128)(2,1)S(1)} %get-tuple-element.1169), channel_id=1, source_target_pairs={{0,128},{128,256},{256,384},{384,512},{512,640},{640,768},{768,896... | collective-permute-start | bytes 211208 | tf_op jit(solution)/shard_map/while/body/eval_jaxpr/ppermute | solution.py:15
  114.2 12.0 %collective-permute-start = (bf16[1,10,10,352]{3,2,1,0:T(8,128)(2,1)S(1)}, bf16[1,10,10,352]{3,2,1,0:T(8,128)(2,1)S(1)}, u32[]{:S(2)}, u32[]{:S(2)}) collective-permute-start(bf16[1,10,10,352]{3,2,1,0:T(8,128)(2,1)S(1)} %get-tuple-element.1169), channel_id=1, source_target_pairs={{0,128},{128,256},{256,384},{384,512},{512,640},{640,768},{768,896... | collective-permute-start | bytes 211208 | tf_op jit(solution)/shard_map/while/body/eval_jaxpr/ppermute | solution.py:15
  126.9 9.2 %collective-permute-start = (bf16[1,10,10,352]{3,2,1,0:T(8,128)(2,1)S(1)}, bf16[1,10,10,352]{3,2,1,0:T(8,128)(2,1)S(1)}, u32[]{:S(2)}, u32[]{:S(2)}) collective-permute-start(bf16[1,10,10,352]{3,2,1,0:T(8,128)(2,1)S(1)} %get-tuple-element.1169), channel_id=1, source_target_pairs={{0,128},{128,256},{256,384},{384,512},{512,640},{640,768},{768,896... | collective-permute-start | bytes 211208 | tf_op jit(solution)/shard_map/while/body/eval_jaxpr/ppermute | solution.py:15
  136.8 13.5 %collective-permute-start = (bf16[1,10,10,352]{3,2,1,0:T(8,128)(2,1)S(1)}, bf16[1,10,10,352]{3,2,1,0:T(8,128)(2,1)S(1)}, u32[]{:S(2)}, u32[]{:S(2)}) collective-permute-start(bf16[1,10,10,352]{3,2,1,0:T(8,128)(2,1)S(1)} %get-tuple-element.1169), channel_id=1, source_target_pairs={{0,128},{128,256},{256,384},{384,512},{512,640},{640,768},{768,896... | collective-permute-start | bytes 211208 | tf_op jit(solution)/shard_map/while/body/eval_jaxpr/ppermute | solution.py:15
  150.9 8.0 %collective-permute-start = (bf16[1,10,10,352]{3,2,1,0:T(8,128)(2,1)S(1)}, bf16[1,10,10,352]{3,2,1,0:T(8,128)(2,1)S(1)}, u32[]{:S(2)}, u32[]{:S(2)}) collective-permute-start(bf16[1,10,10,352]{3,2,1,0:T(8,128)(2,1)S(1)} %get-tuple-element.1169), channel_id=1, source_target_pairs={{0,128},{128,256},{256,384},{384,512},{512,640},{640,768},{768,896... | collective-permute-start | bytes 211208 | tf_op jit(solution)/shard_map/while/body/eval_jaxpr/ppermute | solution.py:15
  163.5 10.9 %collective-permute-start.1 = (bf16[1,10,10,352]{3,2,1,0:T(8,128)(2,1)}, bf16[1,10,10,352]{3,2,1,0:T(8,128)(2,1)S(1)}, u32[]{:S(2)}, u32[]{:S(2)}) collective-permute-start(bf16[1,10,10,352]{3,2,1,0:T(8,128)(2,1)} %get-tuple-element.1055), channel_id=1, source_target_pairs={{128,0},{256,128},{384,256},{512,384},{640,512},{768,640},{896,768... | collective-permute-start | bytes 211208 | tf_op jit(solution)/shard_map/while/body/eval_jaxpr/ppermute | solution.py:15
  175.9 8.6 %collective-permute-start.1 = (bf16[1,10,10,352]{3,2,1,0:T(8,128)(2,1)}, bf16[1,10,10,352]{3,2,1,0:T(8,128)(2,1)S(1)}, u32[]{:S(2)}, u32[]{:S(2)}) collective-permute-start(bf16[1,10,10,352]{3,2,1,0:T(8,128)(2,1)} %get-tuple-element.1055), channel_id=1, source_target_pairs={{128,0},{256,128},{384,256},{512,384},{640,512},{768,640},{896,768... | collective-permute-start | bytes 211208 | tf_op jit(solution)/shard_map/while/body/eval_jaxpr/ppermute | solution.py:15
  185.9 10.9 %collective-permute-start.1 = (bf16[1,10,10,352]{3,2,1,0:T(8,128)(2,1)}, bf16[1,10,10,352]{3,2,1,0:T(8,128)(2,1)S(1)}, u32[]{:S(2)}, u32[]{:S(2)}) collective-permute-start(bf16[1,10,10,352]{3,2,1,0:T(8,128)(2,1)} %get-tuple-element.1055), channel_id=1, source_target_pairs={{128,0},{256,128},{384,256},{512,384},{640,512},{768,640},{896,768... | collective-permute-start | bytes 211208 | tf_op jit(solution)/shard_map/while/body/eval_jaxpr/ppermute | solution.py:15
  198.3 8.2 %collective-permute-start.1 = (bf16[1,10,10,352]{3,2,1,0:T(8,128)(2,1)}, bf16[1,10,10,352]{3,2,1,0:T(8,128)(2,1)S(1)}, u32[]{:S(2)}, u32[]{:S(2)}) collective-permute-start(bf16[1,10,10,352]{3,2,1,0:T(8,128)(2,1)} %get-tuple-element.1055), channel_id=1, source_target_pairs={{128,0},{256,128},{384,256},{512,384},{640,512},{768,640},{896,768... | collective-permute-start | bytes 211208 | tf_op jit(solution)/shard_map/while/body/eval_jaxpr/ppermute | solution.py:15
  207.9 11.4 %collective-permute-start.1 = (bf16[1,10,10,352]{3,2,1,0:T(8,128)(2,1)}, bf16[1,10,10,352]{3,2,1,0:T(8,128)(2,1)S(1)}, u32[]{:S(2)}, u32[]{:S(2)}) collective-permute-start(bf16[1,10,10,352]{3,2,1,0:T(8,128)(2,1)} %get-tuple-element.1055), channel_id=1, source_target_pairs={{128,0},{256,128},{384,256},{512,384},{640,512},{768,640},{896,768... | collective-permute-start | bytes 211208 | tf_op jit(solution)/shard_map/while/body/eval_jaxpr/ppermute | solution.py:15
  220.7 118.5 %collective-permute-start.1 = (bf16[1,10,10,352]{3,2,1,0:T(8,128)(2,1)}, bf16[1,10,10,352]{3,2,1,0:T(8,128)(2,1)S(1)}, u32[]{:S(2)}, u32[]{:S(2)}) collective-permute-start(bf16[1,10,10,352]{3,2,1,0:T(8,128)(2,1)} %get-tuple-element.1055), channel_id=1, source_target_pairs={{128,0},{256,128},{384,256},{512,384},{640,512},{768,640},{896,768... | collective-permute-start | bytes 211208 | tf_op jit(solution)/shard_map/while/body/eval_jaxpr/ppermute | solution.py:15
  358.9 8.2 %collective-permute-start.1 = (bf16[1,10,10,352]{3,2,1,0:T(8,128)(2,1)}, bf16[1,10,10,352]{3,2,1,0:T(8,128)(2,1)S(1)}, u32[]{:S(2)}, u32[]{:S(2)}) collective-permute-start(bf16[1,10,10,352]{3,2,1,0:T(8,128)(2,1)} %get-tuple-element.1055), channel_id=1, source_target_pairs={{128,0},{256,128},{384,256},{512,384},{640,512},{768,640},{896,768... | collective-permute-start | bytes 211208 | tf_op jit(solution)/shard_map/while/body/eval_jaxpr/ppermute | solution.py:15
  386.8 8.2 %collective-permute-start.1 = (bf16[1,10,10,352]{3,2,1,0:T(8,128)(2,1)}, bf16[1,10,10,352]{3,2,1,0:T(8,128)(2,1)S(1)}, u32[]{:S(2)}, u32[]{:S(2)}) collective-permute-start(bf16[1,10,10,352]{3,2,1,0:T(8,128)(2,1)} %get-tuple-element.1055), channel_id=1, source_target_pairs={{128,0},{256,128},{384,256},{512,384},{640,512},{768,640},{896,768... | collective-permute-start | bytes 211208 | tf_op jit(solution)/shard_map/while/body/eval_jaxpr/ppermute | solution.py:15
  414.7 9.5 %collective-permute-start.1 = (bf16[1,10,10,352]{3,2,1,0:T(8,128)(2,1)}, bf16[1,10,10,352]{3,2,1,0:T(8,128)(2,1)S(1)}, u32[]{:S(2)}, u32[]{:S(2)}) collective-permute-start(bf16[1,10,10,352]{3,2,1,0:T(8,128)(2,1)} %get-tuple-element.1055), channel_id=1, source_target_pairs={{128,0},{256,128},{384,256},{512,384},{640,512},{768,640},{896,768... | collective-permute-start | bytes 211208 | tf_op jit(solution)/shard_map/while/body/eval_jaxpr/ppermute | solution.py:15
  443.9 7.0 %collective-permute-start.1 = (bf16[1,10,10,352]{3,2,1,0:T(8,128)(2,1)}, bf16[1,10,10,352]{3,2,1,0:T(8,128)(2,1)S(1)}, u32[]{:S(2)}, u32[]{:S(2)}) collective-permute-start(bf16[1,10,10,352]{3,2,1,0:T(8,128)(2,1)} %get-tuple-element.1055), channel_id=1, source_target_pairs={{128,0},{256,128},{384,256},{512,384},{640,512},{768,640},{896,768... | collective-permute-start | bytes 211208 | tf_op jit(solution)/shard_map/while/body/eval_jaxpr/ppermute | solution.py:15
  452.3 23.2 %collective-permute-start.1 = (bf16[1,10,10,352]{3,2,1,0:T(8,128)(2,1)}, bf16[1,10,10,352]{3,2,1,0:T(8,128)(2,1)S(1)}, u32[]{:S(2)}, u32[]{:S(2)}) collective-permute-start(bf16[1,10,10,352]{3,2,1,0:T(8,128)(2,1)} %get-tuple-element.1055), channel_id=1, source_target_pairs={{128,0},{256,128},{384,256},{512,384},{640,512},{768,640},{896,768... | collective-permute-start | bytes 211208 | tf_op jit(solution)/shard_map/while/body/eval_jaxpr/ppermute | solution.py:15
  491.5 15.9 %collective-permute-start.3 = (f32[32,32,128]{2,1,0:T(8,128)S(1)}, f32[32,32,128]{2,1,0:T(8,128)S(1)}, u32[]{:S(2)}, u32[]{:S(2)}) collective-permute-start(f32[32,32,128]{2,1,0:T(8,128)S(1)} %dynamic-slice_bitcast_fusion.1), channel_id=1, source_target_pairs={{0,2},{2,0},{4,6},{6,4},{8,10},{10,8},{12,14},{14,12},{1,3},{3,1},... | collective-permute-start | bytes 1572872 | tf_op jit(solution)/shard_map/ppermute | solution.py:109
  507.5 16.0 %collective-permute-start.4 = (f32[16,32,128]{2,1,0:T(8,128)S(1)}, f32[16,32,128]{2,1,0:T(8,128)S(1)}, u32[]{:S(2)}, u32[]{:S(2)}) collective-permute-start(f32[16,32,128]{2,1,0:T(8,128)S(1)} %dynamic-slice_bitcast_fusion.2), channel_id=1, source_target_pairs={{0,4},{2,6},{4,0},{6,2},{8,12},{10,14},{12,8},{14,10},{1,5},{3,7},... | collective-permute-start | bytes 786440 | tf_op jit(solution)/shard_map/ppermute | solution.py:109
  523.5 11.2 %collective-permute-start.5 = (f32[8,32,128]{2,1,0:T(8,128)S(1)}, f32[8,32,128]{2,1,0:T(8,128)S(1)}, u32[]{:S(2)}, u32[]{:S(2)}) collective-permute-start(f32[8,32,128]{2,1,0:T(8,128)S(1)} %dynamic-slice_bitcast_fusion.3), channel_id=1, source_target_pairs={{0,8},{2,10},{4,12},{6,14},{8,0},{10,2},{12,4},{14,6},{1,9},{3,11}... | collective-permute-start | bytes 393224 | tf_op jit(solution)/shard_map/ppermute | solution.py:109
  547.7 9.5 %collective-permute-start.8 = (f32[1,32,128]{2,1,0:T(8,128)S(1)}, f32[1,32,128]{2,1,0:T(8,128)S(1)}, u32[]{:S(2)}, u32[]{:S(2)}) collective-permute-start(f32[1,32,128]{2,1,0:T(8,128)S(1)} %constant_dynamic-slice_fusion), channel_id=1, source_target_pairs={{0,64},{16,80},{32,96},{48,112},{64,0},{80,16},{96,32},{112,48},{1... | collective-permute-start | bytes 49160 | tf_op jit(solution)/shard_map/ppermute | solution.py:109
  (319 other events, 1365.4 us)

commit v4 on v3

--- a/solution.py
+++ b/solution.py
@@ -113,7 +113,7 @@
     section = lax.axis_index("section")
     sections = lax.axis_size("section")
     micro_count, img_count, side, _, width = images.shape
-    kernel = dw_kernel[0]
+    kernel = lax.optimization_barrier(tuple(dw_kernel[0, tap] for tap in range(KS * KS)))
     scale = layer_scale[0]
     weight_in = w_in[0]
     weight_out = w_out[0]
@@ -126,17 +126,13 @@
     def run_forward(entering):
         return block_forward(entering, kernel, scale, weight_in, weight_out)
 
-    def skip_forward(entering):
-        return jnp.zeros_like(entering)
-
     def forward_tick(tick, carry):
         incoming, kept = carry
         micro = tick - section
-        active = (micro >= 0) & (micro < micro_count)
         slot = jnp.clip(micro, 0, micro_count - 1)
         own = lax.dynamic_index_in_dim(images, slot, 0, keepdims=False)
         entering = jnp.where(section == 0, own, incoming)
-        leaving = lax.cond(active, run_forward, skip_forward, entering)
+        leaving = run_forward(entering)
         kept = place(kept, entering, micro, micro_count)
         incoming = shifted(leaving, "section", 1)
         return (incoming, kept)
@@ -147,13 +143,6 @@
     def run_backward(entering, upstream):
         return block_backward(entering, upstream, kernel, scale, weight_in, weight_out)
 
-    def skip_backward(entering, upstream):
-        return (
-            jnp.zeros_like(upstream),
-            jnp.zeros((pixel_rows, width), jnp.bfloat16),
-            jnp.zeros((pixel_rows, hidden_width), jnp.bfloat16),
-        )
-
     stores = (
         jnp.zeros((micro_count + 2, pixel_rows, width), jnp.bfloat16),
         jnp.zeros((micro_count + 2, pixel_rows, hidden_width), jnp.bfloat16),
@@ -163,14 +152,11 @@
     def backward_tick(tick, carry):
         incoming, grads, stored, total = carry
         micro = tick - (sections - 1 - section)
-        active = (micro >= 0) & (micro < micro_count)
         slot = jnp.clip(micro, 0, micro_count - 1)
         own = lax.dynamic_index_in_dim(cotangent, slot, 0, keepdims=False)
         upstream = jnp.where(section == sections - 1, own, incoming)
         entering = lax.dynamic_index_in_dim(kept, slot + 1, 0, keepdims=False)
-        input_grad, flat, pre_grad = lax.cond(
-            active, run_backward, skip_backward, entering, upstream
-        )
+        input_grad, flat, pre_grad = run_backward(entering, upstream)
         grads = place(grads, input_grad, micro, micro_count)
         stored = (
             place(stored[0], flat, micro, micro_count),

time: 562 us -> 463 us (0.82)
  the two profiles are of different devices: /device:TPU:2 before, /device:TPU:6 now
where the time goes in v4:
time: 463 us; the launch traced here: 460 us
  other arithmetic  144 us (31%)
  waiting for transfers between devices  133 us (29%)
  starting transfers between devices  110 us (24%)
  local copies, waits for them, and re-layouts  35 us (8%)
  matrix products  33.7 us (7%)
    ppermute x22, waiting for transfers between devices, shifted(): return lax.ppermute(block, axis, route)  90.4 us
    ppermute x22, starting transfers between devices, shifted(): return lax.ppermute(block, axis, route)  73.9 us
    reduce_sum x22, other arithmetic, block_inner(): center = mixed - jnp.mean(mixed, axis=-1, keepdims=True)  55 us
    ppermute x7, waiting for transfers between devices, halve(): return keep + lax.ppermute(send, axis, route)  42.1 us
    dynamic_update_slice x22, other arithmetic, place(): return lax.dynamic_update_index_in_dim(buffer, value, slot, 0)  39.8 us
    ppermute x7, starting transfers between devices, halve(): return keep + lax.ppermute(send, axis, route)  36.6 us
    another operation x22, other arithmetic  15.4 us
    dot_general x11, matrix products, block_backward(): lax.dot_general(branch_grad, weight_out, (((1,), (1,)), ((), ())), prefer...  13.4 us
  transfers between devices with their start and end apart: 29, of which 29 were waited for; matrix products, arithmetic and copies ran while one was open for 4% of the time, Pallas kernels for 0%

profile of v4, /device:TPU:6, one launch (start us, length us, event | category | flops | bytes accessed | tf_op | source)
XLA Modules:
  0.0 459.8 jit_solution(4852111967822544587)
XLA Ops:
  11.4 138.6 %while.39 = (s32[]{:T(128)}, bf16[1,10,10,352]{3,2,1,0:T(8,128)(2,1)S(1)}, bf16[6,1,10,10,352]{4,3,2,1,0:T(8,128)(2,1)}, pred[]{:T(512)}, s32[]{:T(128)}, /*inde...) while((s32[]{:T(128)}, ...), condition=%wide.region_3.4_spmd, body=%wide.region_0.3_spmd.sunk | while | flops 202822496 | bytes 4506576 | solution.py:141
  27.3 5.6 %collective-permute-start = (bf16[1,10,10,352]{3,2,1,0:T(8,128)(2,1)S(1)}, bf16[1,10,10,352]{3,2,1,0:T(8,128)(2,1)S(1)}, u32[]{:S(2)}, u32[]{:S(2)}) collective-permute-start(bf16[1,10,10,352]{3,2,1,0:T(8,128)(2,1)S(1)} %reshape.630), channel_id=1, source_target_pairs={{0,128},{128,256},{256,384},{384,512},{512,640},{640,768},{768,896... | collective-permute-start | bytes 211208 | tf_op jit(solution)/shard_map/while/body/eval_jaxpr/ppermute | solution.py:15
  39.7 5.6 %collective-permute-start = (bf16[1,10,10,352]{3,2,1,0:T(8,128)(2,1)S(1)}, bf16[1,10,10,352]{3,2,1,0:T(8,128)(2,1)S(1)}, u32[]{:S(2)}, u32[]{:S(2)}) collective-permute-start(bf16[1,10,10,352]{3,2,1,0:T(8,128)(2,1)S(1)} %reshape.630), channel_id=1, source_target_pairs={{0,128},{128,256},{256,384},{384,512},{512,640},{640,768},{768,896... | collective-permute-start | bytes 211208 | tf_op jit(solution)/shard_map/while/body/eval_jaxpr/ppermute | solution.py:15
  46.0 6.9 %collective-permute-done = bf16[1,10,10,352]{3,2,1,0:T(8,128)(2,1)S(1)} collective-permute-done((bf16[1,10,10,352]{3,2,1,0:T(8,128)(2,1)S(1)}, bf16[1,10,10,352]{3,2,1,0:T(8,128)(2,1)S(1)}, u32[]{:S(2)}, u32[]{:S(2)}) %collective-permute-start) | collective-permute-done | bytes 70432 | tf_op jit(solution)/shard_map/while/body/eval_jaxpr/ppermute | solution.py:15
  90.9 5.5 %collective-permute-start = (bf16[1,10,10,352]{3,2,1,0:T(8,128)(2,1)S(1)}, bf16[1,10,10,352]{3,2,1,0:T(8,128)(2,1)S(1)}, u32[]{:S(2)}, u32[]{:S(2)}) collective-permute-start(bf16[1,10,10,352]{3,2,1,0:T(8,128)(2,1)S(1)} %reshape.630), channel_id=1, source_target_pairs={{0,128},{128,256},{256,384},{384,512},{512,640},{640,768},{768,896... | collective-permute-start | bytes 211208 | tf_op jit(solution)/shard_map/while/body/eval_jaxpr/ppermute | solution.py:15
  103.2 5.6 %collective-permute-start = (bf16[1,10,10,352]{3,2,1,0:T(8,128)(2,1)S(1)}, bf16[1,10,10,352]{3,2,1,0:T(8,128)(2,1)S(1)}, u32[]{:S(2)}, u32[]{:S(2)}) collective-permute-start(bf16[1,10,10,352]{3,2,1,0:T(8,128)(2,1)S(1)} %reshape.630), channel_id=1, source_target_pairs={{0,128},{128,256},{256,384},{384,512},{512,640},{640,768},{768,896... | collective-permute-start | bytes 211208 | tf_op jit(solution)/shard_map/while/body/eval_jaxpr/ppermute | solution.py:15
  116.1 5.6 %collective-permute-start = (bf16[1,10,10,352]{3,2,1,0:T(8,128)(2,1)S(1)}, bf16[1,10,10,352]{3,2,1,0:T(8,128)(2,1)S(1)}, u32[]{:S(2)}, u32[]{:S(2)}) collective-permute-start(bf16[1,10,10,352]{3,2,1,0:T(8,128)(2,1)S(1)} %reshape.630), channel_id=1, source_target_pairs={{0,128},{128,256},{256,384},{384,512},{512,640},{640,768},{768,896... | collective-permute-start | bytes 211208 | tf_op jit(solution)/shard_map/while/body/eval_jaxpr/ppermute | solution.py:15
  129.4 5.6 %collective-permute-start = (bf16[1,10,10,352]{3,2,1,0:T(8,128)(2,1)S(1)}, bf16[1,10,10,352]{3,2,1,0:T(8,128)(2,1)S(1)}, u32[]{:S(2)}, u32[]{:S(2)}) collective-permute-start(bf16[1,10,10,352]{3,2,1,0:T(8,128)(2,1)S(1)} %reshape.630), channel_id=1, source_target_pairs={{0,128},{128,256},{256,384},{384,512},{512,640},{640,768},{768,896... | collective-permute-start | bytes 211208 | tf_op jit(solution)/shard_map/while/body/eval_jaxpr/ppermute | solution.py:15
  141.9 5.6 %collective-permute-start = (bf16[1,10,10,352]{3,2,1,0:T(8,128)(2,1)S(1)}, bf16[1,10,10,352]{3,2,1,0:T(8,128)(2,1)S(1)}, u32[]{:S(2)}, u32[]{:S(2)}) collective-permute-start(bf16[1,10,10,352]{3,2,1,0:T(8,128)(2,1)S(1)} %reshape.630), channel_id=1, source_target_pairs={{0,128},{128,256},{256,384},{384,512},{512,640},{640,768},{768,896... | collective-permute-start | bytes 211208 | tf_op jit(solution)/shard_map/while/body/eval_jaxpr/ppermute | solution.py:15
  153.1 211.5 %while.40 = (s32[]{:T(128)}, bf16[1,10,10,352]{3,2,1,0:T(8,128)(2,1)S(1)}, bf16[6,1,10,10,352]{4,3,2,1,0:T(8,128)(2,1)}, bf16[6,100,352]{2,1,0:T(8,128)(2,1)}, b...) while((s32[]{:T(128)}, ...), condition=%wide.region_9.10_spmd, body=%wide.region_4.9_spmd.sunk | while | flops 306486496 | bytes 9053822 | solution.py:168
  166.8 5.8 %collective-permute-done.1 = bf16[1,10,10,352]{3,2,1,0:T(8,128)(2,1)S(1)} collective-permute-done((bf16[1,10,10,352]{3,2,1,0:T(8,128)(2,1)S(1)}, bf16[1,10,10,352]{3,2,1,0:T(8,128)(2,1)S(1)}, u32[]{:S(2)}, u32[]{:S(2)}) %collective-permute-start.1) | collective-permute-done | bytes 70432 | tf_op jit(solution)/shard_map/while/body/eval_jaxpr/ppermute | solution.py:15
  186.3 5.4 %collective-permute-done.1 = bf16[1,10,10,352]{3,2,1,0:T(8,128)(2,1)S(1)} collective-permute-done((bf16[1,10,10,352]{3,2,1,0:T(8,128)(2,1)S(1)}, bf16[1,10,10,352]{3,2,1,0:T(8,128)(2,1)S(1)}, u32[]{:S(2)}, u32[]{:S(2)}) %collective-permute-start.1) | collective-permute-done | bytes 70432 | tf_op jit(solution)/shard_map/while/body/eval_jaxpr/ppermute | solution.py:15
  205.3 5.4 %collective-permute-done.1 = bf16[1,10,10,352]{3,2,1,0:T(8,128)(2,1)S(1)} collective-permute-done((bf16[1,10,10,352]{3,2,1,0:T(8,128)(2,1)S(1)}, bf16[1,10,10,352]{3,2,1,0:T(8,128)(2,1)S(1)}, u32[]{:S(2)}, u32[]{:S(2)}) %collective-permute-start.1) | collective-permute-done | bytes 70432 | tf_op jit(solution)/shard_map/while/body/eval_jaxpr/ppermute | solution.py:15
  224.4 6.4 %collective-permute-done.1 = bf16[1,10,10,352]{3,2,1,0:T(8,128)(2,1)S(1)} collective-permute-done((bf16[1,10,10,352]{3,2,1,0:T(8,128)(2,1)S(1)}, bf16[1,10,10,352]{3,2,1,0:T(8,128)(2,1)S(1)}, u32[]{:S(2)}, u32[]{:S(2)}) %collective-permute-start.1) | collective-permute-done | bytes 70432 | tf_op jit(solution)/shard_map/while/body/eval_jaxpr/ppermute | solution.py:15
  244.5 5.8 %collective-permute-done.1 = bf16[1,10,10,352]{3,2,1,0:T(8,128)(2,1)S(1)} collective-permute-done((bf16[1,10,10,352]{3,2,1,0:T(8,128)(2,1)S(1)}, bf16[1,10,10,352]{3,2,1,0:T(8,128)(2,1)S(1)}, u32[]{:S(2)}, u32[]{:S(2)}) %collective-permute-start.1) | collective-permute-done | bytes 70432 | tf_op jit(solution)/shard_map/while/body/eval_jaxpr/ppermute | solution.py:15
  264.0 5.4 %collective-permute-done.1 = bf16[1,10,10,352]{3,2,1,0:T(8,128)(2,1)S(1)} collective-permute-done((bf16[1,10,10,352]{3,2,1,0:T(8,128)(2,1)S(1)}, bf16[1,10,10,352]{3,2,1,0:T(8,128)(2,1)S(1)}, u32[]{:S(2)}, u32[]{:S(2)}) %collective-permute-start.1) | collective-permute-done | bytes 70432 | tf_op jit(solution)/shard_map/while/body/eval_jaxpr/ppermute | solution.py:15
  283.1 5.4 %collective-permute-done.1 = bf16[1,10,10,352]{3,2,1,0:T(8,128)(2,1)S(1)} collective-permute-done((bf16[1,10,10,352]{3,2,1,0:T(8,128)(2,1)S(1)}, bf16[1,10,10,352]{3,2,1,0:T(8,128)(2,1)S(1)}, u32[]{:S(2)}, u32[]{:S(2)}) %collective-permute-start.1) | collective-permute-done | bytes 70432 | tf_op jit(solution)/shard_map/while/body/eval_jaxpr/ppermute | solution.py:15
  302.1 5.4 %collective-permute-done.1 = bf16[1,10,10,352]{3,2,1,0:T(8,128)(2,1)S(1)} collective-permute-done((bf16[1,10,10,352]{3,2,1,0:T(8,128)(2,1)S(1)}, bf16[1,10,10,352]{3,2,1,0:T(8,128)(2,1)S(1)}, u32[]{:S(2)}, u32[]{:S(2)}) %collective-permute-start.1) | collective-permute-done | bytes 70432 | tf_op jit(solution)/shard_map/while/body/eval_jaxpr/ppermute | solution.py:15
  384.6 13.9 %collective-permute-done.3 = f32[32,32,128]{2,1,0:T(8,128)S(1)} collective-permute-done((f32[32,32,128]{2,1,0:T(8,128)S(1)}, f32[32,32,128]{2,1,0:T(8,128)S(1)}, u32[]{:S(2)}, u32[]{:S(2)}) %collective-permute-start.3) | collective-permute-done | bytes 524320 | tf_op jit(solution)/shard_map/ppermute | solution.py:109
  402.6 12.9 %collective-permute-done.4 = f32[16,32,128]{2,1,0:T(8,128)S(1)} collective-permute-done((f32[16,32,128]{2,1,0:T(8,128)S(1)}, f32[16,32,128]{2,1,0:T(8,128)S(1)}, u32[]{:S(2)}, u32[]{:S(2)}) %collective-permute-start.4) | collective-permute-done | bytes 262176 | tf_op jit(solution)/shard_map/ppermute | solution.py:109
  415.6 6.4 %collective-permute-start.5 = (f32[8,32,128]{2,1,0:T(8,128)S(1)}, f32[8,32,128]{2,1,0:T(8,128)S(1)}, u32[]{:S(2)}, u32[]{:S(2)}) collective-permute-start(f32[8,32,128]{2,1,0:T(8,128)S(1)} %dynamic-slice_bitcast_fusion.3), channel_id=1, source_target_pairs={{0,8},{2,10},{4,12},{6,14},{8,0},{10,2},{12,4},{14,6},{1,9},{3,11}... | collective-permute-start | bytes 393224 | tf_op jit(solution)/shard_map/ppermute | solution.py:109
  422.0 7.6 %collective-permute-done.5 = f32[8,32,128]{2,1,0:T(8,128)S(1)} collective-permute-done((f32[8,32,128]{2,1,0:T(8,128)S(1)}, f32[8,32,128]{2,1,0:T(8,128)S(1)}, u32[]{:S(2)}, u32[]{:S(2)}) %collective-permute-start.5) | collective-permute-done | bytes 131104 | tf_op jit(solution)/shard_map/ppermute | solution.py:109
  435.8 7.8 %collective-permute-start.7 = (f32[2,32,128]{2,1,0:T(8,128)S(1)}, f32[2,32,128]{2,1,0:T(8,128)S(1)}, u32[]{:S(2)}, u32[]{:S(2)}) collective-permute-start(f32[2,32,128]{2,1,0:T(8,128)S(1)} %dynamic-slice_bitcast_fusion.5), channel_id=1, source_target_pairs={{0,32},{16,48},{32,0},{48,16},{64,96},{80,112},{96,64},{112,80},{1... | collective-permute-start | bytes 98312 | tf_op jit(solution)/shard_map/ppermute | solution.py:109
  445.5 11.8 %collective-permute-start.8 = (f32[1,32,128]{2,1,0:T(8,128)S(1)}, f32[1,32,128]{2,1,0:T(8,128)S(1)}, u32[]{:S(2)}, u32[]{:S(2)}) collective-permute-start(f32[1,32,128]{2,1,0:T(8,128)S(1)} %constant_dynamic-slice_fusion), channel_id=1, source_target_pairs={{0,64},{16,80},{32,96},{48,112},{64,0},{80,16},{96,32},{112,48},{1... | collective-permute-start | bytes 49160 | tf_op jit(solution)/shard_map/ppermute | solution.py:109
  (462 shorter events, 305.0 us)
Async XLA Ops:
  15.7 7.2 %collective-permute-start = (bf16[1,10,10,352]{3,2,1,0:T(8,128)(2,1)S(1)}, bf16[1,10,10,352]{3,2,1,0:T(8,128)(2,1)S(1)}, u32[]{:S(2)}, u32[]{:S(2)}) collective-permute-start(bf16[1,10,10,352]{3,2,1,0:T(8,128)(2,1)S(1)} %reshape.630), channel_id=1, source_target_pairs={{0,128},{128,256},{256,384},{384,512},{512,640},{640,768},{768,896... | collective-permute-start | bytes 211208 | tf_op jit(solution)/shard_map/while/body/eval_jaxpr/ppermute | solution.py:15
  27.3 8.0 %collective-permute-start = (bf16[1,10,10,352]{3,2,1,0:T(8,128)(2,1)S(1)}, bf16[1,10,10,352]{3,2,1,0:T(8,128)(2,1)S(1)}, u32[]{:S(2)}, u32[]{:S(2)}) collective-permute-start(bf16[1,10,10,352]{3,2,1,0:T(8,128)(2,1)S(1)} %reshape.630), channel_id=1, source_target_pairs={{0,128},{128,256},{256,384},{384,512},{512,640},{640,768},{768,896... | collective-permute-start | bytes 211208 | tf_op jit(solution)/shard_map/while/body/eval_jaxpr/ppermute | solution.py:15
  39.7 13.2 %collective-permute-start = (bf16[1,10,10,352]{3,2,1,0:T(8,128)(2,1)S(1)}, bf16[1,10,10,352]{3,2,1,0:T(8,128)(2,1)S(1)}, u32[]{:S(2)}, u32[]{:S(2)}) collective-permute-start(bf16[1,10,10,352]{3,2,1,0:T(8,128)(2,1)S(1)} %reshape.630), channel_id=1, source_target_pairs={{0,128},{128,256},{256,384},{384,512},{512,640},{640,768},{768,896... | collective-permute-start | bytes 211208 | tf_op jit(solution)/shard_map/while/body/eval_jaxpr/ppermute | solution.py:15
  90.9 7.9 %collective-permute-start = (bf16[1,10,10,352]{3,2,1,0:T(8,128)(2,1)S(1)}, bf16[1,10,10,352]{3,2,1,0:T(8,128)(2,1)S(1)}, u32[]{:S(2)}, u32[]{:S(2)}) collective-permute-start(bf16[1,10,10,352]{3,2,1,0:T(8,128)(2,1)S(1)} %reshape.630), channel_id=1, source_target_pairs={{0,128},{128,256},{256,384},{384,512},{512,640},{640,768},{768,896... | collective-permute-start | bytes 211208 | tf_op jit(solution)/shard_map/while/body/eval_jaxpr/ppermute | solution.py:15
  103.2 8.5 %collective-permute-start = (bf16[1,10,10,352]{3,2,1,0:T(8,128)(2,1)S(1)}, bf16[1,10,10,352]{3,2,1,0:T(8,128)(2,1)S(1)}, u32[]{:S(2)}, u32[]{:S(2)}) collective-permute-start(bf16[1,10,10,352]{3,2,1,0:T(8,128)(2,1)S(1)} %reshape.630), channel_id=1, source_target_pairs={{0,128},{128,256},{256,384},{384,512},{512,640},{640,768},{768,896... | collective-permute-start | bytes 211208 | tf_op jit(solution)/shard_map/while/body/eval_jaxpr/ppermute | solution.py:15
  116.1 8.9 %collective-permute-start = (bf16[1,10,10,352]{3,2,1,0:T(8,128)(2,1)S(1)}, bf16[1,10,10,352]{3,2,1,0:T(8,128)(2,1)S(1)}, u32[]{:S(2)}, u32[]{:S(2)}) collective-permute-start(bf16[1,10,10,352]{3,2,1,0:T(8,128)(2,1)S(1)} %reshape.630), channel_id=1, source_target_pairs={{0,128},{128,256},{256,384},{384,512},{512,640},{640,768},{768,896... | collective-permute-start | bytes 211208 | tf_op jit(solution)/shard_map/while/body/eval_jaxpr/ppermute | solution.py:15
  129.4 8.1 %collective-permute-start = (bf16[1,10,10,352]{3,2,1,0:T(8,128)(2,1)S(1)}, bf16[1,10,10,352]{3,2,1,0:T(8,128)(2,1)S(1)}, u32[]{:S(2)}, u32[]{:S(2)}) collective-permute-start(bf16[1,10,10,352]{3,2,1,0:T(8,128)(2,1)S(1)} %reshape.630), channel_id=1, source_target_pairs={{0,128},{128,256},{256,384},{384,512},{512,640},{640,768},{768,896... | collective-permute-start | bytes 211208 | tf_op jit(solution)/shard_map/while/body/eval_jaxpr/ppermute | solution.py:15
  141.9 8.0 %collective-permute-start = (bf16[1,10,10,352]{3,2,1,0:T(8,128)(2,1)S(1)}, bf16[1,10,10,352]{3,2,1,0:T(8,128)(2,1)S(1)}, u32[]{:S(2)}, u32[]{:S(2)}) collective-permute-start(bf16[1,10,10,352]{3,2,1,0:T(8,128)(2,1)S(1)} %reshape.630), channel_id=1, source_target_pairs={{0,128},{128,256},{256,384},{384,512},{512,640},{640,768},{768,896... | collective-permute-start | bytes 211208 | tf_op jit(solution)/shard_map/while/body/eval_jaxpr/ppermute | solution.py:15
  164.2 8.4 %collective-permute-start.1 = (bf16[1,10,10,352]{3,2,1,0:T(8,128)(2,1)S(1)}, bf16[1,10,10,352]{3,2,1,0:T(8,128)(2,1)S(1)}, u32[]{:S(2)}, u32[]{:S(2)}) collective-permute-start(bf16[1,10,10,352]{3,2,1,0:T(8,128)(2,1)S(1)} %get-tuple-element.4139), channel_id=1, source_target_pairs={{128,0},{256,128},{384,256},{512,384},{640,512},{768,640},{896,768... | collective-permute-start | bytes 211208 | tf_op jit(solution)/shard_map/while/body/eval_jaxpr/ppermute | solution.py:15
  183.7 8.0 %collective-permute-start.1 = (bf16[1,10,10,352]{3,2,1,0:T(8,128)(2,1)S(1)}, bf16[1,10,10,352]{3,2,1,0:T(8,128)(2,1)S(1)}, u32[]{:S(2)}, u32[]{:S(2)}) collective-permute-start(bf16[1,10,10,352]{3,2,1,0:T(8,128)(2,1)S(1)} %get-tuple-element.4139), channel_id=1, source_target_pairs={{128,0},{256,128},{384,256},{512,384},{640,512},{768,640},{896,768... | collective-permute-start | bytes 211208 | tf_op jit(solution)/shard_map/while/body/eval_jaxpr/ppermute | solution.py:15
  202.7 8.0 %collective-permute-start.1 = (bf16[1,10,10,352]{3,2,1,0:T(8,128)(2,1)S(1)}, bf16[1,10,10,352]{3,2,1,0:T(8,128)(2,1)S(1)}, u32[]{:S(2)}, u32[]{:S(2)}) collective-permute-start(bf16[1,10,10,352]{3,2,1,0:T(8,128)(2,1)S(1)} %get-tuple-element.4139), channel_id=1, source_target_pairs={{128,0},{256,128},{384,256},{512,384},{640,512},{768,640},{896,768... | collective-permute-start | bytes 211208 | tf_op jit(solution)/shard_map/while/body/eval_jaxpr/ppermute | solution.py:15
  221.8 9.0 %collective-permute-start.1 = (bf16[1,10,10,352]{3,2,1,0:T(8,128)(2,1)S(1)}, bf16[1,10,10,352]{3,2,1,0:T(8,128)(2,1)S(1)}, u32[]{:S(2)}, u32[]{:S(2)}) collective-permute-start(bf16[1,10,10,352]{3,2,1,0:T(8,128)(2,1)S(1)} %get-tuple-element.4139), channel_id=1, source_target_pairs={{128,0},{256,128},{384,256},{512,384},{640,512},{768,640},{896,768... | collective-permute-start | bytes 211208 | tf_op jit(solution)/shard_map/while/body/eval_jaxpr/ppermute | solution.py:15
  241.9 8.5 %collective-permute-start.1 = (bf16[1,10,10,352]{3,2,1,0:T(8,128)(2,1)S(1)}, bf16[1,10,10,352]{3,2,1,0:T(8,128)(2,1)S(1)}, u32[]{:S(2)}, u32[]{:S(2)}) collective-permute-start(bf16[1,10,10,352]{3,2,1,0:T(8,128)(2,1)S(1)} %get-tuple-element.4139), channel_id=1, source_target_pairs={{128,0},{256,128},{384,256},{512,384},{640,512},{768,640},{896,768... | collective-permute-start | bytes 211208 | tf_op jit(solution)/shard_map/while/body/eval_jaxpr/ppermute | solution.py:15
  261.4 8.0 %collective-permute-start.1 = (bf16[1,10,10,352]{3,2,1,0:T(8,128)(2,1)S(1)}, bf16[1,10,10,352]{3,2,1,0:T(8,128)(2,1)S(1)}, u32[]{:S(2)}, u32[]{:S(2)}) collective-permute-start(bf16[1,10,10,352]{3,2,1,0:T(8,128)(2,1)S(1)} %get-tuple-element.4139), channel_id=1, source_target_pairs={{128,0},{256,128},{384,256},{512,384},{640,512},{768,640},{896,768... | collective-permute-start | bytes 211208 | tf_op jit(solution)/shard_map/while/body/eval_jaxpr/ppermute | solution.py:15
  280.5 8.0 %collective-permute-start.1 = (bf16[1,10,10,352]{3,2,1,0:T(8,128)(2,1)S(1)}, bf16[1,10,10,352]{3,2,1,0:T(8,128)(2,1)S(1)}, u32[]{:S(2)}, u32[]{:S(2)}) collective-permute-start(bf16[1,10,10,352]{3,2,1,0:T(8,128)(2,1)S(1)} %get-tuple-element.4139), channel_id=1, source_target_pairs={{128,0},{256,128},{384,256},{512,384},{640,512},{768,640},{896,768... | collective-permute-start | bytes 211208 | tf_op jit(solution)/shard_map/while/body/eval_jaxpr/ppermute | solution.py:15
  299.5 8.0 %collective-permute-start.1 = (bf16[1,10,10,352]{3,2,1,0:T(8,128)(2,1)S(1)}, bf16[1,10,10,352]{3,2,1,0:T(8,128)(2,1)S(1)}, u32[]{:S(2)}, u32[]{:S(2)}) collective-permute-start(bf16[1,10,10,352]{3,2,1,0:T(8,128)(2,1)S(1)} %get-tuple-element.4139), channel_id=1, source_target_pairs={{128,0},{256,128},{384,256},{512,384},{640,512},{768,640},{896,768... | collective-permute-start | bytes 211208 | tf_op jit(solution)/shard_map/while/body/eval_jaxpr/ppermute | solution.py:15
  318.5 8.0 %collective-permute-start.1 = (bf16[1,10,10,352]{3,2,1,0:T(8,128)(2,1)S(1)}, bf16[1,10,10,352]{3,2,1,0:T(8,128)(2,1)S(1)}, u32[]{:S(2)}, u32[]{:S(2)}) collective-permute-start(bf16[1,10,10,352]{3,2,1,0:T(8,128)(2,1)S(1)} %get-tuple-element.4139), channel_id=1, source_target_pairs={{128,0},{256,128},{384,256},{512,384},{640,512},{768,640},{896,768... | collective-permute-start | bytes 211208 | tf_op jit(solution)/shard_map/while/body/eval_jaxpr/ppermute | solution.py:15
  337.5 8.0 %collective-permute-start.1 = (bf16[1,10,10,352]{3,2,1,0:T(8,128)(2,1)S(1)}, bf16[1,10,10,352]{3,2,1,0:T(8,128)(2,1)S(1)}, u32[]{:S(2)}, u32[]{:S(2)}) collective-permute-start(bf16[1,10,10,352]{3,2,1,0:T(8,128)(2,1)S(1)} %get-tuple-element.4139), channel_id=1, source_target_pairs={{128,0},{256,128},{384,256},{512,384},{640,512},{768,640},{896,768... | collective-permute-start | bytes 211208 | tf_op jit(solution)/shard_map/while/body/eval_jaxpr/ppermute | solution.py:15
  356.6 8.0 %collective-permute-start.1 = (bf16[1,10,10,352]{3,2,1,0:T(8,128)(2,1)S(1)}, bf16[1,10,10,352]{3,2,1,0:T(8,128)(2,1)S(1)}, u32[]{:S(2)}, u32[]{:S(2)}) collective-permute-start(bf16[1,10,10,352]{3,2,1,0:T(8,128)(2,1)S(1)} %get-tuple-element.4139), channel_id=1, source_target_pairs={{128,0},{256,128},{384,256},{512,384},{640,512},{768,640},{896,768... | collective-permute-start | bytes 211208 | tf_op jit(solution)/shard_map/while/body/eval_jaxpr/ppermute | solution.py:15
  382.6 15.9 %collective-permute-start.3 = (f32[32,32,128]{2,1,0:T(8,128)S(1)}, f32[32,32,128]{2,1,0:T(8,128)S(1)}, u32[]{:S(2)}, u32[]{:S(2)}) collective-permute-start(f32[32,32,128]{2,1,0:T(8,128)S(1)} %dynamic-slice_bitcast_fusion.1), channel_id=1, source_target_pairs={{0,2},{2,0},{4,6},{6,4},{8,10},{10,8},{12,14},{14,12},{1,3},{3,1},... | collective-permute-start | bytes 1572872 | tf_op jit(solution)/shard_map/ppermute | solution.py:109
  399.6 15.9 %collective-permute-start.4 = (f32[16,32,128]{2,1,0:T(8,128)S(1)}, f32[16,32,128]{2,1,0:T(8,128)S(1)}, u32[]{:S(2)}, u32[]{:S(2)}) collective-permute-start(f32[16,32,128]{2,1,0:T(8,128)S(1)} %dynamic-slice_bitcast_fusion.2), channel_id=1, source_target_pairs={{0,4},{2,6},{4,0},{6,2},{8,12},{10,14},{12,8},{14,10},{1,5},{3,7},... | collective-permute-start | bytes 786440 | tf_op jit(solution)/shard_map/ppermute | solution.py:109
  415.6 14.0 %collective-permute-start.5 = (f32[8,32,128]{2,1,0:T(8,128)S(1)}, f32[8,32,128]{2,1,0:T(8,128)S(1)}, u32[]{:S(2)}, u32[]{:S(2)}) collective-permute-start(f32[8,32,128]{2,1,0:T(8,128)S(1)} %dynamic-slice_bitcast_fusion.3), channel_id=1, source_target_pairs={{0,8},{2,10},{4,12},{6,14},{8,0},{10,2},{12,4},{14,6},{1,9},{3,11}... | collective-permute-start | bytes 393224 | tf_op jit(solution)/shard_map/ppermute | solution.py:109
  435.8 9.7 %collective-permute-start.7 = (f32[2,32,128]{2,1,0:T(8,128)S(1)}, f32[2,32,128]{2,1,0:T(8,128)S(1)}, u32[]{:S(2)}, u32[]{:S(2)}) collective-permute-start(f32[2,32,128]{2,1,0:T(8,128)S(1)} %dynamic-slice_bitcast_fusion.5), channel_id=1, source_target_pairs={{0,32},{16,48},{32,0},{48,16},{64,96},{80,112},{96,64},{112,80},{1... | collective-permute-start | bytes 98312 | tf_op jit(solution)/shard_map/ppermute | solution.py:109
  445.5 13.5 %collective-permute-start.8 = (f32[1,32,128]{2,1,0:T(8,128)S(1)}, f32[1,32,128]{2,1,0:T(8,128)S(1)}, u32[]{:S(2)}, u32[]{:S(2)}) collective-permute-start(f32[1,32,128]{2,1,0:T(8,128)S(1)} %constant_dynamic-slice_fusion), channel_id=1, source_target_pairs={{0,64},{16,80},{32,96},{48,112},{64,0},{80,16},{96,32},{112,48},{1... | collective-permute-start | bytes 49160 | tf_op jit(solution)/shard_map/ppermute | solution.py:109
  (8 other events, 97.9 us)

commit v5 on v4

--- a/solution.py
+++ b/solution.py
@@ -74,9 +74,18 @@
     return output.astype(jnp.bfloat16).reshape(inputs.shape)
 
 
-def block_backward(inputs, upstream, kernel, scale, weight_in, weight_out):
+def block_forward_saving(inputs, kernel, scale, weight_in, weight_out):
     width = inputs.shape[-1]
     normed, inv_std, flat, slope, hidden = block_inner(inputs, kernel, weight_in)
+    branch = jnp.dot(hidden, weight_out, preferred_element_type=jnp.float32)
+    output = inputs.reshape(-1, width).astype(jnp.float32) + scale * branch
+    return (output.astype(jnp.bfloat16).reshape(inputs.shape), normed, inv_std, slope)
+
+
+def block_backward_saved(normed, inv_std, slope, upstream, kernel, scale, weight_in, weight_out):
+    inputs = upstream
+    width = inputs.shape[-1]
+    flat = normed.reshape(-1, width).astype(jnp.bfloat16)
     up_flat = upstream.reshape(-1, width).astype(jnp.float32)
     branch_grad = (scale * up_flat).astype(jnp.bfloat16)
     hidden_grad = lax.dot_general(
@@ -123,54 +132,55 @@
     factor = 1.0 / (micro_count * pixel_rows)
     blank = jnp.zeros(images.shape[1:], jnp.bfloat16)
 
-    def run_forward(entering):
-        return block_forward(entering, kernel, scale, weight_in, weight_out)
-
     def forward_tick(tick, carry):
         incoming, kept = carry
         micro = tick - section
         slot = jnp.clip(micro, 0, micro_count - 1)
         own = lax.dynamic_index_in_dim(images, slot, 0, keepdims=False)
         entering = jnp.where(section == 0, own, incoming)
-        leaving = run_forward(entering)
-        kept = place(kept, entering, micro, micro_count)
+        leaving, normed, inv_std, slope = block_forward_saving(
+            entering, kernel, scale, weight_in, weight_out
+        )
+        kept = tuple(
+            place(buffer, value, micro, micro_count)
+            for buffer, value in zip(kept, (normed, inv_std, slope))
+        )
         incoming = shifted(leaving, "section", 1)
         return (incoming, kept)
 
     spare = (micro_count + 2,) + images.shape[1:]
-    _, kept = lax.fori_loop(0, ticks, forward_tick, (blank, jnp.zeros(spare, jnp.bfloat16)))
-
-    def run_backward(entering, upstream):
-        return block_backward(entering, upstream, kernel, scale, weight_in, weight_out)
-
-    stores = (
-        jnp.zeros((micro_count + 2, pixel_rows, width), jnp.bfloat16),
-        jnp.zeros((micro_count + 2, pixel_rows, hidden_width), jnp.bfloat16),
-    )
-    summed = jnp.zeros((1,), jnp.float32)
+    kept = (
+        jnp.zeros(spare, jnp.float32),
+        jnp.zeros(spare[:-1] + (1,), jnp.float32),
+        jnp.zeros((micro_count + 2, pixel_rows, hidden_width), jnp.float32),
+    )
+    _, kept = lax.fori_loop(0, ticks, forward_tick, (blank, kept))
+
+    stores = jnp.zeros((micro_count + 2, pixel_rows, hidden_width), jnp.bfloat16)
 
     def backward_tick(tick, carry):
-        incoming, grads, stored, total = carry
+        incoming, grads, stored = carry
         micro = tick - (sections - 1 - section)
         slot = jnp.clip(micro, 0, micro_count - 1)
         own = lax.dynamic_index_in_dim(cotangent, slot, 0, keepdims=False)
         upstream = jnp.where(section == sections - 1, own, incoming)
-        entering = lax.dynamic_index_in_dim(kept, slot + 1, 0, keepdims=False)
-        input_grad, flat, pre_grad = run_backward(entering, upstream)
+        normed, inv_std, slope = (
+            lax.dynamic_index_in_dim(buffer, slot + 1, 0, keepdims=False) for buffer in kept
+        )
+        input_grad, flat, pre_grad = block_backward_saved(
+            normed, inv_std, slope, upstream, kernel, scale, weight_in, weight_out
+        )
         grads = place(grads, input_grad, micro, micro_count)
-        stored = (
-            place(stored[0], flat, micro, micro_count),
-            place(stored[1], pre_grad, micro, micro_count),
-        )
+        stored = place(stored, pre_grad, micro, micro_count)
         incoming = shifted(input_grad, "section", -1)
-        return (incoming, grads, stored, total)
-
-    _, grads, stores, summed = lax.fori_loop(
-        0, ticks, backward_tick, (blank, jnp.zeros(spare, jnp.bfloat16), stores, summed)
+        return (incoming, grads, stored)
+
+    _, grads, stores = lax.fori_loop(
+        0, ticks, backward_tick, (blank, jnp.zeros(spare, jnp.bfloat16), stores)
     )
     grads = grads[1 : micro_count + 1]
-    all_flat = stores[0][1 : micro_count + 1].reshape(micro_count * pixel_rows, width)
-    all_pre = stores[1][1 : micro_count + 1].reshape(micro_count * pixel_rows, hidden_width)
+    all_flat = kept[0][1 : micro_count + 1].reshape(micro_count * pixel_rows, width).astype(jnp.bfloat16)
+    all_pre = stores[1 : micro_count + 1].reshape(micro_count * pixel_rows, hidden_width)
     partial = (
         lax.dot_general(
             all_pre, all_flat, (((0,), (0,)), ((), ())), preferred_element_type=jnp.float32

time: 463 us -> 448 us (0.968)
  other arithmetic: 144 us -> 96.6 us
  local copies, waits for them, and re-layouts: 35 us -> 51.8 us
  matrix products: 33.7 us -> 50.4 us
    reduce_sum x22 -> x11, other arithmetic: 55 us -> 28.5 us  [block_inner(): center = mixed - jnp.mean(mixed, axis=-1, keepdims=True)]
    another operation x22, other arithmetic: 15.4 us -> 0.45 us
    dynamic_slice x0 -> x11, local copies, waits for them, and re-layouts: none -> 10.6 us  [backward_tick(): lax.dynamic_index_in_dim(buffer, slot + 1, 0, keepdims=False)]
    convert_element_type x33 -> x22, other arithmetic: 20.6 us -> 10.4 us  [the longest x11 10.2 us: block_backward_saved(): upstream.astype(jnp.float32) + depthwise_adjoint(mixed_grad, kernel)]
    mul x11, other arithmetic: 1.73 us -> 11.8 us  [block_backward_saved(): mixed_grad = inv_std * (normed_grad - mean_grad - normed * mean_cross)]
    dot_general x11, matrix products: 5.14 us -> 14.5 us  [block_inner(): lax.dot_general(flat, weight_in, (((1,), (1,)), ((), ())), preferred_elem...]
    dot_general x33, matrix products: 25.2 us -> 33.8 us  [the longest x11 24.9 us: block_backward_saved(): lax.dot_general(branch_grad, weight_out, (((1,), (1,)), ((), ())), prefer...]
    mul x0 -> x11, local copies, waits for them, and re-layouts: none -> 7.75 us  [block_backward_saved(): mixed_grad = inv_std * (normed_grad - mean_grad - normed * mean_cross)]
where the time goes in v5:
time: 448 us; the launch traced here: 444 us
  waiting for transfers between devices  136 us (30%)
  starting transfers between devices  106 us (24%)
  other arithmetic  96.6 us (22%)
  local copies, waits for them, and re-layouts  51.8 us (12%)
  matrix products  50.4 us (11%)
    ppermute x22, waiting for transfers between devices, shifted(): return lax.ppermute(block, axis, route)  91 us
    ppermute x22, starting transfers between devices, shifted(): return lax.ppermute(block, axis, route)  73.8 us
    ppermute x7, waiting for transfers between devices, halve(): return keep + lax.ppermute(send, axis, route)  44.7 us
    dynamic_update_slice x33, other arithmetic, place(): return lax.dynamic_update_index_in_dim(buffer, value, slot, 0)  40.3 us
    ppermute x7, starting transfers between devices, halve(): return keep + lax.ppermute(send, axis, route)  32.6 us
    reduce_sum x11, other arithmetic, block_inner(): center = mixed - jnp.mean(mixed, axis=-1, keepdims=True)  28.5 us
    dot_general x11, matrix products, block_backward_saved(): lax.dot_general(branch_grad, weight_out, (((1,), (1,)), ((), ())), prefer...  24.9 us
    dot_general x11, matrix products, block_inner(): lax.dot_general(flat, weight_in, (((1,), (1,)), ((), ())), preferred_elem...  14.5 us
  transfers between devices with their start and end apart: 29, of which 29 were waited for; matrix products, arithmetic and copies ran while one was open for 4% of the time, Pallas kernels for 0%

profile of v5, /device:TPU:6, one launch (start us, length us, event | category | flops | bytes accessed | tf_op | source)
XLA Modules:
  0.0 444.2 jit_solution(3803932322761113214)
XLA Ops:
  14.9 143.9 %while.41 = (s32[]{:T(128)}, bf16[1,10,10,352]{3,2,1,0:T(8,128)(2,1)S(1)}, f32[6,1,10,10,352]{4,3,2,1,0:T(8,128)}, f32[6,1,10,10,1]{3,2,4,1,0:T(8,128)}, f32[6,1...) while((s32[]{:T(128)}, ...), condition=%wide.region_3.4_spmd, body=%wide.region_0.3_spmd.sunk | while | flops 203984320 | bytes 6215344 | solution.py:157
  31.8 5.6 %collective-permute-start = (bf16[1,10,10,352]{3,2,1,0:T(8,128)(2,1)S(1)}, bf16[1,10,10,352]{3,2,1,0:T(8,128)(2,1)S(1)}, u32[]{:S(2)}, u32[]{:S(2)}) collective-permute-start(bf16[1,10,10,352]{3,2,1,0:T(8,128)(2,1)S(1)} %reshape.633), channel_id=1, source_target_pairs={{0,128},{128,256},{256,384},{384,512},{512,640},{640,768},{768,896... | collective-permute-start | bytes 211208 | tf_op jit(solution)/shard_map/while/body/eval_jaxpr/ppermute | solution.py:15
  51.6 6.6 %collective-permute-done = bf16[1,10,10,352]{3,2,1,0:T(8,128)(2,1)S(1)} collective-permute-done((bf16[1,10,10,352]{3,2,1,0:T(8,128)(2,1)S(1)}, bf16[1,10,10,352]{3,2,1,0:T(8,128)(2,1)S(1)}, u32[]{:S(2)}, u32[]{:S(2)}) %collective-permute-start) | collective-permute-done | bytes 70432 | tf_op jit(solution)/shard_map/while/body/eval_jaxpr/ppermute | solution.py:15
  110.8 5.6 %collective-permute-start = (bf16[1,10,10,352]{3,2,1,0:T(8,128)(2,1)S(1)}, bf16[1,10,10,352]{3,2,1,0:T(8,128)(2,1)S(1)}, u32[]{:S(2)}, u32[]{:S(2)}) collective-permute-start(bf16[1,10,10,352]{3,2,1,0:T(8,128)(2,1)S(1)} %reshape.633), channel_id=1, source_target_pairs={{0,128},{128,256},{256,384},{384,512},{512,640},{640,768},{768,896... | collective-permute-start | bytes 211208 | tf_op jit(solution)/shard_map/while/body/eval_jaxpr/ppermute | solution.py:15
  124.1 5.6 %collective-permute-start = (bf16[1,10,10,352]{3,2,1,0:T(8,128)(2,1)S(1)}, bf16[1,10,10,352]{3,2,1,0:T(8,128)(2,1)S(1)}, u32[]{:S(2)}, u32[]{:S(2)}) collective-permute-start(bf16[1,10,10,352]{3,2,1,0:T(8,128)(2,1)S(1)} %reshape.633), channel_id=1, source_target_pairs={{0,128},{128,256},{256,384},{384,512},{512,640},{640,768},{768,896... | collective-permute-start | bytes 211208 | tf_op jit(solution)/shard_map/while/body/eval_jaxpr/ppermute | solution.py:15
  137.9 5.6 %collective-permute-start = (bf16[1,10,10,352]{3,2,1,0:T(8,128)(2,1)S(1)}, bf16[1,10,10,352]{3,2,1,0:T(8,128)(2,1)S(1)}, u32[]{:S(2)}, u32[]{:S(2)}) collective-permute-start(bf16[1,10,10,352]{3,2,1,0:T(8,128)(2,1)S(1)} %reshape.633), channel_id=1, source_target_pairs={{0,128},{128,256},{256,384},{384,512},{512,640},{640,768},{768,896... | collective-permute-start | bytes 211208 | tf_op jit(solution)/shard_map/while/body/eval_jaxpr/ppermute | solution.py:15
  150.8 5.6 %collective-permute-start = (bf16[1,10,10,352]{3,2,1,0:T(8,128)(2,1)S(1)}, bf16[1,10,10,352]{3,2,1,0:T(8,128)(2,1)S(1)}, u32[]{:S(2)}, u32[]{:S(2)}) collective-permute-start(bf16[1,10,10,352]{3,2,1,0:T(8,128)(2,1)S(1)} %reshape.633), channel_id=1, source_target_pairs={{0,128},{128,256},{256,384},{384,512},{512,640},{640,768},{768,896... | collective-permute-start | bytes 211208 | tf_op jit(solution)/shard_map/while/body/eval_jaxpr/ppermute | solution.py:15
  163.6 188.3 %while.42 = (s32[]{:T(128)}, bf16[1,10,10,352]{3,2,1,0:T(8,128)(2,1)S(1)}, bf16[6,1,10,10,352]{4,3,2,1,0:T(8,128)(2,1)}, bf16[6,100,1408]{2,1,0:T(8,128)(2,1)}, ...) while((s32[]{:T(128)}, ...), condition=%wide.region_7.8_spmd, body=%wide.region_4.7_spmd.sunk | while | flops 202400032 | bytes 6513550 | solution.py:178
  174.5 6.6 %collective-permute-done.1 = bf16[1,10,10,352]{3,2,1,0:T(8,128)(2,1)S(1)} collective-permute-done((bf16[1,10,10,352]{3,2,1,0:T(8,128)(2,1)S(1)}, bf16[1,10,10,352]{3,2,1,0:T(8,128)(2,1)S(1)}, u32[]{:S(2)}, u32[]{:S(2)}) %collective-permute-start.1) | collective-permute-done | bytes 70432 | tf_op jit(solution)/shard_map/while/body/eval_jaxpr/ppermute | solution.py:15
  192.0 7.4 %collective-permute-done.1 = bf16[1,10,10,352]{3,2,1,0:T(8,128)(2,1)S(1)} collective-permute-done((bf16[1,10,10,352]{3,2,1,0:T(8,128)(2,1)S(1)}, bf16[1,10,10,352]{3,2,1,0:T(8,128)(2,1)S(1)}, u32[]{:S(2)}, u32[]{:S(2)}) %collective-permute-start.1) | collective-permute-done | bytes 70432 | tf_op jit(solution)/shard_map/while/body/eval_jaxpr/ppermute | solution.py:15
  210.2 6.5 %collective-permute-done.1 = bf16[1,10,10,352]{3,2,1,0:T(8,128)(2,1)S(1)} collective-permute-done((bf16[1,10,10,352]{3,2,1,0:T(8,128)(2,1)S(1)}, bf16[1,10,10,352]{3,2,1,0:T(8,128)(2,1)S(1)}, u32[]{:S(2)}, u32[]{:S(2)}) %collective-permute-start.1) | collective-permute-done | bytes 70432 | tf_op jit(solution)/shard_map/while/body/eval_jaxpr/ppermute | solution.py:15
  227.5 6.1 %collective-permute-done.1 = bf16[1,10,10,352]{3,2,1,0:T(8,128)(2,1)S(1)} collective-permute-done((bf16[1,10,10,352]{3,2,1,0:T(8,128)(2,1)S(1)}, bf16[1,10,10,352]{3,2,1,0:T(8,128)(2,1)S(1)}, u32[]{:S(2)}, u32[]{:S(2)}) %collective-permute-start.1) | collective-permute-done | bytes 70432 | tf_op jit(solution)/shard_map/while/body/eval_jaxpr/ppermute | solution.py:15
  244.5 6.1 %collective-permute-done.1 = bf16[1,10,10,352]{3,2,1,0:T(8,128)(2,1)S(1)} collective-permute-done((bf16[1,10,10,352]{3,2,1,0:T(8,128)(2,1)S(1)}, bf16[1,10,10,352]{3,2,1,0:T(8,128)(2,1)S(1)}, u32[]{:S(2)}, u32[]{:S(2)}) %collective-permute-start.1) | collective-permute-done | bytes 70432 | tf_op jit(solution)/shard_map/while/body/eval_jaxpr/ppermute | solution.py:15
  261.3 6.1 %collective-permute-done.1 = bf16[1,10,10,352]{3,2,1,0:T(8,128)(2,1)S(1)} collective-permute-done((bf16[1,10,10,352]{3,2,1,0:T(8,128)(2,1)S(1)}, bf16[1,10,10,352]{3,2,1,0:T(8,128)(2,1)S(1)}, u32[]{:S(2)}, u32[]{:S(2)}) %collective-permute-start.1) | collective-permute-done | bytes 70432 | tf_op jit(solution)/shard_map/while/body/eval_jaxpr/ppermute | solution.py:15
  278.2 6.1 %collective-permute-done.1 = bf16[1,10,10,352]{3,2,1,0:T(8,128)(2,1)S(1)} collective-permute-done((bf16[1,10,10,352]{3,2,1,0:T(8,128)(2,1)S(1)}, bf16[1,10,10,352]{3,2,1,0:T(8,128)(2,1)S(1)}, u32[]{:S(2)}, u32[]{:S(2)}) %collective-permute-start.1) | collective-permute-done | bytes 70432 | tf_op jit(solution)/shard_map/while/body/eval_jaxpr/ppermute | solution.py:15
  295.1 6.1 %collective-permute-done.1 = bf16[1,10,10,352]{3,2,1,0:T(8,128)(2,1)S(1)} collective-permute-done((bf16[1,10,10,352]{3,2,1,0:T(8,128)(2,1)S(1)}, bf16[1,10,10,352]{3,2,1,0:T(8,128)(2,1)S(1)}, u32[]{:S(2)}, u32[]{:S(2)}) %collective-permute-start.1) | collective-permute-done | bytes 70432 | tf_op jit(solution)/shard_map/while/body/eval_jaxpr/ppermute | solution.py:15
  312.0 6.1 %collective-permute-done.1 = bf16[1,10,10,352]{3,2,1,0:T(8,128)(2,1)S(1)} collective-permute-done((bf16[1,10,10,352]{3,2,1,0:T(8,128)(2,1)S(1)}, bf16[1,10,10,352]{3,2,1,0:T(8,128)(2,1)S(1)}, u32[]{:S(2)}, u32[]{:S(2)}) %collective-permute-start.1) | collective-permute-done | bytes 70432 | tf_op jit(solution)/shard_map/while/body/eval_jaxpr/ppermute | solution.py:15
  329.0 6.1 %collective-permute-done.1 = bf16[1,10,10,352]{3,2,1,0:T(8,128)(2,1)S(1)} collective-permute-done((bf16[1,10,10,352]{3,2,1,0:T(8,128)(2,1)S(1)}, bf16[1,10,10,352]{3,2,1,0:T(8,128)(2,1)S(1)}, u32[]{:S(2)}, u32[]{:S(2)}) %collective-permute-start.1) | collective-permute-done | bytes 70432 | tf_op jit(solution)/shard_map/while/body/eval_jaxpr/ppermute | solution.py:15
  345.9 6.1 %collective-permute-done.1 = bf16[1,10,10,352]{3,2,1,0:T(8,128)(2,1)S(1)} collective-permute-done((bf16[1,10,10,352]{3,2,1,0:T(8,128)(2,1)S(1)}, bf16[1,10,10,352]{3,2,1,0:T(8,128)(2,1)S(1)}, u32[]{:S(2)}, u32[]{:S(2)}) %collective-permute-start.1) | collective-permute-done | bytes 70432 | tf_op jit(solution)/shard_map/while/body/eval_jaxpr/ppermute | solution.py:15
  371.2 13.9 %collective-permute-done.3 = f32[32,32,128]{2,1,0:T(8,128)S(1)} collective-permute-done((f32[32,32,128]{2,1,0:T(8,128)S(1)}, f32[32,32,128]{2,1,0:T(8,128)S(1)}, u32[]{:S(2)}, u32[]{:S(2)}) %collective-permute-start.3) | collective-permute-done | bytes 524320 | tf_op jit(solution)/shard_map/ppermute | solution.py:118
  387.3 13.9 %collective-permute-done.4 = f32[16,32,128]{2,1,0:T(8,128)S(1)} collective-permute-done((f32[16,32,128]{2,1,0:T(8,128)S(1)}, f32[16,32,128]{2,1,0:T(8,128)S(1)}, u32[]{:S(2)}, u32[]{:S(2)}) %collective-permute-start.4) | collective-permute-done | bytes 262176 | tf_op jit(solution)/shard_map/ppermute | solution.py:118
  406.4 8.5 %collective-permute-done.5 = f32[8,32,128]{2,1,0:T(8,128)S(1)} collective-permute-done((f32[8,32,128]{2,1,0:T(8,128)S(1)}, f32[8,32,128]{2,1,0:T(8,128)S(1)}, u32[]{:S(2)}, u32[]{:S(2)}) %collective-permute-start.5) | collective-permute-done | bytes 131104 | tf_op jit(solution)/shard_map/ppermute | solution.py:118
  421.1 6.8 %collective-permute-start.7 = (f32[2,32,128]{2,1,0:T(8,128)S(1)}, f32[2,32,128]{2,1,0:T(8,128)S(1)}, u32[]{:S(2)}, u32[]{:S(2)}) collective-permute-start(f32[2,32,128]{2,1,0:T(8,128)S(1)} %dynamic-slice_bitcast_fusion.6), channel_id=1, source_target_pairs={{0,32},{16,48},{32,0},{48,16},{64,96},{80,112},{96,64},{112,80},{1... | collective-permute-start | bytes 98312 | tf_op jit(solution)/shard_map/ppermute | solution.py:118
  429.9 11.9 %collective-permute-start.8 = (f32[1,32,128]{2,1,0:T(8,128)S(1)}, f32[1,32,128]{2,1,0:T(8,128)S(1)}, u32[]{:S(2)}, u32[]{:S(2)}) collective-permute-start(f32[1,32,128]{2,1,0:T(8,128)S(1)} %constant_dynamic-slice_fusion.1), channel_id=1, source_target_pairs={{0,64},{16,80},{32,96},{48,112},{64,0},{80,16},{96,32},{112,48},{1... | collective-permute-start | bytes 49160 | tf_op jit(solution)/shard_map/ppermute | solution.py:118
  (450 shorter events, 282.3 us)
Async XLA Ops:
  19.8 7.2 %collective-permute-start = (bf16[1,10,10,352]{3,2,1,0:T(8,128)(2,1)S(1)}, bf16[1,10,10,352]{3,2,1,0:T(8,128)(2,1)S(1)}, u32[]{:S(2)}, u32[]{:S(2)}) collective-permute-start(bf16[1,10,10,352]{3,2,1,0:T(8,128)(2,1)S(1)} %reshape.633), channel_id=1, source_target_pairs={{0,128},{128,256},{256,384},{384,512},{512,640},{640,768},{768,896... | collective-permute-start | bytes 211208 | tf_op jit(solution)/shard_map/while/body/eval_jaxpr/ppermute | solution.py:15
  31.8 8.0 %collective-permute-start = (bf16[1,10,10,352]{3,2,1,0:T(8,128)(2,1)S(1)}, bf16[1,10,10,352]{3,2,1,0:T(8,128)(2,1)S(1)}, u32[]{:S(2)}, u32[]{:S(2)}) collective-permute-start(bf16[1,10,10,352]{3,2,1,0:T(8,128)(2,1)S(1)} %reshape.633), channel_id=1, source_target_pairs={{0,128},{128,256},{256,384},{384,512},{512,640},{640,768},{768,896... | collective-permute-start | bytes 211208 | tf_op jit(solution)/shard_map/while/body/eval_jaxpr/ppermute | solution.py:15
  44.6 13.6 %collective-permute-start = (bf16[1,10,10,352]{3,2,1,0:T(8,128)(2,1)S(1)}, bf16[1,10,10,352]{3,2,1,0:T(8,128)(2,1)S(1)}, u32[]{:S(2)}, u32[]{:S(2)}) collective-permute-start(bf16[1,10,10,352]{3,2,1,0:T(8,128)(2,1)S(1)} %reshape.633), channel_id=1, source_target_pairs={{0,128},{128,256},{256,384},{384,512},{512,640},{640,768},{768,896... | collective-permute-start | bytes 211208 | tf_op jit(solution)/shard_map/while/body/eval_jaxpr/ppermute | solution.py:15
  98.1 7.8 %collective-permute-start = (bf16[1,10,10,352]{3,2,1,0:T(8,128)(2,1)S(1)}, bf16[1,10,10,352]{3,2,1,0:T(8,128)(2,1)S(1)}, u32[]{:S(2)}, u32[]{:S(2)}) collective-permute-start(bf16[1,10,10,352]{3,2,1,0:T(8,128)(2,1)S(1)} %reshape.633), channel_id=1, source_target_pairs={{0,128},{128,256},{256,384},{384,512},{512,640},{640,768},{768,896... | collective-permute-start | bytes 211208 | tf_op jit(solution)/shard_map/while/body/eval_jaxpr/ppermute | solution.py:15
  110.8 8.5 %collective-permute-start = (bf16[1,10,10,352]{3,2,1,0:T(8,128)(2,1)S(1)}, bf16[1,10,10,352]{3,2,1,0:T(8,128)(2,1)S(1)}, u32[]{:S(2)}, u32[]{:S(2)}) collective-permute-start(bf16[1,10,10,352]{3,2,1,0:T(8,128)(2,1)S(1)} %reshape.633), channel_id=1, source_target_pairs={{0,128},{128,256},{256,384},{384,512},{512,640},{640,768},{768,896... | collective-permute-start | bytes 211208 | tf_op jit(solution)/shard_map/while/body/eval_jaxpr/ppermute | solution.py:15
  124.1 8.9 %collective-permute-start = (bf16[1,10,10,352]{3,2,1,0:T(8,128)(2,1)S(1)}, bf16[1,10,10,352]{3,2,1,0:T(8,128)(2,1)S(1)}, u32[]{:S(2)}, u32[]{:S(2)}) collective-permute-start(bf16[1,10,10,352]{3,2,1,0:T(8,128)(2,1)S(1)} %reshape.633), channel_id=1, source_target_pairs={{0,128},{128,256},{256,384},{384,512},{512,640},{640,768},{768,896... | collective-permute-start | bytes 211208 | tf_op jit(solution)/shard_map/while/body/eval_jaxpr/ppermute | solution.py:15
  137.9 8.1 %collective-permute-start = (bf16[1,10,10,352]{3,2,1,0:T(8,128)(2,1)S(1)}, bf16[1,10,10,352]{3,2,1,0:T(8,128)(2,1)S(1)}, u32[]{:S(2)}, u32[]{:S(2)}) collective-permute-start(bf16[1,10,10,352]{3,2,1,0:T(8,128)(2,1)S(1)} %reshape.633), channel_id=1, source_target_pairs={{0,128},{128,256},{256,384},{384,512},{512,640},{640,768},{768,896... | collective-permute-start | bytes 211208 | tf_op jit(solution)/shard_map/while/body/eval_jaxpr/ppermute | solution.py:15
  150.8 8.0 %collective-permute-start = (bf16[1,10,10,352]{3,2,1,0:T(8,128)(2,1)S(1)}, bf16[1,10,10,352]{3,2,1,0:T(8,128)(2,1)S(1)}, u32[]{:S(2)}, u32[]{:S(2)}) collective-permute-start(bf16[1,10,10,352]{3,2,1,0:T(8,128)(2,1)S(1)} %reshape.633), channel_id=1, source_target_pairs={{0,128},{128,256},{256,384},{384,512},{512,640},{640,768},{768,896... | collective-permute-start | bytes 211208 | tf_op jit(solution)/shard_map/while/body/eval_jaxpr/ppermute | solution.py:15
  172.6 8.6 %collective-permute-start.1 = (bf16[1,10,10,352]{3,2,1,0:T(8,128)(2,1)S(1)}, bf16[1,10,10,352]{3,2,1,0:T(8,128)(2,1)S(1)}, u32[]{:S(2)}, u32[]{:S(2)}) collective-permute-start(bf16[1,10,10,352]{3,2,1,0:T(8,128)(2,1)S(1)} %get-tuple-element.4248), channel_id=1, source_target_pairs={{128,0},{256,128},{384,256},{512,384},{640,512},{768,640},{896,768... | collective-permute-start | bytes 211208 | tf_op jit(solution)/shard_map/while/body/eval_jaxpr/ppermute | solution.py:15
  190.1 9.3 %collective-permute-start.1 = (bf16[1,10,10,352]{3,2,1,0:T(8,128)(2,1)S(1)}, bf16[1,10,10,352]{3,2,1,0:T(8,128)(2,1)S(1)}, u32[]{:S(2)}, u32[]{:S(2)}) collective-permute-start(bf16[1,10,10,352]{3,2,1,0:T(8,128)(2,1)S(1)} %get-tuple-element.4248), channel_id=1, source_target_pairs={{128,0},{256,128},{384,256},{512,384},{640,512},{768,640},{896,768... | collective-permute-start | bytes 211208 | tf_op jit(solution)/shard_map/while/body/eval_jaxpr/ppermute | solution.py:15
  208.3 8.4 %collective-permute-start.1 = (bf16[1,10,10,352]{3,2,1,0:T(8,128)(2,1)S(1)}, bf16[1,10,10,352]{3,2,1,0:T(8,128)(2,1)S(1)}, u32[]{:S(2)}, u32[]{:S(2)}) collective-permute-start(bf16[1,10,10,352]{3,2,1,0:T(8,128)(2,1)S(1)} %get-tuple-element.4248), channel_id=1, source_target_pairs={{128,0},{256,128},{384,256},{512,384},{640,512},{768,640},{896,768... | collective-permute-start | bytes 211208 | tf_op jit(solution)/shard_map/while/body/eval_jaxpr/ppermute | solution.py:15
  225.6 8.0 %collective-permute-start.1 = (bf16[1,10,10,352]{3,2,1,0:T(8,128)(2,1)S(1)}, bf16[1,10,10,352]{3,2,1,0:T(8,128)(2,1)S(1)}, u32[]{:S(2)}, u32[]{:S(2)}) collective-permute-start(bf16[1,10,10,352]{3,2,1,0:T(8,128)(2,1)S(1)} %get-tuple-element.4248), channel_id=1, source_target_pairs={{128,0},{256,128},{384,256},{512,384},{640,512},{768,640},{896,768... | collective-permute-start | bytes 211208 | tf_op jit(solution)/shard_map/while/body/eval_jaxpr/ppermute | solution.py:15
  242.5 8.0 %collective-permute-start.1 = (bf16[1,10,10,352]{3,2,1,0:T(8,128)(2,1)S(1)}, bf16[1,10,10,352]{3,2,1,0:T(8,128)(2,1)S(1)}, u32[]{:S(2)}, u32[]{:S(2)}) collective-permute-start(bf16[1,10,10,352]{3,2,1,0:T(8,128)(2,1)S(1)} %get-tuple-element.4248), channel_id=1, source_target_pairs={{128,0},{256,128},{384,256},{512,384},{640,512},{768,640},{896,768... | collective-permute-start | bytes 211208 | tf_op jit(solution)/shard_map/while/body/eval_jaxpr/ppermute | solution.py:15
  259.4 8.0 %collective-permute-start.1 = (bf16[1,10,10,352]{3,2,1,0:T(8,128)(2,1)S(1)}, bf16[1,10,10,352]{3,2,1,0:T(8,128)(2,1)S(1)}, u32[]{:S(2)}, u32[]{:S(2)}) collective-permute-start(bf16[1,10,10,352]{3,2,1,0:T(8,128)(2,1)S(1)} %get-tuple-element.4248), channel_id=1, source_target_pairs={{128,0},{256,128},{384,256},{512,384},{640,512},{768,640},{896,768... | collective-permute-start | bytes 211208 | tf_op jit(solution)/shard_map/while/body/eval_jaxpr/ppermute | solution.py:15
  276.3 8.0 %collective-permute-start.1 = (bf16[1,10,10,352]{3,2,1,0:T(8,128)(2,1)S(1)}, bf16[1,10,10,352]{3,2,1,0:T(8,128)(2,1)S(1)}, u32[]{:S(2)}, u32[]{:S(2)}) collective-permute-start(bf16[1,10,10,352]{3,2,1,0:T(8,128)(2,1)S(1)} %get-tuple-element.4248), channel_id=1, source_target_pairs={{128,0},{256,128},{384,256},{512,384},{640,512},{768,640},{896,768... | collective-permute-start | bytes 211208 | tf_op jit(solution)/shard_map/while/body/eval_jaxpr/ppermute | solution.py:15
  293.2 8.0 %collective-permute-start.1 = (bf16[1,10,10,352]{3,2,1,0:T(8,128)(2,1)S(1)}, bf16[1,10,10,352]{3,2,1,0:T(8,128)(2,1)S(1)}, u32[]{:S(2)}, u32[]{:S(2)}) collective-permute-start(bf16[1,10,10,352]{3,2,1,0:T(8,128)(2,1)S(1)} %get-tuple-element.4248), channel_id=1, source_target_pairs={{128,0},{256,128},{384,256},{512,384},{640,512},{768,640},{896,768... | collective-permute-start | bytes 211208 | tf_op jit(solution)/shard_map/while/body/eval_jaxpr/ppermute | solution.py:15
  310.1 8.0 %collective-permute-start.1 = (bf16[1,10,10,352]{3,2,1,0:T(8,128)(2,1)S(1)}, bf16[1,10,10,352]{3,2,1,0:T(8,128)(2,1)S(1)}, u32[]{:S(2)}, u32[]{:S(2)}) collective-permute-start(bf16[1,10,10,352]{3,2,1,0:T(8,128)(2,1)S(1)} %get-tuple-element.4248), channel_id=1, source_target_pairs={{128,0},{256,128},{384,256},{512,384},{640,512},{768,640},{896,768... | collective-permute-start | bytes 211208 | tf_op jit(solution)/shard_map/while/body/eval_jaxpr/ppermute | solution.py:15
  327.0 8.0 %collective-permute-start.1 = (bf16[1,10,10,352]{3,2,1,0:T(8,128)(2,1)S(1)}, bf16[1,10,10,352]{3,2,1,0:T(8,128)(2,1)S(1)}, u32[]{:S(2)}, u32[]{:S(2)}) collective-permute-start(bf16[1,10,10,352]{3,2,1,0:T(8,128)(2,1)S(1)} %get-tuple-element.4248), channel_id=1, source_target_pairs={{128,0},{256,128},{384,256},{512,384},{640,512},{768,640},{896,768... | collective-permute-start | bytes 211208 | tf_op jit(solution)/shard_map/while/body/eval_jaxpr/ppermute | solution.py:15
  344.0 8.0 %collective-permute-start.1 = (bf16[1,10,10,352]{3,2,1,0:T(8,128)(2,1)S(1)}, bf16[1,10,10,352]{3,2,1,0:T(8,128)(2,1)S(1)}, u32[]{:S(2)}, u32[]{:S(2)}) collective-permute-start(bf16[1,10,10,352]{3,2,1,0:T(8,128)(2,1)S(1)} %get-tuple-element.4248), channel_id=1, source_target_pairs={{128,0},{256,128},{384,256},{512,384},{640,512},{768,640},{896,768... | collective-permute-start | bytes 211208 | tf_op jit(solution)/shard_map/while/body/eval_jaxpr/ppermute | solution.py:15
  369.2 15.9 %collective-permute-start.3 = (f32[32,32,128]{2,1,0:T(8,128)S(1)}, f32[32,32,128]{2,1,0:T(8,128)S(1)}, u32[]{:S(2)}, u32[]{:S(2)}) collective-permute-start(f32[32,32,128]{2,1,0:T(8,128)S(1)} %dynamic-slice_bitcast_fusion.2), channel_id=1, source_target_pairs={{0,2},{2,0},{4,6},{6,4},{8,10},{10,8},{12,14},{14,12},{1,3},{3,1},... | collective-permute-start | bytes 1572872 | tf_op jit(solution)/shard_map/ppermute | solution.py:118
  385.2 16.0 %collective-permute-start.4 = (f32[16,32,128]{2,1,0:T(8,128)S(1)}, f32[16,32,128]{2,1,0:T(8,128)S(1)}, u32[]{:S(2)}, u32[]{:S(2)}) collective-permute-start(f32[16,32,128]{2,1,0:T(8,128)S(1)} %dynamic-slice_bitcast_fusion.3), channel_id=1, source_target_pairs={{0,4},{2,6},{4,0},{6,2},{8,12},{10,14},{12,8},{14,10},{1,5},{3,7},... | collective-permute-start | bytes 786440 | tf_op jit(solution)/shard_map/ppermute | solution.py:118
  401.3 13.6 %collective-permute-start.5 = (f32[8,32,128]{2,1,0:T(8,128)S(1)}, f32[8,32,128]{2,1,0:T(8,128)S(1)}, u32[]{:S(2)}, u32[]{:S(2)}) collective-permute-start(f32[8,32,128]{2,1,0:T(8,128)S(1)} %dynamic-slice_bitcast_fusion.4), channel_id=1, source_target_pairs={{0,8},{2,10},{4,12},{6,14},{8,0},{10,2},{12,4},{14,6},{1,9},{3,11}... | collective-permute-start | bytes 393224 | tf_op jit(solution)/shard_map/ppermute | solution.py:118
  421.1 8.7 %collective-permute-start.7 = (f32[2,32,128]{2,1,0:T(8,128)S(1)}, f32[2,32,128]{2,1,0:T(8,128)S(1)}, u32[]{:S(2)}, u32[]{:S(2)}) collective-permute-start(f32[2,32,128]{2,1,0:T(8,128)S(1)} %dynamic-slice_bitcast_fusion.6), channel_id=1, source_target_pairs={{0,32},{16,48},{32,0},{48,16},{64,96},{80,112},{96,64},{112,80},{1... | collective-permute-start | bytes 98312 | tf_op jit(solution)/shard_map/ppermute | solution.py:118
  429.9 13.6 %collective-permute-start.8 = (f32[1,32,128]{2,1,0:T(8,128)S(1)}, f32[1,32,128]{2,1,0:T(8,128)S(1)}, u32[]{:S(2)}, u32[]{:S(2)}) collective-permute-start(f32[1,32,128]{2,1,0:T(8,128)S(1)} %constant_dynamic-slice_fusion.1), channel_id=1, source_target_pairs={{0,64},{16,80},{32,96},{48,112},{64,0},{80,16},{96,32},{112,48},{1... | collective-permute-start | bytes 49160 | tf_op jit(solution)/shard_map/ppermute | solution.py:118
  (38 other events, 162.8 us)

commit v6 on v5

--- a/solution.py
+++ b/solution.py
@@ -115,7 +115,8 @@
     keep = lax.dynamic_index_in_dim(pairs, mine, 1, keepdims=False)
     send = lax.dynamic_index_in_dim(pairs, 1 - mine, 1, keepdims=False)
     route = [(i, i ^ bit) for i in range(lax.axis_size(axis))]
-    return keep + lax.ppermute(send, axis, route)
+    arrived = lax.ppermute(send.astype(jnp.bfloat16), axis, route)
+    return keep + arrived.astype(jnp.float32)
 
 
 def body(images, cotangent, dw_kernel, layer_scale, w_in, w_out):

time: 448 us -> 431 us (0.962)
  the two profiles are of different devices: /device:TPU:6 before, /device:TPU:54 now
where the time goes in v6:
time: 431 us; the launch traced here: 428 us
  starting transfers between devices  120 us (28%)
  waiting for transfers between devices  106 us (25%)
  other arithmetic  96.4 us (22%)
  local copies, waits for them, and re-layouts  51.8 us (12%)
  matrix products  50.4 us (12%)
    ppermute x22, starting transfers between devices, shifted(): return lax.ppermute(block, axis, route)  81.2 us
    ppermute x22, waiting for transfers between devices, shifted(): return lax.ppermute(block, axis, route)  80.4 us
    dynamic_update_slice x33, other arithmetic, place(): return lax.dynamic_update_index_in_dim(buffer, value, slot, 0)  40.3 us
    ppermute x7, starting transfers between devices, halve(): arrived = lax.ppermute(send.astype(jnp.bfloat16), axis, route)  38.3 us
    reduce_sum x11, other arithmetic, block_inner(): center = mixed - jnp.mean(mixed, axis=-1, keepdims=True)  28.5 us
    ppermute x7, waiting for transfers between devices, halve(): arrived = lax.ppermute(send.astype(jnp.bfloat16), axis, route)  25.7 us
    dot_general x11, matrix products, block_backward_saved(): lax.dot_general(branch_grad, weight_out, (((1,), (1,)), ((), ())), prefer...  24.9 us
    dot_general x11, matrix products, block_inner(): lax.dot_general(flat, weight_in, (((1,), (1,)), ((), ())), preferred_elem...  14.5 us
  transfers between devices with their start and end apart: 29, of which 29 were waited for; matrix products, arithmetic and copies ran while one was open for 4% of the time, Pallas kernels for 0%

profile of v6, /device:TPU:54, one launch (start us, length us, event | category | flops | bytes accessed | tf_op | source)
XLA Modules:
  0.0 427.5 jit_solution(13623180716039859818)
XLA Ops:
  14.9 141.1 %while.41 = (s32[]{:T(128)}, bf16[1,10,10,352]{3,2,1,0:T(8,128)(2,1)S(1)}, f32[6,1,10,10,352]{4,3,2,1,0:T(8,128)}, f32[6,1,10,10,1]{3,2,4,1,0:T(8,128)}, f32[6,1...) while((s32[]{:T(128)}, ...), condition=%wide.region_3.4_spmd, body=%wide.region_0.3_spmd.sunk | while | flops 203984320 | bytes 6215344 | solution.py:158
  31.8 5.6 %collective-permute-start = (bf16[1,10,10,352]{3,2,1,0:T(8,128)(2,1)S(1)}, bf16[1,10,10,352]{3,2,1,0:T(8,128)(2,1)S(1)}, u32[]{:S(2)}, u32[]{:S(2)}) collective-permute-start(bf16[1,10,10,352]{3,2,1,0:T(8,128)(2,1)S(1)} %reshape.641), channel_id=1, source_target_pairs={{0,128},{128,256},{256,384},{384,512},{512,640},{640,768},{768,896... | collective-permute-start | bytes 211208 | tf_op jit(solution)/shard_map/while/body/eval_jaxpr/ppermute | solution.py:15
  44.6 5.6 %collective-permute-start = (bf16[1,10,10,352]{3,2,1,0:T(8,128)(2,1)S(1)}, bf16[1,10,10,352]{3,2,1,0:T(8,128)(2,1)S(1)}, u32[]{:S(2)}, u32[]{:S(2)}) collective-permute-start(bf16[1,10,10,352]{3,2,1,0:T(8,128)(2,1)S(1)} %reshape.641), channel_id=1, source_target_pairs={{0,128},{128,256},{256,384},{384,512},{512,640},{640,768},{768,896... | collective-permute-start | bytes 211208 | tf_op jit(solution)/shard_map/while/body/eval_jaxpr/ppermute | solution.py:15
  83.1 5.6 %collective-permute-start = (bf16[1,10,10,352]{3,2,1,0:T(8,128)(2,1)S(1)}, bf16[1,10,10,352]{3,2,1,0:T(8,128)(2,1)S(1)}, u32[]{:S(2)}, u32[]{:S(2)}) collective-permute-start(bf16[1,10,10,352]{3,2,1,0:T(8,128)(2,1)S(1)} %reshape.641), channel_id=1, source_target_pairs={{0,128},{128,256},{256,384},{384,512},{512,640},{640,768},{768,896... | collective-permute-start | bytes 211208 | tf_op jit(solution)/shard_map/while/body/eval_jaxpr/ppermute | solution.py:15
  108.8 5.6 %collective-permute-start = (bf16[1,10,10,352]{3,2,1,0:T(8,128)(2,1)S(1)}, bf16[1,10,10,352]{3,2,1,0:T(8,128)(2,1)S(1)}, u32[]{:S(2)}, u32[]{:S(2)}) collective-permute-start(bf16[1,10,10,352]{3,2,1,0:T(8,128)(2,1)S(1)} %reshape.641), channel_id=1, source_target_pairs={{0,128},{128,256},{256,384},{384,512},{512,640},{640,768},{768,896... | collective-permute-start | bytes 211208 | tf_op jit(solution)/shard_map/while/body/eval_jaxpr/ppermute | solution.py:15
  121.6 5.6 %collective-permute-start = (bf16[1,10,10,352]{3,2,1,0:T(8,128)(2,1)S(1)}, bf16[1,10,10,352]{3,2,1,0:T(8,128)(2,1)S(1)}, u32[]{:S(2)}, u32[]{:S(2)}) collective-permute-start(bf16[1,10,10,352]{3,2,1,0:T(8,128)(2,1)S(1)} %reshape.641), channel_id=1, source_target_pairs={{0,128},{128,256},{256,384},{384,512},{512,640},{640,768},{768,896... | collective-permute-start | bytes 211208 | tf_op jit(solution)/shard_map/while/body/eval_jaxpr/ppermute | solution.py:15
  134.4 5.6 %collective-permute-start = (bf16[1,10,10,352]{3,2,1,0:T(8,128)(2,1)S(1)}, bf16[1,10,10,352]{3,2,1,0:T(8,128)(2,1)S(1)}, u32[]{:S(2)}, u32[]{:S(2)}) collective-permute-start(bf16[1,10,10,352]{3,2,1,0:T(8,128)(2,1)S(1)} %reshape.641), channel_id=1, source_target_pairs={{0,128},{128,256},{256,384},{384,512},{512,640},{640,768},{768,896... | collective-permute-start | bytes 211208 | tf_op jit(solution)/shard_map/while/body/eval_jaxpr/ppermute | solution.py:15
  148.1 5.6 %collective-permute-start = (bf16[1,10,10,352]{3,2,1,0:T(8,128)(2,1)S(1)}, bf16[1,10,10,352]{3,2,1,0:T(8,128)(2,1)S(1)}, u32[]{:S(2)}, u32[]{:S(2)}) collective-permute-start(bf16[1,10,10,352]{3,2,1,0:T(8,128)(2,1)S(1)} %reshape.641), channel_id=1, source_target_pairs={{0,128},{128,256},{256,384},{384,512},{512,640},{640,768},{768,896... | collective-permute-start | bytes 211208 | tf_op jit(solution)/shard_map/while/body/eval_jaxpr/ppermute | solution.py:15
  160.9 187.9 %while.42 = (s32[]{:T(128)}, bf16[1,10,10,352]{3,2,1,0:T(8,128)(2,1)S(1)}, bf16[6,1,10,10,352]{4,3,2,1,0:T(8,128)(2,1)}, bf16[6,100,1408]{2,1,0:T(8,128)(2,1)}, ...) while((s32[]{:T(128)}, ...), condition=%wide.region_7.8_spmd, body=%wide.region_4.7_spmd.sunk | while | flops 202400032 | bytes 6513550 | solution.py:179
  171.7 6.5 %collective-permute-done.1 = bf16[1,10,10,352]{3,2,1,0:T(8,128)(2,1)S(1)} collective-permute-done((bf16[1,10,10,352]{3,2,1,0:T(8,128)(2,1)S(1)}, bf16[1,10,10,352]{3,2,1,0:T(8,128)(2,1)S(1)}, u32[]{:S(2)}, u32[]{:S(2)}) %collective-permute-start.1) | collective-permute-done | bytes 70432 | tf_op jit(solution)/shard_map/while/body/eval_jaxpr/ppermute | solution.py:15
  189.1 6.1 %collective-permute-done.1 = bf16[1,10,10,352]{3,2,1,0:T(8,128)(2,1)S(1)} collective-permute-done((bf16[1,10,10,352]{3,2,1,0:T(8,128)(2,1)S(1)}, bf16[1,10,10,352]{3,2,1,0:T(8,128)(2,1)S(1)}, u32[]{:S(2)}, u32[]{:S(2)}) %collective-permute-start.1) | collective-permute-done | bytes 70432 | tf_op jit(solution)/shard_map/while/body/eval_jaxpr/ppermute | solution.py:15
  206.0 7.1 %collective-permute-done.1 = bf16[1,10,10,352]{3,2,1,0:T(8,128)(2,1)S(1)} collective-permute-done((bf16[1,10,10,352]{3,2,1,0:T(8,128)(2,1)S(1)}, bf16[1,10,10,352]{3,2,1,0:T(8,128)(2,1)S(1)}, u32[]{:S(2)}, u32[]{:S(2)}) %collective-permute-start.1) | collective-permute-done | bytes 70432 | tf_op jit(solution)/shard_map/while/body/eval_jaxpr/ppermute | solution.py:15
  223.9 6.5 %collective-permute-done.1 = bf16[1,10,10,352]{3,2,1,0:T(8,128)(2,1)S(1)} collective-permute-done((bf16[1,10,10,352]{3,2,1,0:T(8,128)(2,1)S(1)}, bf16[1,10,10,352]{3,2,1,0:T(8,128)(2,1)S(1)}, u32[]{:S(2)}, u32[]{:S(2)}) %collective-permute-start.1) | collective-permute-done | bytes 70432 | tf_op jit(solution)/shard_map/while/body/eval_jaxpr/ppermute | solution.py:15
  241.3 6.1 %collective-permute-done.1 = bf16[1,10,10,352]{3,2,1,0:T(8,128)(2,1)S(1)} collective-permute-done((bf16[1,10,10,352]{3,2,1,0:T(8,128)(2,1)S(1)}, bf16[1,10,10,352]{3,2,1,0:T(8,128)(2,1)S(1)}, u32[]{:S(2)}, u32[]{:S(2)}) %collective-permute-start.1) | collective-permute-done | bytes 70432 | tf_op jit(solution)/shard_map/while/body/eval_jaxpr/ppermute | solution.py:15
  258.2 6.1 %collective-permute-done.1 = bf16[1,10,10,352]{3,2,1,0:T(8,128)(2,1)S(1)} collective-permute-done((bf16[1,10,10,352]{3,2,1,0:T(8,128)(2,1)S(1)}, bf16[1,10,10,352]{3,2,1,0:T(8,128)(2,1)S(1)}, u32[]{:S(2)}, u32[]{:S(2)}) %collective-permute-start.1) | collective-permute-done | bytes 70432 | tf_op jit(solution)/shard_map/while/body/eval_jaxpr/ppermute | solution.py:15
  275.1 6.1 %collective-permute-done.1 = bf16[1,10,10,352]{3,2,1,0:T(8,128)(2,1)S(1)} collective-permute-done((bf16[1,10,10,352]{3,2,1,0:T(8,128)(2,1)S(1)}, bf16[1,10,10,352]{3,2,1,0:T(8,128)(2,1)S(1)}, u32[]{:S(2)}, u32[]{:S(2)}) %collective-permute-start.1) | collective-permute-done | bytes 70432 | tf_op jit(solution)/shard_map/while/body/eval_jaxpr/ppermute | solution.py:15
  292.0 6.1 %collective-permute-done.1 = bf16[1,10,10,352]{3,2,1,0:T(8,128)(2,1)S(1)} collective-permute-done((bf16[1,10,10,352]{3,2,1,0:T(8,128)(2,1)S(1)}, bf16[1,10,10,352]{3,2,1,0:T(8,128)(2,1)S(1)}, u32[]{:S(2)}, u32[]{:S(2)}) %collective-permute-start.1) | collective-permute-done | bytes 70432 | tf_op jit(solution)/shard_map/while/body/eval_jaxpr/ppermute | solution.py:15
  308.9 6.1 %collective-permute-done.1 = bf16[1,10,10,352]{3,2,1,0:T(8,128)(2,1)S(1)} collective-permute-done((bf16[1,10,10,352]{3,2,1,0:T(8,128)(2,1)S(1)}, bf16[1,10,10,352]{3,2,1,0:T(8,128)(2,1)S(1)}, u32[]{:S(2)}, u32[]{:S(2)}) %collective-permute-start.1) | collective-permute-done | bytes 70432 | tf_op jit(solution)/shard_map/while/body/eval_jaxpr/ppermute | solution.py:15
  325.8 6.1 %collective-permute-done.1 = bf16[1,10,10,352]{3,2,1,0:T(8,128)(2,1)S(1)} collective-permute-done((bf16[1,10,10,352]{3,2,1,0:T(8,128)(2,1)S(1)}, bf16[1,10,10,352]{3,2,1,0:T(8,128)(2,1)S(1)}, u32[]{:S(2)}, u32[]{:S(2)}) %collective-permute-start.1) | collective-permute-done | bytes 70432 | tf_op jit(solution)/shard_map/while/body/eval_jaxpr/ppermute | solution.py:15
  342.8 6.1 %collective-permute-done.1 = bf16[1,10,10,352]{3,2,1,0:T(8,128)(2,1)S(1)} collective-permute-done((bf16[1,10,10,352]{3,2,1,0:T(8,128)(2,1)S(1)}, bf16[1,10,10,352]{3,2,1,0:T(8,128)(2,1)S(1)}, u32[]{:S(2)}, u32[]{:S(2)}) %collective-permute-start.1) | collective-permute-done | bytes 70432 | tf_op jit(solution)/shard_map/while/body/eval_jaxpr/ppermute | solution.py:15
  367.4 7.9 %collective-permute-done.3 = bf16[32,32,128]{2,1,0:T(8,128)(2,1)S(1)} collective-permute-done((bf16[32,32,128]{2,1,0:T(8,128)(2,1)S(1)}, bf16[32,32,128]{2,1,0:T(8,128)(2,1)S(1)}, u32[]{:S(2)}, u32[]{:S(2)}) %collective-permute-start.3) | collective-permute-done | bytes 262176 | tf_op jit(solution)/shard_map/ppermute | solution.py:118
  379.3 6.5 %collective-permute-done.4 = bf16[16,32,128]{2,1,0:T(8,128)(2,1)S(1)} collective-permute-done((bf16[16,32,128]{2,1,0:T(8,128)(2,1)S(1)}, bf16[16,32,128]{2,1,0:T(8,128)(2,1)S(1)}, u32[]{:S(2)}, u32[]{:S(2)}) %collective-permute-start.4) | collective-permute-done | bytes 131104 | tf_op jit(solution)/shard_map/ppermute | solution.py:118
  403.7 7.9 %collective-permute-start.7 = (bf16[2,32,128]{2,1,0:T(8,128)(2,1)S(1)}, bf16[2,32,128]{2,1,0:T(8,128)(2,1)S(1)}, u32[]{:S(2)}, u32[]{:S(2)}) collective-permute-start(bf16[2,32,128]{2,1,0:T(8,128)(2,1)S(1)} %fusion.213), channel_id=1, source_target_pairs={{0,32},{16,48},{32,0},{48,16},{64,96},{80,112},{96,64},{112,80},{1... | collective-permute-start | bytes 49160 | tf_op jit(solution)/shard_map/ppermute | solution.py:118
  413.4 11.8 %collective-permute-start.8 = (bf16[1,32,128]{2,1,0:T(8,128)(2,1)S(1)}, bf16[1,32,128]{2,1,0:T(8,128)(2,1)S(1)}, u32[]{:S(2)}, u32[]{:S(2)}) collective-permute-start(bf16[1,32,128]{2,1,0:T(8,128)(2,1)S(1)} %dynamic-slice_convert_fusion.6), channel_id=1, source_target_pairs={{0,64},{16,80},{32,96},{48,112},{64,0},{80,16},{96,32},{112,48},{1... | collective-permute-start | bytes 24584 | tf_op jit(solution)/shard_map/ppermute | solution.py:118
  (450 shorter events, 282.4 us)
Async XLA Ops:
  31.8 8.0 %collective-permute-start = (bf16[1,10,10,352]{3,2,1,0:T(8,128)(2,1)S(1)}, bf16[1,10,10,352]{3,2,1,0:T(8,128)(2,1)S(1)}, u32[]{:S(2)}, u32[]{:S(2)}) collective-permute-start(bf16[1,10,10,352]{3,2,1,0:T(8,128)(2,1)S(1)} %reshape.641), channel_id=1, source_target_pairs={{0,128},{128,256},{256,384},{384,512},{512,640},{640,768},{768,896... | collective-permute-start | bytes 211208 | tf_op jit(solution)/shard_map/while/body/eval_jaxpr/ppermute | solution.py:15
  44.6 8.0 %collective-permute-start = (bf16[1,10,10,352]{3,2,1,0:T(8,128)(2,1)S(1)}, bf16[1,10,10,352]{3,2,1,0:T(8,128)(2,1)S(1)}, u32[]{:S(2)}, u32[]{:S(2)}) collective-permute-start(bf16[1,10,10,352]{3,2,1,0:T(8,128)(2,1)S(1)} %reshape.641), channel_id=1, source_target_pairs={{0,128},{128,256},{256,384},{384,512},{512,640},{640,768},{768,896... | collective-permute-start | bytes 211208 | tf_op jit(solution)/shard_map/while/body/eval_jaxpr/ppermute | solution.py:15
  57.5 8.0 %collective-permute-start = (bf16[1,10,10,352]{3,2,1,0:T(8,128)(2,1)S(1)}, bf16[1,10,10,352]{3,2,1,0:T(8,128)(2,1)S(1)}, u32[]{:S(2)}, u32[]{:S(2)}) collective-permute-start(bf16[1,10,10,352]{3,2,1,0:T(8,128)(2,1)S(1)} %reshape.641), channel_id=1, source_target_pairs={{0,128},{128,256},{256,384},{384,512},{512,640},{640,768},{768,896... | collective-permute-start | bytes 211208 | tf_op jit(solution)/shard_map/while/body/eval_jaxpr/ppermute | solution.py:15
  83.1 8.0 %collective-permute-start = (bf16[1,10,10,352]{3,2,1,0:T(8,128)(2,1)S(1)}, bf16[1,10,10,352]{3,2,1,0:T(8,128)(2,1)S(1)}, u32[]{:S(2)}, u32[]{:S(2)}) collective-permute-start(bf16[1,10,10,352]{3,2,1,0:T(8,128)(2,1)S(1)} %reshape.641), channel_id=1, source_target_pairs={{0,128},{128,256},{256,384},{384,512},{512,640},{640,768},{768,896... | collective-permute-start | bytes 211208 | tf_op jit(solution)/shard_map/while/body/eval_jaxpr/ppermute | solution.py:15
  108.8 8.0 %collective-permute-start = (bf16[1,10,10,352]{3,2,1,0:T(8,128)(2,1)S(1)}, bf16[1,10,10,352]{3,2,1,0:T(8,128)(2,1)S(1)}, u32[]{:S(2)}, u32[]{:S(2)}) collective-permute-start(bf16[1,10,10,352]{3,2,1,0:T(8,128)(2,1)S(1)} %reshape.641), channel_id=1, source_target_pairs={{0,128},{128,256},{256,384},{384,512},{512,640},{640,768},{768,896... | collective-permute-start | bytes 211208 | tf_op jit(solution)/shard_map/while/body/eval_jaxpr/ppermute | solution.py:15
  121.6 8.0 %collective-permute-start = (bf16[1,10,10,352]{3,2,1,0:T(8,128)(2,1)S(1)}, bf16[1,10,10,352]{3,2,1,0:T(8,128)(2,1)S(1)}, u32[]{:S(2)}, u32[]{:S(2)}) collective-permute-start(bf16[1,10,10,352]{3,2,1,0:T(8,128)(2,1)S(1)} %reshape.641), channel_id=1, source_target_pairs={{0,128},{128,256},{256,384},{384,512},{512,640},{640,768},{768,896... | collective-permute-start | bytes 211208 | tf_op jit(solution)/shard_map/while/body/eval_jaxpr/ppermute | solution.py:15
  134.4 8.8 %collective-permute-start = (bf16[1,10,10,352]{3,2,1,0:T(8,128)(2,1)S(1)}, bf16[1,10,10,352]{3,2,1,0:T(8,128)(2,1)S(1)}, u32[]{:S(2)}, u32[]{:S(2)}) collective-permute-start(bf16[1,10,10,352]{3,2,1,0:T(8,128)(2,1)S(1)} %reshape.641), channel_id=1, source_target_pairs={{0,128},{128,256},{256,384},{384,512},{512,640},{640,768},{768,896... | collective-permute-start | bytes 211208 | tf_op jit(solution)/shard_map/while/body/eval_jaxpr/ppermute | solution.py:15
  148.1 8.0 %collective-permute-start = (bf16[1,10,10,352]{3,2,1,0:T(8,128)(2,1)S(1)}, bf16[1,10,10,352]{3,2,1,0:T(8,128)(2,1)S(1)}, u32[]{:S(2)}, u32[]{:S(2)}) collective-permute-start(bf16[1,10,10,352]{3,2,1,0:T(8,128)(2,1)S(1)} %reshape.641), channel_id=1, source_target_pairs={{0,128},{128,256},{256,384},{384,512},{512,640},{640,768},{768,896... | collective-permute-start | bytes 211208 | tf_op jit(solution)/shard_map/while/body/eval_jaxpr/ppermute | solution.py:15
  169.8 8.4 %collective-permute-start.1 = (bf16[1,10,10,352]{3,2,1,0:T(8,128)(2,1)S(1)}, bf16[1,10,10,352]{3,2,1,0:T(8,128)(2,1)S(1)}, u32[]{:S(2)}, u32[]{:S(2)}) collective-permute-start(bf16[1,10,10,352]{3,2,1,0:T(8,128)(2,1)S(1)} %get-tuple-element.4248), channel_id=1, source_target_pairs={{128,0},{256,128},{384,256},{512,384},{640,512},{768,640},{896,768... | collective-permute-start | bytes 211208 | tf_op jit(solution)/shard_map/while/body/eval_jaxpr/ppermute | solution.py:15
  187.2 8.0 %collective-permute-start.1 = (bf16[1,10,10,352]{3,2,1,0:T(8,128)(2,1)S(1)}, bf16[1,10,10,352]{3,2,1,0:T(8,128)(2,1)S(1)}, u32[]{:S(2)}, u32[]{:S(2)}) collective-permute-start(bf16[1,10,10,352]{3,2,1,0:T(8,128)(2,1)S(1)} %get-tuple-element.4248), channel_id=1, source_target_pairs={{128,0},{256,128},{384,256},{512,384},{640,512},{768,640},{896,768... | collective-permute-start | bytes 211208 | tf_op jit(solution)/shard_map/while/body/eval_jaxpr/ppermute | solution.py:15
  204.0 9.0 %collective-permute-start.1 = (bf16[1,10,10,352]{3,2,1,0:T(8,128)(2,1)S(1)}, bf16[1,10,10,352]{3,2,1,0:T(8,128)(2,1)S(1)}, u32[]{:S(2)}, u32[]{:S(2)}) collective-permute-start(bf16[1,10,10,352]{3,2,1,0:T(8,128)(2,1)S(1)} %get-tuple-element.4248), channel_id=1, source_target_pairs={{128,0},{256,128},{384,256},{512,384},{640,512},{768,640},{896,768... | collective-permute-start | bytes 211208 | tf_op jit(solution)/shard_map/while/body/eval_jaxpr/ppermute | solution.py:15
  222.0 8.4 %collective-permute-start.1 = (bf16[1,10,10,352]{3,2,1,0:T(8,128)(2,1)S(1)}, bf16[1,10,10,352]{3,2,1,0:T(8,128)(2,1)S(1)}, u32[]{:S(2)}, u32[]{:S(2)}) collective-permute-start(bf16[1,10,10,352]{3,2,1,0:T(8,128)(2,1)S(1)} %get-tuple-element.4248), channel_id=1, source_target_pairs={{128,0},{256,128},{384,256},{512,384},{640,512},{768,640},{896,768... | collective-permute-start | bytes 211208 | tf_op jit(solution)/shard_map/while/body/eval_jaxpr/ppermute | solution.py:15
  239.4 8.0 %collective-permute-start.1 = (bf16[1,10,10,352]{3,2,1,0:T(8,128)(2,1)S(1)}, bf16[1,10,10,352]{3,2,1,0:T(8,128)(2,1)S(1)}, u32[]{:S(2)}, u32[]{:S(2)}) collective-permute-start(bf16[1,10,10,352]{3,2,1,0:T(8,128)(2,1)S(1)} %get-tuple-element.4248), channel_id=1, source_target_pairs={{128,0},{256,128},{384,256},{512,384},{640,512},{768,640},{896,768... | collective-permute-start | bytes 211208 | tf_op jit(solution)/shard_map/while/body/eval_jaxpr/ppermute | solution.py:15
  256.3 8.0 %collective-permute-start.1 = (bf16[1,10,10,352]{3,2,1,0:T(8,128)(2,1)S(1)}, bf16[1,10,10,352]{3,2,1,0:T(8,128)(2,1)S(1)}, u32[]{:S(2)}, u32[]{:S(2)}) collective-permute-start(bf16[1,10,10,352]{3,2,1,0:T(8,128)(2,1)S(1)} %get-tuple-element.4248), channel_id=1, source_target_pairs={{128,0},{256,128},{384,256},{512,384},{640,512},{768,640},{896,768... | collective-permute-start | bytes 211208 | tf_op jit(solution)/shard_map/while/body/eval_jaxpr/ppermute | solution.py:15
  273.2 8.0 %collective-permute-start.1 = (bf16[1,10,10,352]{3,2,1,0:T(8,128)(2,1)S(1)}, bf16[1,10,10,352]{3,2,1,0:T(8,128)(2,1)S(1)}, u32[]{:S(2)}, u32[]{:S(2)}) collective-permute-start(bf16[1,10,10,352]{3,2,1,0:T(8,128)(2,1)S(1)} %get-tuple-element.4248), channel_id=1, source_target_pairs={{128,0},{256,128},{384,256},{512,384},{640,512},{768,640},{896,768... | collective-permute-start | bytes 211208 | tf_op jit(solution)/shard_map/while/body/eval_jaxpr/ppermute | solution.py:15
  290.1 8.0 %collective-permute-start.1 = (bf16[1,10,10,352]{3,2,1,0:T(8,128)(2,1)S(1)}, bf16[1,10,10,352]{3,2,1,0:T(8,128)(2,1)S(1)}, u32[]{:S(2)}, u32[]{:S(2)}) collective-permute-start(bf16[1,10,10,352]{3,2,1,0:T(8,128)(2,1)S(1)} %get-tuple-element.4248), channel_id=1, source_target_pairs={{128,0},{256,128},{384,256},{512,384},{640,512},{768,640},{896,768... | collective-permute-start | bytes 211208 | tf_op jit(solution)/shard_map/while/body/eval_jaxpr/ppermute | solution.py:15
  307.0 8.0 %collective-permute-start.1 = (bf16[1,10,10,352]{3,2,1,0:T(8,128)(2,1)S(1)}, bf16[1,10,10,352]{3,2,1,0:T(8,128)(2,1)S(1)}, u32[]{:S(2)}, u32[]{:S(2)}) collective-permute-start(bf16[1,10,10,352]{3,2,1,0:T(8,128)(2,1)S(1)} %get-tuple-element.4248), channel_id=1, source_target_pairs={{128,0},{256,128},{384,256},{512,384},{640,512},{768,640},{896,768... | collective-permute-start | bytes 211208 | tf_op jit(solution)/shard_map/while/body/eval_jaxpr/ppermute | solution.py:15
  323.9 8.0 %collective-permute-start.1 = (bf16[1,10,10,352]{3,2,1,0:T(8,128)(2,1)S(1)}, bf16[1,10,10,352]{3,2,1,0:T(8,128)(2,1)S(1)}, u32[]{:S(2)}, u32[]{:S(2)}) collective-permute-start(bf16[1,10,10,352]{3,2,1,0:T(8,128)(2,1)S(1)} %get-tuple-element.4248), channel_id=1, source_target_pairs={{128,0},{256,128},{384,256},{512,384},{640,512},{768,640},{896,768... | collective-permute-start | bytes 211208 | tf_op jit(solution)/shard_map/while/body/eval_jaxpr/ppermute | solution.py:15
  340.8 8.0 %collective-permute-start.1 = (bf16[1,10,10,352]{3,2,1,0:T(8,128)(2,1)S(1)}, bf16[1,10,10,352]{3,2,1,0:T(8,128)(2,1)S(1)}, u32[]{:S(2)}, u32[]{:S(2)}) collective-permute-start(bf16[1,10,10,352]{3,2,1,0:T(8,128)(2,1)S(1)} %get-tuple-element.4248), channel_id=1, source_target_pairs={{128,0},{256,128},{384,256},{512,384},{640,512},{768,640},{896,768... | collective-permute-start | bytes 211208 | tf_op jit(solution)/shard_map/while/body/eval_jaxpr/ppermute | solution.py:15
  365.1 10.2 %collective-permute-start.3 = (bf16[32,32,128]{2,1,0:T(8,128)(2,1)S(1)}, bf16[32,32,128]{2,1,0:T(8,128)(2,1)S(1)}, u32[]{:S(2)}, u32[]{:S(2)}) collective-permute-start(bf16[32,32,128]{2,1,0:T(8,128)(2,1)S(1)} %fusion.209), channel_id=1, source_target_pairs={{0,2},{2,0},{4,6},{6,4},{8,10},{10,8},{12,14},{14,12},{1,3},{3,1},... | collective-permute-start | bytes 786440 | tf_op jit(solution)/shard_map/ppermute | solution.py:118
  375.5 10.3 %collective-permute-start.4 = (bf16[16,32,128]{2,1,0:T(8,128)(2,1)S(1)}, bf16[16,32,128]{2,1,0:T(8,128)(2,1)S(1)}, u32[]{:S(2)}, u32[]{:S(2)}) collective-permute-start(bf16[16,32,128]{2,1,0:T(8,128)(2,1)S(1)} %fusion.210), channel_id=1, source_target_pairs={{0,4},{2,6},{4,0},{6,2},{8,12},{10,14},{12,8},{14,10},{1,5},{3,7},... | collective-permute-start | bytes 393224 | tf_op jit(solution)/shard_map/ppermute | solution.py:118
  385.8 10.8 %collective-permute-start.5 = (bf16[8,32,128]{2,1,0:T(8,128)(2,1)S(1)}, bf16[8,32,128]{2,1,0:T(8,128)(2,1)S(1)}, u32[]{:S(2)}, u32[]{:S(2)}) collective-permute-start(bf16[8,32,128]{2,1,0:T(8,128)(2,1)S(1)} %fusion.211), channel_id=1, source_target_pairs={{0,8},{2,10},{4,12},{6,14},{8,0},{10,2},{12,4},{14,6},{1,9},{3,11}... | collective-permute-start | bytes 196616 | tf_op jit(solution)/shard_map/ppermute | solution.py:118
  403.7 9.7 %collective-permute-start.7 = (bf16[2,32,128]{2,1,0:T(8,128)(2,1)S(1)}, bf16[2,32,128]{2,1,0:T(8,128)(2,1)S(1)}, u32[]{:S(2)}, u32[]{:S(2)}) collective-permute-start(bf16[2,32,128]{2,1,0:T(8,128)(2,1)S(1)} %fusion.213), channel_id=1, source_target_pairs={{0,32},{16,48},{32,0},{48,16},{64,96},{80,112},{96,64},{112,80},{1... | collective-permute-start | bytes 49160 | tf_op jit(solution)/shard_map/ppermute | solution.py:118
  413.4 13.4 %collective-permute-start.8 = (bf16[1,32,128]{2,1,0:T(8,128)(2,1)S(1)}, bf16[1,32,128]{2,1,0:T(8,128)(2,1)S(1)}, u32[]{:S(2)}, u32[]{:S(2)}) collective-permute-start(bf16[1,32,128]{2,1,0:T(8,128)(2,1)S(1)} %dynamic-slice_convert_fusion.6), channel_id=1, source_target_pairs={{0,64},{16,80},{32,96},{48,112},{64,0},{80,16},{96,32},{112,48},{1... | collective-permute-start | bytes 24584 | tf_op jit(solution)/shard_map/ppermute | solution.py:118
  (38 other events, 167.0 us)

commit v7 on v6

--- a/solution.py
+++ b/solution.py
@@ -133,8 +133,7 @@
     factor = 1.0 / (micro_count * pixel_rows)
     blank = jnp.zeros(images.shape[1:], jnp.bfloat16)
 
-    def forward_tick(tick, carry):
-        incoming, kept = carry
+    def forward_step(tick, incoming, kept):
         micro = tick - section
         slot = jnp.clip(micro, 0, micro_count - 1)
         own = lax.dynamic_index_in_dim(images, slot, 0, keepdims=False)
@@ -146,8 +145,11 @@
             place(buffer, value, micro, micro_count)
             for buffer, value in zip(kept, (normed, inv_std, slope))
         )
-        incoming = shifted(leaving, "section", 1)
-        return (incoming, kept)
+        return (leaving, kept)
+
+    def forward_tick(tick, carry):
+        leaving, kept = forward_step(tick, *carry)
+        return (shifted(leaving, "section", 1), kept)
 
     spare = (micro_count + 2,) + images.shape[1:]
     kept = (
@@ -155,12 +157,12 @@
         jnp.zeros(spare[:-1] + (1,), jnp.float32),
         jnp.zeros((micro_count + 2, pixel_rows, hidden_width), jnp.float32),
     )
-    _, kept = lax.fori_loop(0, ticks, forward_tick, (blank, kept))
+    incoming, kept = lax.fori_loop(0, ticks - 1, forward_tick, (blank, kept))
+    _, kept = forward_step(ticks - 1, incoming, kept)
 
     stores = jnp.zeros((micro_count + 2, pixel_rows, hidden_width), jnp.bfloat16)
 
-    def backward_tick(tick, carry):
-        incoming, grads, stored = carry
+    def backward_step(tick, incoming, grads, stored):
         micro = tick - (sections - 1 - section)
         slot = jnp.clip(micro, 0, micro_count - 1)
         own = lax.dynamic_index_in_dim(cotangent, slot, 0, keepdims=False)
@@ -173,12 +175,16 @@
         )
         grads = place(grads, input_grad, micro, micro_count)
         stored = place(stored, pre_grad, micro, micro_count)
-        incoming = shifted(input_grad, "section", -1)
-        return (incoming, grads, stored)
-
-    _, grads, stores = lax.fori_loop(
-        0, ticks, backward_tick, (blank, jnp.zeros(spare, jnp.bfloat16), stores)
-    )
+        return (input_grad, grads, stored)
+
+    def backward_tick(tick, carry):
+        input_grad, grads, stored = backward_step(tick, *carry)
+        return (shifted(input_grad, "section", -1), grads, stored)
+
+    incoming, grads, stores = lax.fori_loop(
+        0, ticks - 1, backward_tick, (blank, jnp.zeros(spare, jnp.bfloat16), stores)
+    )
+    _, grads, stores = backward_step(ticks - 1, incoming, grads, stores)
     grads = grads[1 : micro_count + 1]
     all_flat = kept[0][1 : micro_count + 1].reshape(micro_count * pixel_rows, width).astype(jnp.bfloat16)
     all_pre = stores[1 : micro_count + 1].reshape(micro_count * pixel_rows, hidden_width)

time: 431 us -> 425 us (0.986)
  waiting for transfers between devices: 106 us -> 91.7 us
  local copies, waits for them, and re-layouts: 51.8 us -> 59.8 us
  starting transfers between devices: 120 us -> 113 us
  other arithmetic: 96.4 us -> 101 us
    ppermute x22 -> x20, waiting for transfers between devices: 80.4 us -> 72.5 us  [shifted(): return lax.ppermute(block, axis, route)]
    ppermute x22 -> x20, starting transfers between devices: 81.2 us -> 73.7 us  [shifted(): return lax.ppermute(block, axis, route)]
    ppermute x7, waiting for transfers between devices: 25.7 us -> 19.2 us  [halve(): arrived = lax.ppermute(send.astype(jnp.bfloat16), axis, route)]
    convert_element_type x11 -> x10, other arithmetic: 10.2 us -> 9.27 us  [block_backward_saved(): upstream.astype(jnp.float32) + depthwise_adjoint(mixed_grad, kernel)]
    dynamic_update_slice x33 -> x32, other arithmetic: 40.3 us -> 39.4 us  [place(): return lax.dynamic_update_index_in_dim(buffer, value, slot, 0)]
  transfers between devices with their start and end apart: 29 -> 27, of which waited for: 29 -> 26; matrix products, arithmetic and copies ran while one was open for 4% -> 6% of each run, Pallas kernels for 0% -> 0%
where the time goes in v7:
time: 425 us; the launch traced here: 421 us
  starting transfers between devices  113 us (27%)
  other arithmetic  101 us (24%)
  waiting for transfers between devices  91.7 us (22%)
  local copies, waits for them, and re-layouts  59.8 us (14%)
  matrix products  52.7 us (12%)
    ppermute x20, starting transfers between devices, shifted(): return lax.ppermute(block, axis, route)  73.7 us
    ppermute x20, waiting for transfers between devices, shifted(): return lax.ppermute(block, axis, route)  72.5 us
    dynamic_update_slice x32, other arithmetic, place(): return lax.dynamic_update_index_in_dim(buffer, value, slot, 0)  39.4 us
    ppermute x7, starting transfers between devices, halve(): arrived = lax.ppermute(send.astype(jnp.bfloat16), axis, route)  38.8 us
    reduce_sum x11, other arithmetic, block_inner(): center = mixed - jnp.mean(mixed, axis=-1, keepdims=True)  28.4 us
    dot_general x11, matrix products, block_backward_saved(): lax.dot_general(branch_grad, weight_out, (((1,), (1,)), ((), ())), prefer...  25.1 us
    ppermute x7, waiting for transfers between devices, halve(): arrived = lax.ppermute(send.astype(jnp.bfloat16), axis, route)  19.2 us
    dot_general x11, matrix products, block_inner(): lax.dot_general(flat, weight_in, (((1,), (1,)), ((), ())), preferred_elem...  14.5 us
  transfers between devices with their start and end apart: 27, of which 26 were waited for; matrix products, arithmetic and copies ran while one was open for 6% of the time, Pallas kernels for 0%

profile of v7, /device:TPU:54, one launch (start us, length us, event | category | flops | bytes accessed | tf_op | source)
XLA Modules:
  0.0 421.4 jit_solution(6545574475918609934)
XLA Ops:
  14.4 127.4 %while.41 = (s32[]{:T(128)}, bf16[1,10,10,352]{3,2,1,0:T(8,128)(2,1)S(1)}, f32[6,1,10,10,352]{4,3,2,1,0:T(8,128)}, f32[6,1,10,10,1]{3,2,4,1,0:T(8,128)}, f32[6,1...) while((s32[]{:T(128)}, ...), condition=%wide.region_3.4_spmd, body=%wide.region_0.3_spmd.sunk | while | flops 203984320 | bytes 6215344 | solution.py:160
  31.2 5.6 %collective-permute-start = (bf16[1,10,10,352]{3,2,1,0:T(8,128)(2,1)S(1)}, bf16[1,10,10,352]{3,2,1,0:T(8,128)(2,1)S(1)}, u32[]{:S(2)}, u32[]{:S(2)}) collective-permute-start(bf16[1,10,10,352]{3,2,1,0:T(8,128)(2,1)S(1)} %reshape.924), channel_id=1, source_target_pairs={{0,128},{128,256},{256,384},{384,512},{512,640},{640,768},{768,896... | collective-permute-start | bytes 211208 | tf_op jit(solution)/shard_map/while/body/eval_jaxpr/ppermute | solution.py:15
  44.1 5.6 %collective-permute-start = (bf16[1,10,10,352]{3,2,1,0:T(8,128)(2,1)S(1)}, bf16[1,10,10,352]{3,2,1,0:T(8,128)(2,1)S(1)}, u32[]{:S(2)}, u32[]{:S(2)}) collective-permute-start(bf16[1,10,10,352]{3,2,1,0:T(8,128)(2,1)S(1)} %reshape.924), channel_id=1, source_target_pairs={{0,128},{128,256},{256,384},{384,512},{512,640},{640,768},{768,896... | collective-permute-start | bytes 211208 | tf_op jit(solution)/shard_map/while/body/eval_jaxpr/ppermute | solution.py:15
  56.9 5.5 %collective-permute-start = (bf16[1,10,10,352]{3,2,1,0:T(8,128)(2,1)S(1)}, bf16[1,10,10,352]{3,2,1,0:T(8,128)(2,1)S(1)}, u32[]{:S(2)}, u32[]{:S(2)}) collective-permute-start(bf16[1,10,10,352]{3,2,1,0:T(8,128)(2,1)S(1)} %reshape.924), channel_id=1, source_target_pairs={{0,128},{128,256},{256,384},{384,512},{512,640},{640,768},{768,896... | collective-permute-start | bytes 211208 | tf_op jit(solution)/shard_map/while/body/eval_jaxpr/ppermute | solution.py:15
  82.5 5.6 %collective-permute-start = (bf16[1,10,10,352]{3,2,1,0:T(8,128)(2,1)S(1)}, bf16[1,10,10,352]{3,2,1,0:T(8,128)(2,1)S(1)}, u32[]{:S(2)}, u32[]{:S(2)}) collective-permute-start(bf16[1,10,10,352]{3,2,1,0:T(8,128)(2,1)S(1)} %reshape.924), channel_id=1, source_target_pairs={{0,128},{128,256},{256,384},{384,512},{512,640},{640,768},{768,896... | collective-permute-start | bytes 211208 | tf_op jit(solution)/shard_map/while/body/eval_jaxpr/ppermute | solution.py:15
  95.4 5.5 %collective-permute-start = (bf16[1,10,10,352]{3,2,1,0:T(8,128)(2,1)S(1)}, bf16[1,10,10,352]{3,2,1,0:T(8,128)(2,1)S(1)}, u32[]{:S(2)}, u32[]{:S(2)}) collective-permute-start(bf16[1,10,10,352]{3,2,1,0:T(8,128)(2,1)S(1)} %reshape.924), channel_id=1, source_target_pairs={{0,128},{128,256},{256,384},{384,512},{512,640},{640,768},{768,896... | collective-permute-start | bytes 211208 | tf_op jit(solution)/shard_map/while/body/eval_jaxpr/ppermute | solution.py:15
  108.2 5.6 %collective-permute-start = (bf16[1,10,10,352]{3,2,1,0:T(8,128)(2,1)S(1)}, bf16[1,10,10,352]{3,2,1,0:T(8,128)(2,1)S(1)}, u32[]{:S(2)}, u32[]{:S(2)}) collective-permute-start(bf16[1,10,10,352]{3,2,1,0:T(8,128)(2,1)S(1)} %reshape.924), channel_id=1, source_target_pairs={{0,128},{128,256},{256,384},{384,512},{512,640},{640,768},{768,896... | collective-permute-start | bytes 211208 | tf_op jit(solution)/shard_map/while/body/eval_jaxpr/ppermute | solution.py:15
  121.0 5.6 %collective-permute-start = (bf16[1,10,10,352]{3,2,1,0:T(8,128)(2,1)S(1)}, bf16[1,10,10,352]{3,2,1,0:T(8,128)(2,1)S(1)}, u32[]{:S(2)}, u32[]{:S(2)}) collective-permute-start(bf16[1,10,10,352]{3,2,1,0:T(8,128)(2,1)S(1)} %reshape.924), channel_id=1, source_target_pairs={{0,128},{128,256},{256,384},{384,512},{512,640},{640,768},{768,896... | collective-permute-start | bytes 211208 | tf_op jit(solution)/shard_map/while/body/eval_jaxpr/ppermute | solution.py:15
  133.8 5.6 %collective-permute-start = (bf16[1,10,10,352]{3,2,1,0:T(8,128)(2,1)S(1)}, bf16[1,10,10,352]{3,2,1,0:T(8,128)(2,1)S(1)}, u32[]{:S(2)}, u32[]{:S(2)}) collective-permute-start(bf16[1,10,10,352]{3,2,1,0:T(8,128)(2,1)S(1)} %reshape.924), channel_id=1, source_target_pairs={{0,128},{128,256},{256,384},{384,512},{512,640},{640,768},{768,896... | collective-permute-start | bytes 211208 | tf_op jit(solution)/shard_map/while/body/eval_jaxpr/ppermute | solution.py:15
  158.4 170.9 %while.42 = (s32[]{:T(128)}, bf16[1,10,10,352]{3,2,1,0:T(8,128)(2,1)S(1)}, bf16[6,1,10,10,352]{4,3,2,1,0:T(8,128)(2,1)}, bf16[6,100,1408]{2,1,0:T(8,128)(2,1)}, ...) while((s32[]{:T(128)}, ...), condition=%wide.region_9.10_spmd, body=%wide.region_6.9_spmd.sunk | while | flops 202400032 | bytes 6513550 | solution.py:184
  169.3 6.5 %collective-permute-done.1 = bf16[1,10,10,352]{3,2,1,0:T(8,128)(2,1)S(1)} collective-permute-done((bf16[1,10,10,352]{3,2,1,0:T(8,128)(2,1)S(1)}, bf16[1,10,10,352]{3,2,1,0:T(8,128)(2,1)S(1)}, u32[]{:S(2)}, u32[]{:S(2)}) %collective-permute-start.1) | collective-permute-done | bytes 70432 | tf_op jit(solution)/shard_map/while/body/eval_jaxpr/ppermute | solution.py:15
  186.6 6.1 %collective-permute-done.1 = bf16[1,10,10,352]{3,2,1,0:T(8,128)(2,1)S(1)} collective-permute-done((bf16[1,10,10,352]{3,2,1,0:T(8,128)(2,1)S(1)}, bf16[1,10,10,352]{3,2,1,0:T(8,128)(2,1)S(1)}, u32[]{:S(2)}, u32[]{:S(2)}) %collective-permute-start.1) | collective-permute-done | bytes 70432 | tf_op jit(solution)/shard_map/while/body/eval_jaxpr/ppermute | solution.py:15
  203.5 6.1 %collective-permute-done.1 = bf16[1,10,10,352]{3,2,1,0:T(8,128)(2,1)S(1)} collective-permute-done((bf16[1,10,10,352]{3,2,1,0:T(8,128)(2,1)S(1)}, bf16[1,10,10,352]{3,2,1,0:T(8,128)(2,1)S(1)}, u32[]{:S(2)}, u32[]{:S(2)}) %collective-permute-start.1) | collective-permute-done | bytes 70432 | tf_op jit(solution)/shard_map/while/body/eval_jaxpr/ppermute | solution.py:15
  220.4 7.1 %collective-permute-done.1 = bf16[1,10,10,352]{3,2,1,0:T(8,128)(2,1)S(1)} collective-permute-done((bf16[1,10,10,352]{3,2,1,0:T(8,128)(2,1)S(1)}, bf16[1,10,10,352]{3,2,1,0:T(8,128)(2,1)S(1)}, u32[]{:S(2)}, u32[]{:S(2)}) %collective-permute-start.1) | collective-permute-done | bytes 70432 | tf_op jit(solution)/shard_map/while/body/eval_jaxpr/ppermute | solution.py:15
  238.4 6.5 %collective-permute-done.1 = bf16[1,10,10,352]{3,2,1,0:T(8,128)(2,1)S(1)} collective-permute-done((bf16[1,10,10,352]{3,2,1,0:T(8,128)(2,1)S(1)}, bf16[1,10,10,352]{3,2,1,0:T(8,128)(2,1)S(1)}, u32[]{:S(2)}, u32[]{:S(2)}) %collective-permute-start.1) | collective-permute-done | bytes 70432 | tf_op jit(solution)/shard_map/while/body/eval_jaxpr/ppermute | solution.py:15
  255.7 6.1 %collective-permute-done.1 = bf16[1,10,10,352]{3,2,1,0:T(8,128)(2,1)S(1)} collective-permute-done((bf16[1,10,10,352]{3,2,1,0:T(8,128)(2,1)S(1)}, bf16[1,10,10,352]{3,2,1,0:T(8,128)(2,1)S(1)}, u32[]{:S(2)}, u32[]{:S(2)}) %collective-permute-start.1) | collective-permute-done | bytes 70432 | tf_op jit(solution)/shard_map/while/body/eval_jaxpr/ppermute | solution.py:15
  272.6 6.1 %collective-permute-done.1 = bf16[1,10,10,352]{3,2,1,0:T(8,128)(2,1)S(1)} collective-permute-done((bf16[1,10,10,352]{3,2,1,0:T(8,128)(2,1)S(1)}, bf16[1,10,10,352]{3,2,1,0:T(8,128)(2,1)S(1)}, u32[]{:S(2)}, u32[]{:S(2)}) %collective-permute-start.1) | collective-permute-done | bytes 70432 | tf_op jit(solution)/shard_map/while/body/eval_jaxpr/ppermute | solution.py:15
  289.5 6.1 %collective-permute-done.1 = bf16[1,10,10,352]{3,2,1,0:T(8,128)(2,1)S(1)} collective-permute-done((bf16[1,10,10,352]{3,2,1,0:T(8,128)(2,1)S(1)}, bf16[1,10,10,352]{3,2,1,0:T(8,128)(2,1)S(1)}, u32[]{:S(2)}, u32[]{:S(2)}) %collective-permute-start.1) | collective-permute-done | bytes 70432 | tf_op jit(solution)/shard_map/while/body/eval_jaxpr/ppermute | solution.py:15
  306.4 6.1 %collective-permute-done.1 = bf16[1,10,10,352]{3,2,1,0:T(8,128)(2,1)S(1)} collective-permute-done((bf16[1,10,10,352]{3,2,1,0:T(8,128)(2,1)S(1)}, bf16[1,10,10,352]{3,2,1,0:T(8,128)(2,1)S(1)}, u32[]{:S(2)}, u32[]{:S(2)}) %collective-permute-start.1) | collective-permute-done | bytes 70432 | tf_op jit(solution)/shard_map/while/body/eval_jaxpr/ppermute | solution.py:15
  323.3 6.1 %collective-permute-done.1 = bf16[1,10,10,352]{3,2,1,0:T(8,128)(2,1)S(1)} collective-permute-done((bf16[1,10,10,352]{3,2,1,0:T(8,128)(2,1)S(1)}, bf16[1,10,10,352]{3,2,1,0:T(8,128)(2,1)S(1)}, u32[]{:S(2)}, u32[]{:S(2)}) %collective-permute-start.1) | collective-permute-done | bytes 70432 | tf_op jit(solution)/shard_map/while/body/eval_jaxpr/ppermute | solution.py:15
  358.2 6.2 %collective-permute-done.3 = bf16[32,32,128]{2,1,0:T(8,128)(2,1)S(1)} collective-permute-done((bf16[32,32,128]{2,1,0:T(8,128)(2,1)S(1)}, bf16[32,32,128]{2,1,0:T(8,128)(2,1)S(1)}, u32[]{:S(2)}, u32[]{:S(2)}) %collective-permute-start.3) | collective-permute-done | bytes 262176 | tf_op jit(solution)/shard_map/ppermute | solution.py:118
  369.2 5.8 %collective-permute-done.4 = bf16[16,32,128]{2,1,0:T(8,128)(2,1)S(1)} collective-permute-done((bf16[16,32,128]{2,1,0:T(8,128)(2,1)S(1)}, bf16[16,32,128]{2,1,0:T(8,128)(2,1)S(1)}, u32[]{:S(2)}, u32[]{:S(2)}) %collective-permute-start.4) | collective-permute-done | bytes 131104 | tf_op jit(solution)/shard_map/ppermute | solution.py:118
  392.9 7.9 %collective-permute-start.7 = (bf16[2,32,128]{2,1,0:T(8,128)(2,1)S(1)}, bf16[2,32,128]{2,1,0:T(8,128)(2,1)S(1)}, u32[]{:S(2)}, u32[]{:S(2)}) collective-permute-start(bf16[2,32,128]{2,1,0:T(8,128)(2,1)S(1)} %fusion.425), channel_id=1, source_target_pairs={{0,32},{16,48},{32,0},{48,16},{64,96},{80,112},{96,64},{112,80},{1... | collective-permute-start | bytes 49160 | tf_op jit(solution)/shard_map/ppermute | solution.py:118
  407.2 11.9 %collective-permute-start.8 = (bf16[1,32,128]{2,1,0:T(8,128)(2,1)S(1)}, bf16[1,32,128]{2,1,0:T(8,128)(2,1)S(1)}, u32[]{:S(2)}, u32[]{:S(2)}) collective-permute-start(bf16[1,32,128]{2,1,0:T(8,128)(2,1)S(1)} %dynamic-slice_convert_fusion.6), channel_id=1, source_target_pairs={{0,64},{16,80},{32,96},{48,112},{64,0},{80,16},{96,32},{112,48},{1... | collective-permute-start | bytes 24584 | tf_op jit(solution)/shard_map/ppermute | solution.py:118
  (562 shorter events, 278.6 us)
Async XLA Ops:
  31.2 8.0 %collective-permute-start = (bf16[1,10,10,352]{3,2,1,0:T(8,128)(2,1)S(1)}, bf16[1,10,10,352]{3,2,1,0:T(8,128)(2,1)S(1)}, u32[]{:S(2)}, u32[]{:S(2)}) collective-permute-start(bf16[1,10,10,352]{3,2,1,0:T(8,128)(2,1)S(1)} %reshape.924), channel_id=1, source_target_pairs={{0,128},{128,256},{256,384},{384,512},{512,640},{640,768},{768,896... | collective-permute-start | bytes 211208 | tf_op jit(solution)/shard_map/while/body/eval_jaxpr/ppermute | solution.py:15
  44.1 8.0 %collective-permute-start = (bf16[1,10,10,352]{3,2,1,0:T(8,128)(2,1)S(1)}, bf16[1,10,10,352]{3,2,1,0:T(8,128)(2,1)S(1)}, u32[]{:S(2)}, u32[]{:S(2)}) collective-permute-start(bf16[1,10,10,352]{3,2,1,0:T(8,128)(2,1)S(1)} %reshape.924), channel_id=1, source_target_pairs={{0,128},{128,256},{256,384},{384,512},{512,640},{640,768},{768,896... | collective-permute-start | bytes 211208 | tf_op jit(solution)/shard_map/while/body/eval_jaxpr/ppermute | solution.py:15
  56.9 8.0 %collective-permute-start = (bf16[1,10,10,352]{3,2,1,0:T(8,128)(2,1)S(1)}, bf16[1,10,10,352]{3,2,1,0:T(8,128)(2,1)S(1)}, u32[]{:S(2)}, u32[]{:S(2)}) collective-permute-start(bf16[1,10,10,352]{3,2,1,0:T(8,128)(2,1)S(1)} %reshape.924), channel_id=1, source_target_pairs={{0,128},{128,256},{256,384},{384,512},{512,640},{640,768},{768,896... | collective-permute-start | bytes 211208 | tf_op jit(solution)/shard_map/while/body/eval_jaxpr/ppermute | solution.py:15
  69.7 7.9 %collective-permute-start = (bf16[1,10,10,352]{3,2,1,0:T(8,128)(2,1)S(1)}, bf16[1,10,10,352]{3,2,1,0:T(8,128)(2,1)S(1)}, u32[]{:S(2)}, u32[]{:S(2)}) collective-permute-start(bf16[1,10,10,352]{3,2,1,0:T(8,128)(2,1)S(1)} %reshape.924), channel_id=1, source_target_pairs={{0,128},{128,256},{256,384},{384,512},{512,640},{640,768},{768,896... | collective-permute-start | bytes 211208 | tf_op jit(solution)/shard_map/while/body/eval_jaxpr/ppermute | solution.py:15
  82.5 8.0 %collective-permute-start = (bf16[1,10,10,352]{3,2,1,0:T(8,128)(2,1)S(1)}, bf16[1,10,10,352]{3,2,1,0:T(8,128)(2,1)S(1)}, u32[]{:S(2)}, u32[]{:S(2)}) collective-permute-start(bf16[1,10,10,352]{3,2,1,0:T(8,128)(2,1)S(1)} %reshape.924), channel_id=1, source_target_pairs={{0,128},{128,256},{256,384},{384,512},{512,640},{640,768},{768,896... | collective-permute-start | bytes 211208 | tf_op jit(solution)/shard_map/while/body/eval_jaxpr/ppermute | solution.py:15
  95.4 8.0 %collective-permute-start = (bf16[1,10,10,352]{3,2,1,0:T(8,128)(2,1)S(1)}, bf16[1,10,10,352]{3,2,1,0:T(8,128)(2,1)S(1)}, u32[]{:S(2)}, u32[]{:S(2)}) collective-permute-start(bf16[1,10,10,352]{3,2,1,0:T(8,128)(2,1)S(1)} %reshape.924), channel_id=1, source_target_pairs={{0,128},{128,256},{256,384},{384,512},{512,640},{640,768},{768,896... | collective-permute-start | bytes 211208 | tf_op jit(solution)/shard_map/while/body/eval_jaxpr/ppermute | solution.py:15
  108.2 8.0 %collective-permute-start = (bf16[1,10,10,352]{3,2,1,0:T(8,128)(2,1)S(1)}, bf16[1,10,10,352]{3,2,1,0:T(8,128)(2,1)S(1)}, u32[]{:S(2)}, u32[]{:S(2)}) collective-permute-start(bf16[1,10,10,352]{3,2,1,0:T(8,128)(2,1)S(1)} %reshape.924), channel_id=1, source_target_pairs={{0,128},{128,256},{256,384},{384,512},{512,640},{640,768},{768,896... | collective-permute-start | bytes 211208 | tf_op jit(solution)/shard_map/while/body/eval_jaxpr/ppermute | solution.py:15
  121.0 8.0 %collective-permute-start = (bf16[1,10,10,352]{3,2,1,0:T(8,128)(2,1)S(1)}, bf16[1,10,10,352]{3,2,1,0:T(8,128)(2,1)S(1)}, u32[]{:S(2)}, u32[]{:S(2)}) collective-permute-start(bf16[1,10,10,352]{3,2,1,0:T(8,128)(2,1)S(1)} %reshape.924), channel_id=1, source_target_pairs={{0,128},{128,256},{256,384},{384,512},{512,640},{640,768},{768,896... | collective-permute-start | bytes 211208 | tf_op jit(solution)/shard_map/while/body/eval_jaxpr/ppermute | solution.py:15
  133.8 8.0 %collective-permute-start = (bf16[1,10,10,352]{3,2,1,0:T(8,128)(2,1)S(1)}, bf16[1,10,10,352]{3,2,1,0:T(8,128)(2,1)S(1)}, u32[]{:S(2)}, u32[]{:S(2)}) collective-permute-start(bf16[1,10,10,352]{3,2,1,0:T(8,128)(2,1)S(1)} %reshape.924), channel_id=1, source_target_pairs={{0,128},{128,256},{256,384},{384,512},{512,640},{640,768},{768,896... | collective-permute-start | bytes 211208 | tf_op jit(solution)/shard_map/while/body/eval_jaxpr/ppermute | solution.py:15
  167.4 8.4 %collective-permute-start.1 = (bf16[1,10,10,352]{3,2,1,0:T(8,128)(2,1)S(1)}, bf16[1,10,10,352]{3,2,1,0:T(8,128)(2,1)S(1)}, u32[]{:S(2)}, u32[]{:S(2)}) collective-permute-start(bf16[1,10,10,352]{3,2,1,0:T(8,128)(2,1)S(1)} %get-tuple-element.4261), channel_id=1, source_target_pairs={{128,0},{256,128},{384,256},{512,384},{640,512},{768,640},{896,768... | collective-permute-start | bytes 211208 | tf_op jit(solution)/shard_map/while/body/eval_jaxpr/ppermute | solution.py:15
  184.7 8.0 %collective-permute-start.1 = (bf16[1,10,10,352]{3,2,1,0:T(8,128)(2,1)S(1)}, bf16[1,10,10,352]{3,2,1,0:T(8,128)(2,1)S(1)}, u32[]{:S(2)}, u32[]{:S(2)}) collective-permute-start(bf16[1,10,10,352]{3,2,1,0:T(8,128)(2,1)S(1)} %get-tuple-element.4261), channel_id=1, source_target_pairs={{128,0},{256,128},{384,256},{512,384},{640,512},{768,640},{896,768... | collective-permute-start | bytes 211208 | tf_op jit(solution)/shard_map/while/body/eval_jaxpr/ppermute | solution.py:15
  201.6 8.0 %collective-permute-start.1 = (bf16[1,10,10,352]{3,2,1,0:T(8,128)(2,1)S(1)}, bf16[1,10,10,352]{3,2,1,0:T(8,128)(2,1)S(1)}, u32[]{:S(2)}, u32[]{:S(2)}) collective-permute-start(bf16[1,10,10,352]{3,2,1,0:T(8,128)(2,1)S(1)} %get-tuple-element.4261), channel_id=1, source_target_pairs={{128,0},{256,128},{384,256},{512,384},{640,512},{768,640},{896,768... | collective-permute-start | bytes 211208 | tf_op jit(solution)/shard_map/while/body/eval_jaxpr/ppermute | solution.py:15
  218.5 9.0 %collective-permute-start.1 = (bf16[1,10,10,352]{3,2,1,0:T(8,128)(2,1)S(1)}, bf16[1,10,10,352]{3,2,1,0:T(8,128)(2,1)S(1)}, u32[]{:S(2)}, u32[]{:S(2)}) collective-permute-start(bf16[1,10,10,352]{3,2,1,0:T(8,128)(2,1)S(1)} %get-tuple-element.4261), channel_id=1, source_target_pairs={{128,0},{256,128},{384,256},{512,384},{640,512},{768,640},{896,768... | collective-permute-start | bytes 211208 | tf_op jit(solution)/shard_map/while/body/eval_jaxpr/ppermute | solution.py:15
  236.5 8.4 %collective-permute-start.1 = (bf16[1,10,10,352]{3,2,1,0:T(8,128)(2,1)S(1)}, bf16[1,10,10,352]{3,2,1,0:T(8,128)(2,1)S(1)}, u32[]{:S(2)}, u32[]{:S(2)}) collective-permute-start(bf16[1,10,10,352]{3,2,1,0:T(8,128)(2,1)S(1)} %get-tuple-element.4261), channel_id=1, source_target_pairs={{128,0},{256,128},{384,256},{512,384},{640,512},{768,640},{896,768... | collective-permute-start | bytes 211208 | tf_op jit(solution)/shard_map/while/body/eval_jaxpr/ppermute | solution.py:15
  253.8 8.0 %collective-permute-start.1 = (bf16[1,10,10,352]{3,2,1,0:T(8,128)(2,1)S(1)}, bf16[1,10,10,352]{3,2,1,0:T(8,128)(2,1)S(1)}, u32[]{:S(2)}, u32[]{:S(2)}) collective-permute-start(bf16[1,10,10,352]{3,2,1,0:T(8,128)(2,1)S(1)} %get-tuple-element.4261), channel_id=1, source_target_pairs={{128,0},{256,128},{384,256},{512,384},{640,512},{768,640},{896,768... | collective-permute-start | bytes 211208 | tf_op jit(solution)/shard_map/while/body/eval_jaxpr/ppermute | solution.py:15
  270.6 8.0 %collective-permute-start.1 = (bf16[1,10,10,352]{3,2,1,0:T(8,128)(2,1)S(1)}, bf16[1,10,10,352]{3,2,1,0:T(8,128)(2,1)S(1)}, u32[]{:S(2)}, u32[]{:S(2)}) collective-permute-start(bf16[1,10,10,352]{3,2,1,0:T(8,128)(2,1)S(1)} %get-tuple-element.4261), channel_id=1, source_target_pairs={{128,0},{256,128},{384,256},{512,384},{640,512},{768,640},{896,768... | collective-permute-start | bytes 211208 | tf_op jit(solution)/shard_map/while/body/eval_jaxpr/ppermute | solution.py:15
  287.6 8.0 %collective-permute-start.1 = (bf16[1,10,10,352]{3,2,1,0:T(8,128)(2,1)S(1)}, bf16[1,10,10,352]{3,2,1,0:T(8,128)(2,1)S(1)}, u32[]{:S(2)}, u32[]{:S(2)}) collective-permute-start(bf16[1,10,10,352]{3,2,1,0:T(8,128)(2,1)S(1)} %get-tuple-element.4261), channel_id=1, source_target_pairs={{128,0},{256,128},{384,256},{512,384},{640,512},{768,640},{896,768... | collective-permute-start | bytes 211208 | tf_op jit(solution)/shard_map/while/body/eval_jaxpr/ppermute | solution.py:15
  304.5 8.0 %collective-permute-start.1 = (bf16[1,10,10,352]{3,2,1,0:T(8,128)(2,1)S(1)}, bf16[1,10,10,352]{3,2,1,0:T(8,128)(2,1)S(1)}, u32[]{:S(2)}, u32[]{:S(2)}) collective-permute-start(bf16[1,10,10,352]{3,2,1,0:T(8,128)(2,1)S(1)} %get-tuple-element.4261), channel_id=1, source_target_pairs={{128,0},{256,128},{384,256},{512,384},{640,512},{768,640},{896,768... | collective-permute-start | bytes 211208 | tf_op jit(solution)/shard_map/while/body/eval_jaxpr/ppermute | solution.py:15
  321.4 8.0 %collective-permute-start.1 = (bf16[1,10,10,352]{3,2,1,0:T(8,128)(2,1)S(1)}, bf16[1,10,10,352]{3,2,1,0:T(8,128)(2,1)S(1)}, u32[]{:S(2)}, u32[]{:S(2)}) collective-permute-start(bf16[1,10,10,352]{3,2,1,0:T(8,128)(2,1)S(1)} %get-tuple-element.4261), channel_id=1, source_target_pairs={{128,0},{256,128},{384,256},{512,384},{640,512},{768,640},{896,768... | collective-permute-start | bytes 211208 | tf_op jit(solution)/shard_map/while/body/eval_jaxpr/ppermute | solution.py:15
  354.2 10.2 %collective-permute-start.3 = (bf16[32,32,128]{2,1,0:T(8,128)(2,1)S(1)}, bf16[32,32,128]{2,1,0:T(8,128)(2,1)S(1)}, u32[]{:S(2)}, u32[]{:S(2)}) collective-permute-start(bf16[32,32,128]{2,1,0:T(8,128)(2,1)S(1)} %fusion.223), channel_id=1, source_target_pairs={{0,2},{2,0},{4,6},{6,4},{8,10},{10,8},{12,14},{14,12},{1,3},{3,1},... | collective-permute-start | bytes 786440 | tf_op jit(solution)/shard_map/ppermute | solution.py:118
  364.7 10.3 %collective-permute-start.4 = (bf16[16,32,128]{2,1,0:T(8,128)(2,1)S(1)}, bf16[16,32,128]{2,1,0:T(8,128)(2,1)S(1)}, u32[]{:S(2)}, u32[]{:S(2)}) collective-permute-start(bf16[16,32,128]{2,1,0:T(8,128)(2,1)S(1)} %fusion.420), channel_id=1, source_target_pairs={{0,4},{2,6},{4,0},{6,2},{8,12},{10,14},{12,8},{14,10},{1,5},{3,7},... | collective-permute-start | bytes 393224 | tf_op jit(solution)/shard_map/ppermute | solution.py:118
  375.0 10.8 %collective-permute-start.5 = (bf16[8,32,128]{2,1,0:T(8,128)(2,1)S(1)}, bf16[8,32,128]{2,1,0:T(8,128)(2,1)S(1)}, u32[]{:S(2)}, u32[]{:S(2)}) collective-permute-start(bf16[8,32,128]{2,1,0:T(8,128)(2,1)S(1)} %fusion.423), channel_id=1, source_target_pairs={{0,8},{2,10},{4,12},{6,14},{8,0},{10,2},{12,4},{14,6},{1,9},{3,11}... | collective-permute-start | bytes 196616 | tf_op jit(solution)/shard_map/ppermute | solution.py:118
  392.9 14.2 %collective-permute-start.7 = (bf16[2,32,128]{2,1,0:T(8,128)(2,1)S(1)}, bf16[2,32,128]{2,1,0:T(8,128)(2,1)S(1)}, u32[]{:S(2)}, u32[]{:S(2)}) collective-permute-start(bf16[2,32,128]{2,1,0:T(8,128)(2,1)S(1)} %fusion.425), channel_id=1, source_target_pairs={{0,32},{16,48},{32,0},{48,16},{64,96},{80,112},{96,64},{112,80},{1... | collective-permute-start | bytes 49160 | tf_op jit(solution)/shard_map/ppermute | solution.py:118
  407.2 13.5 %collective-permute-start.8 = (bf16[1,32,128]{2,1,0:T(8,128)(2,1)S(1)}, bf16[1,32,128]{2,1,0:T(8,128)(2,1)S(1)}, u32[]{:S(2)}, u32[]{:S(2)}) collective-permute-start(bf16[1,32,128]{2,1,0:T(8,128)(2,1)S(1)} %dynamic-slice_convert_fusion.6), channel_id=1, source_target_pairs={{0,64},{16,80},{32,96},{48,112},{64,0},{80,16},{96,32},{112,48},{1... | collective-permute-start | bytes 24584 | tf_op jit(solution)/shard_map/ppermute | solution.py:118
  (95 other events, 647.5 us)
